TPU v7x, 256 devices: a whole 4x4x8 slice. The times are simulated.
256 devices in a mesh: seq: 64 (over x, y_hi, z), head: 4 (over y_lo, core).
Axes of the slice: x: 4, y: 4 (y_hi: 2, y_lo: 2; y = y_hi * 2 + y_lo), z: 8, core: 2. Of those that a mesh axis runs over, the one named last changes fastest.
Arguments:
- tokens: bfloat16 [16384, 5376], P('seq'), may hold values from -6 to 6
- q_weight: bfloat16 [5376, 2048], P('seq', 'head')
- k_weight: bfloat16 [5376, 1024], P('seq', 'head')
- v_weight: bfloat16 [5376, 1024], P('seq', 'head'), may hold values from -0.078125 to 0.078125
- q_gain: float32 [128], replicated, may hold values from 0.5 to 6
- k_gain: float32 [128], replicated, may hold values from 0.5 to 6
- windows: int32 [16], P('head'), may hold values from 512 to 1024, as said below
- token_weight: float32 [16384], P('seq'), may hold values from 0.3 to 6
- loss_mask: int32 [16384], P('seq'), may hold values from 0 to 1, as said below
- grad_attn: bfloat16 [16384, 2048], P('seq', 'head'), may hold values from -6 to 6
Outputs:
- attn: bfloat16 [16384, 2048], P('seq', 'head')
- grad_tokens: bfloat16 [16384, 5376], P('seq', 'head')
Inputs may be any that keep to these rules, and one draw needn't show every extreme that they name: `windows`: some head has a window of exactly 1024 keys and some head exactly 512. `loss_mask`: the first token always counts.
All inputs are finite; a program needn't handle non-finite values.
Results may differ from a plain program's by a relative error of at most 0.038.
The roundings to bfloat16 on the way count: a program that leaves them out, or rounds other values in their place, can miss the bound.
Values may be sent and summed in bfloat16 or wider, within the bound.
No kernel may reach another device: no remote copies, remote signals or barrier semaphores. Data moves between devices by JAX's collectives and lax.ppermute only.
A program may use at most 128 MiB of HBM per device.

v0:
```python
import jax
import jax.numpy as jnp
from jax import lax
from jax.sharding import PartitionSpec as P

QPRE = 168
WINDOW = 1024


norm_eps = 1e-06


def passed_along(block, axis, distance):
    devices = range(lax.axis_size(axis))
    route = [(i - distance, i) for i in devices if i - distance in devices]
    return lax.ppermute(block, axis, route)


def rotate_table(positions, head_width):
    half_width = head_width // 2
    frequency = 10000.0 ** (-(jnp.arange(half_width, dtype=jnp.float32) * 2.0) / head_width)
    angles = positions.astype(jnp.float32)[:, None] * frequency[None, :]
    return (jnp.cos(angles)[:, None, :], jnp.sin(angles)[:, None, :])


def norm_rotate(linear, gain_vec, cosine, sine_table):
    mean_square = jnp.mean(linear * linear, axis=-1, keepdims=True)
    normed = linear * lax.rsqrt(mean_square + norm_eps) * gain_vec
    half_width = linear.shape[-1] // 2
    first_half = normed[..., :half_width]
    second_half = normed[..., half_width:]
    return jnp.concatenate(
        [
            first_half * cosine - second_half * sine_table,
            second_half * cosine + first_half * sine_table,
        ],
        axis=-1,
    )


def block_grad(queries, key_rows, value_rows, cotangent, query_pos, key_pos, windows, score_scale):
    tok_rows, q_heads, head_width = queries.shape
    kv_heads = key_rows.shape[1]
    group_size = q_heads // kv_heads
    query_grp = queries.reshape(tok_rows, kv_heads, group_size, head_width)
    cotan_grp = cotangent.reshape(tok_rows, kv_heads, group_size, head_width)
    scores = score_scale * jnp.einsum(
        "tgjd,sgd->gjts", query_grp, key_rows, preferred_element_type=jnp.float32
    )
    distance = query_pos[:, None] - key_pos[None, :]
    reach = windows.reshape(kv_heads, group_size)[:, :, None, None]
    allowed = (
        (distance[None, None] >= 0)
        & (distance[None, None] < reach)
        & (key_pos >= 0)[None, None, None, :]
    )
    masked = jnp.where(allowed, scores, jnp.float32(-1e30))
    row_peak = jnp.max(masked, axis=-1, keepdims=True)
    row_total = jnp.sum(
        jnp.where(allowed, jnp.exp(masked - row_peak), jnp.float32(0.0)), axis=-1, keepdims=True
    )
    logsum = row_peak + jnp.log(row_total)
    probability = jnp.where(allowed, jnp.exp(masked - logsum), jnp.float32(0.0))
    probs_b = probability.astype(jnp.bfloat16)
    attended = jnp.einsum(
        "gjts,sgd->tgjd", probs_b, value_rows, preferred_element_type=jnp.float32
    ).astype(jnp.bfloat16)
    row_delta = jnp.sum(cotan_grp.astype(jnp.float32) * attended.astype(jnp.float32), axis=-1)
    dprobs = jnp.einsum("tgjd,sgd->gjts", cotan_grp, value_rows, preferred_element_type=jnp.float32)
    dscore = (probability * (dprobs - jnp.transpose(row_delta, (1, 2, 0))[..., None])).astype(
        jnp.bfloat16
    )
    dquery = score_scale * jnp.einsum(
        "gjts,sgd->tgjd", dscore, key_rows, preferred_element_type=jnp.float32
    )
    key_grads = score_scale * jnp.einsum(
        "gjts,tgjd->sgd", dscore, query_grp, preferred_element_type=jnp.float32
    )
    dvalues = jnp.einsum("gjts,tgjd->sgd", probs_b, cotan_grp, preferred_element_type=jnp.float32)
    return (
        attended.reshape(tok_rows, q_heads * head_width),
        dquery.reshape(tok_rows, q_heads, head_width),
        key_grads,
        dvalues,
    )


def body(
    tokens,
    q_weight,
    k_weight,
    v_weight,
    q_gain,
    k_gain,
    windows,
    token_weight,
    loss_mask,
    grad_attn,
):
    tok_rows = tokens.shape[0]
    head_width = q_gain.shape[0]
    q_heads = q_weight.shape[1] // head_width
    kv_heads = k_weight.shape[1] // head_width
    pred_count = WINDOW // tok_rows
    key_span = (pred_count + 1) * tok_rows
    score_scale = QPRE ** (-0.5)
    first_row = lax.axis_index("seq") * tok_rows
    positions = first_row + jnp.arange(tok_rows, dtype=jnp.int32)
    key_pos = first_row - pred_count * tok_rows + jnp.arange(key_span, dtype=jnp.int32)
    kept_weight = token_weight * loss_mask.astype(jnp.float32)
    normalizer = lax.psum(jnp.sum(kept_weight), "seq")
    factor = kept_weight * (tok_rows * lax.axis_size("seq") / normalizer)
    cotangent = (
        (grad_attn.astype(jnp.float32) * factor[:, None])
        .astype(jnp.bfloat16)
        .reshape(tok_rows, q_heads, head_width)
    )
    row_pieces = (q_weight, k_weight, v_weight)
    contract = (((1,), (1,)), ((), ()))
    pieces_now = (
        lax.all_gather(row_pieces[0], "seq", axis=0, tiled=True),
        lax.all_gather(row_pieces[1], "seq", axis=0, tiled=True),
        lax.all_gather(row_pieces[2], "seq", axis=0, tiled=True),
    )
    q_linear, k_linear, v_linear = tuple(
        (jnp.dot(tokens, matrix, preferred_element_type=jnp.float32) for matrix in pieces_now)
    )
    q_linear = q_linear.reshape(tok_rows, q_heads, head_width)
    k_linear = k_linear.reshape(tok_rows, kv_heads, head_width)
    values = v_linear.astype(jnp.bfloat16)
    cosine, sine_table = rotate_table(positions, head_width)
    q_rot = norm_rotate(q_linear, q_gain, cosine, sine_table).astype(jnp.bfloat16)
    k_rot = norm_rotate(k_linear, k_gain, cosine, sine_table).astype(jnp.bfloat16)
    stacked = jnp.stack([k_rot.reshape(tok_rows, kv_heads * head_width), values])
    received = []
    for offset in range(1, pred_count + 1):
        received.append(passed_along(stacked, "seq", offset))
    extended = jnp.concatenate(received[::-1] + [stacked], axis=1)
    key_rows = extended[0].reshape(key_span, kv_heads, head_width)
    value_rows = extended[1].reshape(key_span, kv_heads, head_width)
    attended, dquery, key_grads, dvalues = block_grad(
        q_rot, key_rows, value_rows, cotangent, positions, key_pos, windows, score_scale
    )
    stacked_grads = jnp.stack(
        [
            key_grads.reshape(key_span, kv_heads * head_width),
            dvalues.reshape(key_span, kv_heads * head_width),
        ]
    )
    local_grads = stacked_grads[:, pred_count * tok_rows :]
    for offset in range(1, pred_count + 1):
        local_grads = local_grads + passed_along(
            stacked_grads[
                :, (pred_count - offset) * tok_rows : (pred_count - offset + 1) * tok_rows
            ].astype(jnp.bfloat16),
            "seq",
            -offset,
        ).astype(jnp.float32)
    key_total = local_grads[0].reshape(tok_rows, kv_heads, head_width)
    _, back_query = jax.vjp(
        lambda linear_in: norm_rotate(linear_in, q_gain, cosine, sine_table), q_linear
    )
    _, back_key = jax.vjp(
        lambda linear_in: norm_rotate(linear_in, k_gain, cosine, sine_table), k_linear
    )
    dq_lin = back_query(dquery)[0].astype(jnp.bfloat16).reshape(tok_rows, q_heads * head_width)
    dk_lin = back_key(key_total)[0].astype(jnp.bfloat16).reshape(tok_rows, kv_heads * head_width)
    dv_lin = local_grads[1].astype(jnp.bfloat16)
    joined_grad = jnp.concatenate([dq_lin, dk_lin, dv_lin], axis=1)
    joined_rows = jnp.concatenate([q_weight, k_weight, v_weight], axis=1)
    partial_grad = lax.dot_general(
        joined_grad,
        lax.all_gather(joined_rows, "seq", axis=0, tiled=True),
        contract,
        preferred_element_type=jnp.float32,
    )
    grad_tokens = lax.psum_scatter(
        partial_grad.astype(jnp.bfloat16), "head", scatter_dimension=1, tiled=True
    )
    return (attended, grad_tokens)


def solution(mesh):
    in_specs = (
        P("seq", None),
        P("seq", "head"),
        P("seq", "head"),
        P("seq", "head"),
        P(),
        P(),
        P("head"),
        P("seq"),
        P("seq"),
        P("seq", "head"),
    )
    out_specs = (P("seq", "head"), P("seq", "head"))
    return jax.shard_map(body, mesh=mesh, in_specs=in_specs, out_specs=out_specs, check_vma=False)
```

profile of v0, /device:TPU:38, one launch (start us, length us, event | category | flops | bytes accessed | tf_op | source)
XLA Modules:
  0.0 649.3 jit_solution(4675035902666896577)
XLA Ops:
  12.5 161.4 %psum.7 = f32[]{:T(128)} all-reduce(f32[]{:T(128)} %fusion.23), channel_id=1, replica_groups=mesh['seq'=64,'head'=4] {'seq'}, use_global_device_ids=true, to_apply=%region_5.6 | all-reduce | flops 1 | bytes 8 | tf_op jit(solution)/shard_map/psum | solution.py:111
  179.6 5.2 reshape.217
  188.2 67.9 %all-gather.11.cloned.1.call-done = bf16[64,84,256]{2,1,0:T(8,128)(2,1)} async-done(((bf16[1,84,256]{2,1,0:T(8,128)(2,1)}), bf16[64,84,256]{2,1,0:T(8,128)(2,1)}) %all-gather.11.cloned.1.call-update) | async-done | bytes 2752528 | tf_op jit(solution)/shard_map/all_gather | solution.py:123
  256.1 5.2 reshape.219
  264.7 5.3 collective-permute-start
  270.0 4.0 collective-permute-start.1
  280.0 4.8 collective-permute-start.3
  285.7 18.6 %collective-permute-done.1 = bf16[2,256,256]{2,1,0:T(8,128)(2,1)} collective-permute-done((bf16[2,256,256]{2,1,0:T(8,128)(2,1)}, bf16[2,256,256]{2,1,0:T(8,128)(2,1)}, u32[]{:S(2)}, u32[]{:S(2)}) %collective-permute-start.1) | collective-permute-done | bytes 262176 | tf_op jit(solution)/shard_map/ppermute | solution.py:16
  305.3 9.0 %collective-permute-done.2 = bf16[2,256,256]{2,1,0:T(8,128)(2,1)} collective-permute-done((bf16[2,256,256]{2,1,0:T(8,128)(2,1)}, bf16[2,256,256]{2,1,0:T(8,128)(2,1)}, u32[]{:S(2)}, u32[]{:S(2)}) %collective-permute-start.2) | collective-permute-done | bytes 262176 | tf_op jit(solution)/shard_map/ppermute | solution.py:16
  324.5 78.6 %all-gather.13.cloned.1.call-done = bf16[64,84,512]{2,1,0:T(8,128)(2,1)} async-done(((bf16[1,84,512]{2,1,0:T(8,128)(2,1)}), bf16[64,84,512]{2,1,0:T(8,128)(2,1)}) %all-gather.13.cloned.1.call-update) | async-done | bytes 5505040 | tf_op jit(solution)/shard_map/all_gather | solution.py:121
  403.1 8.9 %reshape.221 = bf16[5376,512]{1,0:T(8,128)(2,1)} reshape(bf16[64,84,512]{2,1,0:T(8,128)(2,1)} %all-gather.13.cloned.1.call-done) | data formatting | bytes 11010048
  412.0 4.9 fusion.35
  419.8 3.2 fusion.34
  437.9 4.2 fusion.28
  446.3 4.1 collective-permute-start.5
  450.5 5.3 collective-permute-start.6
  455.8 6.7 %collective-permute-start.7 = (bf16[2,256,256]{1,2,0:T(8,128)(2,1)}, bf16[2,256,256]{1,2,0:T(8,128)(2,1)}, u32[]{:S(2)}, u32[]{:S(2)}) collective-permute-start(bf16[2,256,256]{1,2,0:T(8,128)(2,1)} %get-tuple-element.15), channel_id=1, source_target_pairs={{16,0},{20,4},{24,8},{28,12},{32,16},{36,20},{40,24},{44,28},{48,3... | collective-permute-start | bytes 786440 | tf_op jit(solution)/shard_map/ppermute | solution.py:16
  465.4 10.9 %collective-permute-done.5 = bf16[2,256,256]{1,2,0:T(8,128)(2,1)} collective-permute-done((bf16[2,256,256]{1,2,0:T(8,128)(2,1)}, bf16[2,256,256]{1,2,0:T(8,128)(2,1)}, u32[]{:S(2)}, u32[]{:S(2)}) %collective-permute-start.5) | collective-permute-done | bytes 262176 | tf_op jit(solution)/shard_map/ppermute | solution.py:16
  476.3 16.6 %collective-permute-done.6 = bf16[2,256,256]{1,2,0:T(8,128)(2,1)} collective-permute-done((bf16[2,256,256]{1,2,0:T(8,128)(2,1)}, bf16[2,256,256]{1,2,0:T(8,128)(2,1)}, u32[]{:S(2)}, u32[]{:S(2)}) %collective-permute-start.6) | collective-permute-done | bytes 262176 | tf_op jit(solution)/shard_map/ppermute | solution.py:16
  493.0 8.8 %collective-permute-done.7 = bf16[2,256,256]{1,2,0:T(8,128)(2,1)} collective-permute-done((bf16[2,256,256]{1,2,0:T(8,128)(2,1)}, bf16[2,256,256]{1,2,0:T(8,128)(2,1)}, u32[]{:S(2)}, u32[]{:S(2)}) %collective-permute-start.7) | collective-permute-done | bytes 262176 | tf_op jit(solution)/shard_map/ppermute | solution.py:16
  503.6 82.0 %all-gather.15.cloned.1.call-done = bf16[64,84,1024]{2,1,0:T(8,128)(2,1)} async-done(((bf16[1,84,1024]{2,1,0:T(8,128)(2,1)}), bf16[64,84,1024]{2,1,0:T(8,128)(2,1)}) %all-gather.15.cloned.1.call-update) | async-done | bytes 11010064 | tf_op jit(solution)/shard_map/all_gather | solution.py:173
  585.7 13.9 %reshape.223 = bf16[5376,1024]{1,0:T(8,128)(2,1)} reshape(bf16[64,84,1024]{2,1,0:T(8,128)(2,1)} %all-gather.15.cloned.1.call-done) | data formatting | bytes 22020096
  599.5 8.9 %convolution_convert_fusion = bf16[256,5376]{0,1:T(8,128)(2,1)} fusion(bf16[5376,1024]{1,0:T(8,128)(2,1)} %reshape.223, bf16[256,256]{1,0:T(8,128)(2,1)S(1)} %copy.121, bf16[256,256]{1,0:T(8,128)(2,1)S(1)} %copy.120, bf16[256,512]{1,0:T(8,128)(2,1)S(1)} %bitcast.92), kind=kOutput, calls=%fused_computation | convolution fusion | flops 2821521408 | bytes 14286848 | tf_op jit(solution)/shard_map/dot_general | solution.py:171
  610.2 32.6 %reduce-scatter.2.cloned.1.call-done = bf16[256,1344]{0,1:T(8,128)(2,1)} async-done(((bf16[256,5376]{0,1:T(8,128)(2,1)}), bf16[256,1344]{0,1:T(8,128)(2,1)}) %reduce-scatter.2.cloned.1.call-update) | async-done | bytes 688144 | tf_op jit(solution)/shard_map/reduce_scatter | solution.py:177
  (163 shorter events, 63.0 us)
Async XLA Ops:
  7.2 177.6 %copy-start = (bf16[256,5376]{1,0:T(8,128)(2,1)S(1)}, bf16[256,5376]{1,0:T(8,128)(2,1)}, u32[]{:S(2)}) copy-start(bf16[256,5376]{1,0:T(8,128)(2,1)} %param.10) | copy-start | bytes 8257540
  7.2 172.4 %all-gather.9.cloned.1.call-start = ((), (), s32[]{:S(2)}) async-start(), calls=%async_computation.2 | async-start | bytes 2928640 | tf_op jit(solution)/shard_map/all_gather | solution.py:122
  7.9 248.2 %all-gather.11.cloned.1.call-start = ((), (), s32[]{:S(2)}) async-start(), calls=%async_computation.3 | async-start | bytes 2928640 | tf_op jit(solution)/shard_map/all_gather | solution.py:123
  8.7 394.5 %all-gather.13.cloned.1.call-start = ((), (), s32[]{:S(2)}) async-start(), calls=%async_computation.4 | async-start | bytes 5857280 | tf_op jit(solution)/shard_map/all_gather | solution.py:121
  9.4 576.3 %all-gather.15.cloned.1.call-start = ((), (), s32[]{:S(2)}) async-start(), calls=%async_computation.5 | async-start | bytes 11714560 | tf_op jit(solution)/shard_map/all_gather | solution.py:173
  11.1 631.7 %reduce-scatter.2.cloned.1.call-start = ((), (), s32[]{:S(2)}) async-start(), calls=%async_computation.1 | async-start | bytes 3440640 | tf_op jit(solution)/shard_map/reduce_scatter | solution.py:177
  174.4 244.7 %copy-start.9 = (f32[256,64]{1,0:T(8,128)}, f32[256,64]{1,0:T(8,128)S(1)}, u32[]{:S(2)}) copy-start(f32[256,64]{1,0:T(8,128)S(1)} %get-tuple-element.28) | copy-start | bytes 196612
  174.4 244.7 %copy-start.11 = (f32[256,64]{1,0:T(8,128)}, f32[256,64]{1,0:T(8,128)S(1)}, u32[]{:S(2)}) copy-start(f32[256,64]{1,0:T(8,128)S(1)} %get-tuple-element.29) | copy-start | bytes 196612
  261.2 16.3 %copy-start.38 = (s32[4]{0:T(128)S(1)}, s32[4]{0:T(128)}, u32[]{:S(2)}) copy-start(s32[4]{0:T(128)} %param.16) | copy-start | bytes 52
  264.7 20.1 %collective-permute-start = (bf16[2,256,256]{2,1,0:T(8,128)(2,1)}, bf16[2,256,256]{2,1,0:T(8,128)(2,1)}, u32[]{:S(2)}, u32[]{:S(2)}) collective-permute-start(bf16[2,256,256]{2,1,0:T(8,128)(2,1)} %pad_maximum_fusion.1), channel_id=1, source_target_pairs={{0,16},{4,20},{8,24},{12,28},{16,32},{20,36},{24,40},{28,44},{32,4... | collective-permute-start | bytes 786440 | tf_op jit(solution)/shard_map/ppermute | solution.py:16
  270.0 34.3 %collective-permute-start.1 = (bf16[2,256,256]{2,1,0:T(8,128)(2,1)}, bf16[2,256,256]{2,1,0:T(8,128)(2,1)}, u32[]{:S(2)}, u32[]{:S(2)}) collective-permute-start(bf16[2,256,256]{2,1,0:T(8,128)(2,1)} %pad_maximum_fusion.1), channel_id=1, source_target_pairs={{0,12},{4,16},{8,20},{12,24},{16,28},{20,32},{24,36},{28,40},{32,4... | collective-permute-start | bytes 786440 | tf_op jit(solution)/shard_map/ppermute | solution.py:16
  274.8 39.5 %collective-permute-start.2 = (bf16[2,256,256]{2,1,0:T(8,128)(2,1)}, bf16[2,256,256]{2,1,0:T(8,128)(2,1)}, u32[]{:S(2)}, u32[]{:S(2)}) collective-permute-start(bf16[2,256,256]{2,1,0:T(8,128)(2,1)} %pad_maximum_fusion.1), channel_id=1, source_target_pairs={{0,8},{4,12},{8,16},{12,20},{16,24},{20,28},{24,32},{28,36},{32,40... | collective-permute-start | bytes 786440 | tf_op jit(solution)/shard_map/ppermute | solution.py:16
  280.0 35.4 %collective-permute-start.3 = (bf16[2,256,256]{2,1,0:T(8,128)(2,1)}, bf16[2,256,256]{2,1,0:T(8,128)(2,1)S(1)}, u32[]{:S(2)}, u32[]{:S(2)}) collective-permute-start(bf16[2,256,256]{2,1,0:T(8,128)(2,1)} %pad_maximum_fusion.1), channel_id=1, source_target_pairs={{0,4},{4,8},{8,12},{12,16},{16,20},{20,24},{24,28},{28,32},{32,36}... | collective-permute-start | bytes 786440 | tf_op jit(solution)/shard_map/ppermute | solution.py:16
  442.1 21.3 %copy-start.17 = (f32[256,4]{1,0:T(8,128)S(1)}, f32[256,4]{1,0:T(8,128)}, u32[]{:S(2)}) copy-start(f32[256,4]{1,0:T(8,128)} %copy-done.16) | copy-start | bytes 12292
  442.1 21.3 %copy-start.31 = (f32[128]{0:T(128)S(1)}, f32[128]{0:T(128)}, u32[]{:S(2)}) copy-start(f32[128]{0:T(128)} %param.14) | copy-start | bytes 1540
  443.5 21.9 %collective-permute-start.4 = (bf16[2,256,256]{1,2,0:T(8,128)(2,1)}, bf16[2,256,256]{1,2,0:T(8,128)(2,1)}, u32[]{:S(2)}, u32[]{:S(2)}) collective-permute-start(bf16[2,256,256]{1,2,0:T(8,128)(2,1)} %get-tuple-element.14), channel_id=1, source_target_pairs={{4,0},{8,4},{12,8},{16,12},{20,16},{24,20},{28,24},{32,28},{36,32}... | collective-permute-start | bytes 786440 | tf_op jit(solution)/shard_map/ppermute | solution.py:16
  446.3 30.0 %collective-permute-start.5 = (bf16[2,256,256]{1,2,0:T(8,128)(2,1)}, bf16[2,256,256]{1,2,0:T(8,128)(2,1)}, u32[]{:S(2)}, u32[]{:S(2)}) collective-permute-start(bf16[2,256,256]{1,2,0:T(8,128)(2,1)} %get-tuple-element.17), channel_id=1, source_target_pairs={{8,0},{12,4},{16,8},{20,12},{24,16},{28,20},{32,24},{36,28},{40,32... | collective-permute-start | bytes 786440 | tf_op jit(solution)/shard_map/ppermute | solution.py:16
  450.5 42.5 %collective-permute-start.6 = (bf16[2,256,256]{1,2,0:T(8,128)(2,1)}, bf16[2,256,256]{1,2,0:T(8,128)(2,1)}, u32[]{:S(2)}, u32[]{:S(2)}) collective-permute-start(bf16[2,256,256]{1,2,0:T(8,128)(2,1)} %get-tuple-element.16), channel_id=1, source_target_pairs={{12,0},{16,4},{20,8},{24,12},{28,16},{32,20},{36,24},{40,28},{44,3... | collective-permute-start | bytes 786440 | tf_op jit(solution)/shard_map/ppermute | solution.py:16
  455.8 45.9 %collective-permute-start.7 = (bf16[2,256,256]{1,2,0:T(8,128)(2,1)}, bf16[2,256,256]{1,2,0:T(8,128)(2,1)}, u32[]{:S(2)}, u32[]{:S(2)}) collective-permute-start(bf16[2,256,256]{1,2,0:T(8,128)(2,1)} %get-tuple-element.15), channel_id=1, source_target_pairs={{16,0},{20,4},{24,8},{28,12},{32,16},{36,20},{40,24},{44,28},{48,3... | collective-permute-start | bytes 786440 | tf_op jit(solution)/shard_map/ppermute | solution.py:16
  463.4 38.3 %copy-start.7 = (f32[2,128,1280,1]{2,1,3,0:T(8,128)S(1)}, f32[2,128,1280,1]{2,1,3,0:T(8,128)}, u32[]{:S(2)}) copy-start(f32[2,128,1280,1]{2,1,3,0:T(8,128)} %copy-done.6) | copy-start | bytes 3932164
  465.3 37.8 %copy-start.22 = (f32[256,64]{0,1:T(8,128)S(1)}, f32[256,64]{0,1:T(8,128)}, u32[]{:S(2)}) copy-start(f32[256,64]{0,1:T(8,128)} %copy.98) | copy-start | bytes 196612
  465.3 37.8 %copy-start.24 = (f32[256,64]{0,1:T(8,128)S(1)}, f32[256,64]{0,1:T(8,128)}, u32[]{:S(2)}) copy-start(f32[256,64]{0,1:T(8,128)} %copy.99) | copy-start | bytes 196612
  465.4 37.8 %copy-start.33 = (f32[128]{0:T(128)S(1)}, f32[128]{0:T(128)}, u32[]{:S(2)}) copy-start(f32[128]{0:T(128)} %param.15) | copy-start | bytes 1540
  599.5 43.2 %copy-start.1 = (bf16[256,5376]{1,0:T(8,128)(2,1)S(1)}, bf16[256,5376]{1,0:T(8,128)(2,1)}, u32[]{:S(2)}) copy-start(bf16[256,5376]{1,0:T(8,128)(2,1)} %param.10) | copy-start | bytes 8257540
  (28 other events, 86.8 us)
Sparse Core Ops, SparseCore 0:
  11.5 123.1 all-gather.8
  138.2 117.7 all-gather.10
  259.6 143.5 all-gather.12
  406.6 179.0 all-gather.14
  608.6 34.1 reduce-scatter.1
where the time goes:
time: 652 us; the launch traced here: 649 us
  waiting for transfers between devices  327 us (50%)
  blocking collectives  161 us (25%)
  local copies, waits for them, and re-layouts  56.8 us (9%)
  matrix products  36.2 us (6%)
  starting transfers between devices  36 us (6%)
  other arithmetic  16.4 us (3%)
  between operations  15.3 us (2%)
    psum x1, blocking collectives, body(): normalizer = lax.psum(jnp.sum(kept_weight), 'seq')  161 us
    all_gather x1, waiting for transfers between devices, body(): lax.all_gather(joined_rows, 'seq', axis=0, tiled=True)  82 us
    all_gather x1, waiting for transfers between devices, body(): lax.all_gather(row_pieces[0], 'seq', axis=0, tiled=True)  78.6 us
    all_gather x1, waiting for transfers between devices, body(): lax.all_gather(row_pieces[2], 'seq', axis=0, tiled=True)  67.9 us
    ppermute x8, waiting for transfers between devices, passed_along(): return lax.ppermute(block, axis, route)  64 us
    unnamed x90, local copies, waits for them, and re-layouts  39.9 us
    ppermute x8, starting transfers between devices, passed_along(): return lax.ppermute(block, axis, route)  35.8 us
    reduce_scatter x1, waiting for transfers between devices, body(): lax.psum_scatter(partial_grad.astype(jnp.bfloat16), 'head', scatter_dimen...  32.6 us
  transfers between devices with their start and end apart: 13, of which 9 were waited for; matrix products, arithmetic and copies ran while one was open for 13% of the time, Pallas kernels for 0%

commit v1 on v0

--- a/solution.py
+++ b/solution.py
@@ -115,16 +115,16 @@
         .astype(jnp.bfloat16)
         .reshape(tok_rows, q_heads, head_width)
     )
-    row_pieces = (q_weight, k_weight, v_weight)
     contract = (((1,), (1,)), ((), ()))
-    pieces_now = (
-        lax.all_gather(row_pieces[0], "seq", axis=0, tiled=True),
-        lax.all_gather(row_pieces[1], "seq", axis=0, tiled=True),
-        lax.all_gather(row_pieces[2], "seq", axis=0, tiled=True),
+    q_cols = q_weight.shape[1]
+    k_cols = k_weight.shape[1]
+    joined_rows = lax.all_gather(
+        jnp.concatenate([q_weight, k_weight, v_weight], axis=1), "seq", axis=0, tiled=True
     )
-    q_linear, k_linear, v_linear = tuple(
-        (jnp.dot(tokens, matrix, preferred_element_type=jnp.float32) for matrix in pieces_now)
-    )
+    all_linear = jnp.dot(tokens, joined_rows, preferred_element_type=jnp.float32)
+    q_linear = all_linear[:, :q_cols]
+    k_linear = all_linear[:, q_cols : q_cols + k_cols]
+    v_linear = all_linear[:, q_cols + k_cols :]
     q_linear = q_linear.reshape(tok_rows, q_heads, head_width)
     k_linear = k_linear.reshape(tok_rows, kv_heads, head_width)
     values = v_linear.astype(jnp.bfloat16)
@@ -167,10 +167,9 @@
     dk_lin = back_key(key_total)[0].astype(jnp.bfloat16).reshape(tok_rows, kv_heads * head_width)
     dv_lin = local_grads[1].astype(jnp.bfloat16)
     joined_grad = jnp.concatenate([dq_lin, dk_lin, dv_lin], axis=1)
-    joined_rows = jnp.concatenate([q_weight, k_weight, v_weight], axis=1)
     partial_grad = lax.dot_general(
         joined_grad,
-        lax.all_gather(joined_rows, "seq", axis=0, tiled=True),
+        joined_rows,
         contract,
         preferred_element_type=jnp.float32,
     )

time: 652 us -> 370 us (0.57)
  waiting for transfers between devices: 327 us -> 87.4 us
  local copies, waits for them, and re-layouts: 56.8 us -> 24.2 us
  matrix products: 36.2 us -> 21 us
  starting transfers between devices: 36 us -> 45.2 us
    all_gather x4 -> x1, waiting for transfers between devices: 228 us -> 0.01 us  [body(): lax.all_gather(jnp.concatenate([q_weight, k_weight, v_weight], axis=1), '...]
    unnamed x90 -> x30, local copies, waits for them, and re-layouts: 39.9 us -> 18.9 us
    ppermute x8, waiting for transfers between devices: 64 us -> 50.1 us  [passed_along(): return lax.ppermute(block, axis, route)]
    dot_general x4 -> x2, matrix products: 19.6 us -> 10.3 us  [the longest x1 5.86 us: body(): jnp.dot(tokens, joined_rows, preferred_element_type=jnp.float32)]
    ppermute x8, starting transfers between devices: 35.8 us -> 45.1 us  [passed_along(): return lax.ppermute(block, axis, route)]
  transfers between devices with their start and end apart: 13 -> 10, of which waited for: 9 -> 7; matrix products, arithmetic and copies ran while one was open for 13% -> 4% of each run, Pallas kernels for 0% -> 0%
where the time goes in v1:
time: 370 us; the launch traced here: 368 us
  blocking collectives  163 us (44%)
  waiting for transfers between devices  87.4 us (24%)
  starting transfers between devices  45.2 us (12%)
  local copies, waits for them, and re-layouts  24.2 us (7%)
  matrix products  21 us (6%)
  between operations  15.2 us (4%)
  other arithmetic  12.1 us (3%)
    psum x1, blocking collectives, body(): normalizer = lax.psum(jnp.sum(kept_weight), 'seq')  163 us
    ppermute x8, waiting for transfers between devices, passed_along(): return lax.ppermute(block, axis, route)  50.1 us
    ppermute x8, starting transfers between devices, passed_along(): return lax.ppermute(block, axis, route)  45.1 us
    reduce_scatter x1, waiting for transfers between devices, body(): lax.psum_scatter(partial_grad.astype(jnp.bfloat16), 'head', scatter_dimen...  37.3 us
    unnamed x30, local copies, waits for them, and re-layouts  18.9 us
  transfers between devices with their start and end apart: 10, of which 7 were waited for; matrix products, arithmetic and copies ran while one was open for 4% of the time, Pallas kernels for 0%

profile of v1, /device:TPU:38, one launch (start us, length us, event | category | flops | bytes accessed | tf_op | source)
XLA Modules:
  0.0 367.9 jit_solution(1612949384198747687)
XLA Ops:
  10.4 162.8 %psum.7 = f32[]{:T(128)} all-reduce(f32[]{:T(128)} %fusion.21), channel_id=1, replica_groups=mesh['seq'=64,'head'=4] {'seq'}, use_global_device_ids=true, to_apply=%region_5.6 | all-reduce | flops 1 | bytes 8 | tf_op jit(solution)/shard_map/psum | solution.py:111
  179.2 14.0 %reshape.217 = bf16[5376,1024]{1,0:T(8,128)(2,1)} reshape(bf16[64,84,1024]{2,1,0:T(8,128)(2,1)} %all-gather.3.cloned.1.call-done) | data formatting | bytes 22020096
  193.3 5.9 %convolution_bitcast_fusion.1 = f32[256,1024]{0,1:T(8,128)S(1)} fusion(bf16[5376,1024]{1,0:T(8,128)(2,1)} %reshape.217, bf16[256,5376]{1,0:T(8,128)(2,1)S(1)} %copy-done), kind=kOutput, calls=%fused_computation.15 | convolution fusion | flops 2818572288 | bytes 14811136 | tf_op jit(solution)/shard_map/dot_general | solution.py:124
  200.2 5.2 %collective-permute-start = (bf16[2,256,256]{1,2,0:T(8,128)(2,1)}, bf16[2,256,256]{1,2,0:T(8,128)(2,1)}, u32[]{:S(2)}, u32[]{:S(2)}) collective-permute-start(bf16[2,256,256]{1,2,0:T(8,128)(2,1)} %pad_maximum_fusion.1), channel_id=1, source_target_pairs={{0,16},{4,20},{8,24},{12,28},{16,32},{20,36},{24,40},{28,44},{32,4... | collective-permute-start | bytes 786440 | tf_op jit(solution)/shard_map/ppermute | solution.py:16
  205.3 8.9 %collective-permute-start.1 = (bf16[2,256,256]{1,2,0:T(8,128)(2,1)}, bf16[2,256,256]{1,2,0:T(8,128)(2,1)}, u32[]{:S(2)}, u32[]{:S(2)}) collective-permute-start(bf16[2,256,256]{1,2,0:T(8,128)(2,1)} %pad_maximum_fusion.1), channel_id=1, source_target_pairs={{0,12},{4,16},{8,20},{12,24},{16,28},{20,32},{24,36},{28,40},{32,4... | collective-permute-start | bytes 786440 | tf_op jit(solution)/shard_map/ppermute | solution.py:16
  214.3 5.3 %collective-permute-start.2 = (bf16[2,256,256]{1,2,0:T(8,128)(2,1)}, bf16[2,256,256]{1,2,0:T(8,128)(2,1)}, u32[]{:S(2)}, u32[]{:S(2)}) collective-permute-start(bf16[2,256,256]{1,2,0:T(8,128)(2,1)} %pad_maximum_fusion.1), channel_id=1, source_target_pairs={{0,8},{4,12},{8,16},{12,20},{16,24},{20,28},{24,32},{28,36},{32,40... | collective-permute-start | bytes 786440 | tf_op jit(solution)/shard_map/ppermute | solution.py:16
  219.6 7.3 %collective-permute-start.3 = (bf16[2,256,256]{1,2,0:T(8,128)(2,1)}, bf16[2,256,256]{1,2,0:T(8,128)(2,1)}, u32[]{:S(2)}, u32[]{:S(2)}) collective-permute-start(bf16[2,256,256]{1,2,0:T(8,128)(2,1)} %pad_maximum_fusion.1), channel_id=1, source_target_pairs={{0,4},{4,8},{8,12},{12,16},{16,20},{20,24},{24,28},{28,32},{32,36}... | collective-permute-start | bytes 786440 | tf_op jit(solution)/shard_map/ppermute | solution.py:16
  232.5 7.8 %collective-permute-done.1 = bf16[2,256,256]{1,2,0:T(8,128)(2,1)} collective-permute-done((bf16[2,256,256]{1,2,0:T(8,128)(2,1)}, bf16[2,256,256]{1,2,0:T(8,128)(2,1)}, u32[]{:S(2)}, u32[]{:S(2)}) %collective-permute-start.1) | collective-permute-done | bytes 262176 | tf_op jit(solution)/shard_map/ppermute | solution.py:16
  241.3 6.5 %collective-permute-done.2 = bf16[2,256,256]{1,2,0:T(8,128)(2,1)} collective-permute-done((bf16[2,256,256]{1,2,0:T(8,128)(2,1)}, bf16[2,256,256]{1,2,0:T(8,128)(2,1)}, u32[]{:S(2)}, u32[]{:S(2)}) %collective-permute-start.2) | collective-permute-done | bytes 262176 | tf_op jit(solution)/shard_map/ppermute | solution.py:16
  248.7 2.1 collective-permute-done.3
  252.0 2.1 fusion.31
  254.1 2.3 select_reduce_fusion
  256.4 1.9 multiply_reduce_fusion.1
  258.3 2.0 fusion.26
  260.4 3.1 fusion.1
  265.5 6.7 %collective-permute-start.4 = (bf16[2,256,256]{1,2,0:T(8,128)(2,1)S(1)}, bf16[2,256,256]{1,2,0:T(8,128)(2,1)S(1)}, u32[]{:S(2)}, u32[]{:S(2)}) collective-permute-start(bf16[2,256,256]{1,2,0:T(8,128)(2,1)S(1)} %get-tuple-element.8), channel_id=1, source_target_pairs={{4,0},{8,4},{12,8},{16,12},{20,16},{24,20},{28,24},{32,28},{36,32}... | collective-permute-start | bytes 786440 | tf_op jit(solution)/shard_map/ppermute | solution.py:16
  272.2 3.9 %collective-permute-start.5 = (bf16[2,256,256]{1,2,0:T(8,128)(2,1)S(1)}, bf16[2,256,256]{1,2,0:T(8,128)(2,1)S(1)}, u32[]{:S(2)}, u32[]{:S(2)}) collective-permute-start(bf16[2,256,256]{1,2,0:T(8,128)(2,1)S(1)} %get-tuple-element.11), channel_id=1, source_target_pairs={{8,0},{12,4},{16,8},{20,12},{24,16},{28,20},{32,24},{36,28},{40,32... | collective-permute-start | bytes 786440 | tf_op jit(solution)/shard_map/ppermute | solution.py:16
  276.1 1.9 collective-permute-start.6
  278.1 5.9 %collective-permute-start.7 = (bf16[2,256,256]{1,2,0:T(8,128)(2,1)S(1)}, bf16[2,256,256]{1,2,0:T(8,128)(2,1)S(1)}, u32[]{:S(2)}, u32[]{:S(2)}) collective-permute-start(bf16[2,256,256]{1,2,0:T(8,128)(2,1)S(1)} %get-tuple-element.9), channel_id=1, source_target_pairs={{16,0},{20,4},{24,8},{28,12},{32,16},{36,20},{40,24},{44,28},{48,3... | collective-permute-start | bytes 786440 | tf_op jit(solution)/shard_map/ppermute | solution.py:16
  284.3 9.0 %collective-permute-done.5 = bf16[2,256,256]{1,2,0:T(8,128)(2,1)S(1)} collective-permute-done((bf16[2,256,256]{1,2,0:T(8,128)(2,1)S(1)}, bf16[2,256,256]{1,2,0:T(8,128)(2,1)S(1)}, u32[]{:S(2)}, u32[]{:S(2)}) %collective-permute-start.5) | collective-permute-done | bytes 262176 | tf_op jit(solution)/shard_map/ppermute | solution.py:16
  293.2 19.4 %collective-permute-done.6 = bf16[2,256,256]{1,2,0:T(8,128)(2,1)S(1)} collective-permute-done((bf16[2,256,256]{1,2,0:T(8,128)(2,1)S(1)}, bf16[2,256,256]{1,2,0:T(8,128)(2,1)S(1)}, u32[]{:S(2)}, u32[]{:S(2)}) %collective-permute-start.6) | collective-permute-done | bytes 262176 | tf_op jit(solution)/shard_map/ppermute | solution.py:16
  312.6 5.3 %collective-permute-done.7 = bf16[2,256,256]{1,2,0:T(8,128)(2,1)S(1)} collective-permute-done((bf16[2,256,256]{1,2,0:T(8,128)(2,1)S(1)}, bf16[2,256,256]{1,2,0:T(8,128)(2,1)S(1)}, u32[]{:S(2)}, u32[]{:S(2)}) %collective-permute-start.7) | collective-permute-done | bytes 262176 | tf_op jit(solution)/shard_map/ppermute | solution.py:16
  318.5 4.4 %convolution_convert_fusion = bf16[256,5376]{0,1:T(8,128)(2,1)} fusion(bf16[5376,1024]{1,0:T(8,128)(2,1)S(1)} %bitcast.86, bf16[256,256]{0,1:T(8,128)(2,1)S(1)} %fusion.18, bf16[256,256]{0,1:T(8,128)(2,1)S(1)} %bitcast.105, bf16[256,512]{0,1:T(8,128)(2,1)S(1)} %bitcast.101), kind=kOutput, calls=%fused_computation | convolution fusion | flops 2821521408 | bytes 14286848 | tf_op jit(solution)/shard_map/dot_general | solution.py:170
  323.8 37.3 %reduce-scatter.2.cloned.1.call-done = bf16[256,1344]{0,1:T(8,128)(2,1)} async-done(((bf16[256,5376]{0,1:T(8,128)(2,1)}), bf16[256,1344]{0,1:T(8,128)(2,1)}) %reduce-scatter.2.cloned.1.call-update) | async-done | bytes 688144 | tf_op jit(solution)/shard_map/reduce_scatter | solution.py:176
  (81 shorter events, 21.6 us)
Async XLA Ops:
  7.2 186.1 %copy-start = (bf16[256,5376]{1,0:T(8,128)(2,1)S(1)}, bf16[256,5376]{1,0:T(8,128)(2,1)}, u32[]{:S(2)}) copy-start(bf16[256,5376]{1,0:T(8,128)(2,1)} %param.10) | copy-start | bytes 8257540
  7.2 172.1 %all-gather.3.cloned.1.call-start = ((), (), s32[]{:S(2)}) async-start(), calls=%async_computation.2 | async-start | bytes 11714560 | tf_op jit(solution)/shard_map/all_gather | solution.py:121
  9.0 352.1 %reduce-scatter.2.cloned.1.call-start = ((), (), s32[]{:S(2)}) async-start(), calls=%async_computation.1 | async-start | bytes 3440640 | tf_op jit(solution)/shard_map/reduce_scatter | solution.py:176
  193.3 6.0 %copy-start.8 = (f32[128]{0:T(128)S(1)}, f32[128]{0:T(128)}, u32[]{:S(2)}) copy-start(f32[128]{0:T(128)} %param.15) | copy-start | bytes 1540
  199.1 27.9 %copy-start.1 = (f32[256,1024]{0,1:T(8,128)}, f32[256,1024]{0,1:T(8,128)S(1)}, u32[]{:S(2)}) copy-start(f32[256,1024]{0,1:T(8,128)S(1)} %convolution_bitcast_fusion.1) | copy-start | bytes 3145732
  199.1 27.9 %copy-start.7 = (f32[128]{0:T(128)S(1)}, f32[128]{0:T(128)}, u32[]{:S(2)}) copy-start(f32[128]{0:T(128)} %param.14) | copy-start | bytes 1540
  200.2 31.2 %collective-permute-start = (bf16[2,256,256]{1,2,0:T(8,128)(2,1)}, bf16[2,256,256]{1,2,0:T(8,128)(2,1)}, u32[]{:S(2)}, u32[]{:S(2)}) collective-permute-start(bf16[2,256,256]{1,2,0:T(8,128)(2,1)} %pad_maximum_fusion.1), channel_id=1, source_target_pairs={{0,16},{4,20},{8,24},{12,28},{16,32},{20,36},{24,40},{28,44},{32,4... | collective-permute-start | bytes 786440 | tf_op jit(solution)/shard_map/ppermute | solution.py:16
  205.3 34.9 %collective-permute-start.1 = (bf16[2,256,256]{1,2,0:T(8,128)(2,1)}, bf16[2,256,256]{1,2,0:T(8,128)(2,1)}, u32[]{:S(2)}, u32[]{:S(2)}) collective-permute-start(bf16[2,256,256]{1,2,0:T(8,128)(2,1)} %pad_maximum_fusion.1), channel_id=1, source_target_pairs={{0,12},{4,16},{8,20},{12,24},{16,28},{20,32},{24,36},{28,40},{32,4... | collective-permute-start | bytes 786440 | tf_op jit(solution)/shard_map/ppermute | solution.py:16
  214.3 33.5 %collective-permute-start.2 = (bf16[2,256,256]{1,2,0:T(8,128)(2,1)}, bf16[2,256,256]{1,2,0:T(8,128)(2,1)}, u32[]{:S(2)}, u32[]{:S(2)}) collective-permute-start(bf16[2,256,256]{1,2,0:T(8,128)(2,1)} %pad_maximum_fusion.1), channel_id=1, source_target_pairs={{0,8},{4,12},{8,16},{12,20},{16,24},{20,28},{24,32},{28,36},{32,40... | collective-permute-start | bytes 786440 | tf_op jit(solution)/shard_map/ppermute | solution.py:16
  219.6 31.3 %collective-permute-start.3 = (bf16[2,256,256]{1,2,0:T(8,128)(2,1)}, bf16[2,256,256]{1,2,0:T(8,128)(2,1)}, u32[]{:S(2)}, u32[]{:S(2)}) collective-permute-start(bf16[2,256,256]{1,2,0:T(8,128)(2,1)} %pad_maximum_fusion.1), channel_id=1, source_target_pairs={{0,4},{4,8},{8,12},{12,16},{16,20},{20,24},{24,28},{28,32},{32,36}... | collective-permute-start | bytes 786440 | tf_op jit(solution)/shard_map/ppermute | solution.py:16
  231.4 20.6 %copy-start.3 = (s32[256,1280]{0,1:T(8,128)S(1)}, s32[256,1280]{0,1:T(8,128)}, u32[]{:S(2)}) copy-start(s32[256,1280]{0,1:T(8,128)} %broadcast_subtract_fusion) | copy-start | bytes 3932164
  231.4 20.6 %copy-start.4 = (bf16[256,4,64]{2,0,1:T(8,128)(2,1)S(1)}, bf16[256,4,64]{2,0,1:T(8,128)(2,1)}, u32[]{:S(2)}) copy-start(bf16[256,4,64]{2,0,1:T(8,128)(2,1)} %copy.36) | copy-start | bytes 393220
  231.4 20.6 %copy-start.5 = (bf16[256,4,64]{2,0,1:T(8,128)(2,1)S(1)}, bf16[256,4,64]{2,0,1:T(8,128)(2,1)}, u32[]{:S(2)}) copy-start(bf16[256,4,64]{2,0,1:T(8,128)(2,1)} %copy.37) | copy-start | bytes 393220
  254.1 2.3 copy-start.6
  264.0 54.4 %slice-start = ((s8[11010048]{0:T(1024)(128)(4,1)}), s8[4194304]{0:T(1024)(128)(4,1)S(1)}, s32[]{:S(2)}) async-start(s8[11010048]{0:T(1024)(128)(4,1)} %bitcast.85), calls=%async_computation.3 | async-start | bytes 8388608
  265.2 18.8 %copy-start.2 = (f32[256,1024]{0,1:T(8,128)S(1)}, f32[256,1024]{0,1:T(8,128)}, u32[]{:S(2)}) copy-start(f32[256,1024]{0,1:T(8,128)} %copy-done.1) | copy-start | bytes 3145732
  265.2 53.3 %slice-start.1 = ((s8[11010048]{0:T(1024)(128)(4,1)}), s8[4194304]{0:T(1024)(128)(4,1)S(1)}, s32[]{:S(2)}) async-start(s8[11010048]{0:T(1024)(128)(4,1)} %bitcast.85), calls=%async_computation.4 | async-start | bytes 8388608
  265.5 18.8 %collective-permute-start.4 = (bf16[2,256,256]{1,2,0:T(8,128)(2,1)S(1)}, bf16[2,256,256]{1,2,0:T(8,128)(2,1)S(1)}, u32[]{:S(2)}, u32[]{:S(2)}) collective-permute-start(bf16[2,256,256]{1,2,0:T(8,128)(2,1)S(1)} %get-tuple-element.8), channel_id=1, source_target_pairs={{4,0},{8,4},{12,8},{16,12},{20,16},{24,20},{28,24},{32,28},{36,32}... | collective-permute-start | bytes 786440 | tf_op jit(solution)/shard_map/ppermute | solution.py:16
  272.2 21.0 %collective-permute-start.5 = (bf16[2,256,256]{1,2,0:T(8,128)(2,1)S(1)}, bf16[2,256,256]{1,2,0:T(8,128)(2,1)S(1)}, u32[]{:S(2)}, u32[]{:S(2)}) collective-permute-start(bf16[2,256,256]{1,2,0:T(8,128)(2,1)S(1)} %get-tuple-element.11), channel_id=1, source_target_pairs={{8,0},{12,4},{16,8},{20,12},{24,16},{28,20},{32,24},{36,28},{40,32... | collective-permute-start | bytes 786440 | tf_op jit(solution)/shard_map/ppermute | solution.py:16
  276.1 36.5 %collective-permute-start.6 = (bf16[2,256,256]{1,2,0:T(8,128)(2,1)S(1)}, bf16[2,256,256]{1,2,0:T(8,128)(2,1)S(1)}, u32[]{:S(2)}, u32[]{:S(2)}) collective-permute-start(bf16[2,256,256]{1,2,0:T(8,128)(2,1)S(1)} %get-tuple-element.10), channel_id=1, source_target_pairs={{12,0},{16,4},{20,8},{24,12},{28,16},{32,20},{36,24},{40,28},{44,3... | collective-permute-start | bytes 786440 | tf_op jit(solution)/shard_map/ppermute | solution.py:16
  278.1 39.9 %collective-permute-start.7 = (bf16[2,256,256]{1,2,0:T(8,128)(2,1)S(1)}, bf16[2,256,256]{1,2,0:T(8,128)(2,1)S(1)}, u32[]{:S(2)}, u32[]{:S(2)}) collective-permute-start(bf16[2,256,256]{1,2,0:T(8,128)(2,1)S(1)} %get-tuple-element.9), channel_id=1, source_target_pairs={{16,0},{20,4},{24,8},{28,12},{32,16},{36,20},{40,24},{44,28},{48,3... | collective-permute-start | bytes 786440 | tf_op jit(solution)/shard_map/ppermute | solution.py:16
  284.1 34.4 %slice-start.2 = ((s8[11010048]{0:T(1024)(128)(4,1)}), s8[2621440]{0:T(1024)(128)(4,1)S(1)}, s32[]{:S(2)}) async-start(s8[11010048]{0:T(1024)(128)(4,1)} %bitcast.85), calls=%async_computation.5 | async-start | bytes 5242880
Sparse Core Ops, SparseCore 0:
  12.2 166.6 all-gather.2
  323.0 37.9 reduce-scatter.1

commit v2 on v1

--- a/solution.py
+++ b/solution.py
@@ -14,6 +14,31 @@
     devices = range(lax.axis_size(axis))
     route = [(i - distance, i) for i in devices if i - distance in devices]
     return lax.ppermute(block, axis, route)
+
+
+def butterfly_sum(value, axis):
+    size = lax.axis_size(axis)
+    step = 1
+    while step < size:
+        value = value + lax.ppermute(value, axis, [(i, i ^ step) for i in range(size)])
+        step *= 2
+    return value
+
+
+def head_scatter_sum(partial, axis):
+    rows, width = partial.shape
+    index = lax.axis_index(axis)
+    parts = partial.reshape(rows, 2, 2, width // 4)
+    low_bit = index % 2
+    high_bit = index // 2
+    kept = lax.dynamic_index_in_dim(parts, low_bit, axis=2, keepdims=False)
+    sent = lax.dynamic_index_in_dim(parts, 1 - low_bit, axis=2, keepdims=False)
+    got = lax.ppermute(sent.astype(jnp.bfloat16), axis, [(i, i ^ 1) for i in range(4)])
+    kept = kept + got.astype(jnp.float32)
+    final = lax.dynamic_index_in_dim(kept, high_bit, axis=1, keepdims=False)
+    sent = lax.dynamic_index_in_dim(kept, 1 - high_bit, axis=1, keepdims=False)
+    got = lax.ppermute(sent.astype(jnp.bfloat16), axis, [(i, i ^ 2) for i in range(4)])
+    return (final + got.astype(jnp.float32)).astype(jnp.bfloat16)
 
 
 def rotate_table(positions, head_width):
@@ -108,7 +133,7 @@
     positions = first_row + jnp.arange(tok_rows, dtype=jnp.int32)
     key_pos = first_row - pred_count * tok_rows + jnp.arange(key_span, dtype=jnp.int32)
     kept_weight = token_weight * loss_mask.astype(jnp.float32)
-    normalizer = lax.psum(jnp.sum(kept_weight), "seq")
+    normalizer = butterfly_sum(jnp.sum(kept_weight), "seq")
     factor = kept_weight * (tok_rows * lax.axis_size("seq") / normalizer)
     cotangent = (
         (grad_attn.astype(jnp.float32) * factor[:, None])
@@ -173,9 +198,7 @@
         contract,
         preferred_element_type=jnp.float32,
     )
-    grad_tokens = lax.psum_scatter(
-        partial_grad.astype(jnp.bfloat16), "head", scatter_dimension=1, tiled=True
-    )
+    grad_tokens = head_scatter_sum(partial_grad, "head")
     return (attended, grad_tokens)
 
 

time: 370 us -> 362 us (0.978)
  blocking collectives: 163 us -> 0 us
  waiting for transfers between devices: 87.4 us -> 216 us
  starting transfers between devices: 45.2 us -> 58.4 us
  local copies, waits for them, and re-layouts: 24.2 us -> 31.2 us
  other arithmetic: 12.1 us -> 16.9 us
    psum x1 -> x0, blocking collectives: 163 us -> none  [body(): normalizer = lax.psum(jnp.sum(kept_weight), 'seq')]
    all_gather x1, waiting for transfers between devices: 0.01 us -> 130 us  [body(): lax.all_gather(jnp.concatenate([q_weight, k_weight, v_weight], axis=1), '...]
    reduce_scatter x1 -> x0, waiting for transfers between devices: 37.3 us -> none  [body(): lax.psum_scatter(partial_grad.astype(jnp.bfloat16), 'head', scatter_dimen...]
    ppermute x0 -> x8, waiting for transfers between devices: none -> 25.2 us  [the longest x1 15.3 us: head_scatter_sum(): lax.ppermute(sent.astype(jnp.bfloat16), axis, [(i, i ^ 2) for i in range(...]
    ppermute x0 -> x8, starting transfers between devices: none -> 22.2 us  [the longest x6 21.7 us: butterfly_sum(): lax.ppermute(value, axis, [(i, i ^ step) for i in range(size)])]
    ppermute x8, waiting for transfers between devices: 50.1 us -> 60.5 us  [passed_along(): return lax.ppermute(block, axis, route)]
    ppermute x8, starting transfers between devices: 45.1 us -> 36.1 us  [passed_along(): return lax.ppermute(block, axis, route)]
    unnamed x30 -> x34, local copies, waits for them, and re-layouts: 18.9 us -> 23.7 us
  transfers between devices with their start and end apart: 10 -> 17, of which waited for: 7 -> 15; matrix products, arithmetic and copies ran while one was open for 4% -> 4% of each run, Pallas kernels for 0% -> 0%
where the time goes in v2:
time: 362 us; the launch traced here: 361 us
  waiting for transfers between devices  216 us (60%)
  starting transfers between devices  58.4 us (16%)
  local copies, waits for them, and re-layouts  31.2 us (9%)
  matrix products  20.2 us (6%)
  between operations  18.7 us (5%)
  other arithmetic  16.9 us (5%)
    all_gather x1, waiting for transfers between devices, body(): lax.all_gather(jnp.concatenate([q_weight, k_weight, v_weight], axis=1), '...  130 us
    ppermute x8, waiting for transfers between devices, passed_along(): return lax.ppermute(block, axis, route)  60.5 us
    ppermute x8, starting transfers between devices, passed_along(): return lax.ppermute(block, axis, route)  36.1 us
    unnamed x34, local copies, waits for them, and re-layouts  23.7 us
    ppermute x6, starting transfers between devices, butterfly_sum(): lax.ppermute(value, axis, [(i, i ^ step) for i in range(size)])  21.7 us
    ppermute x1, waiting for transfers between devices, head_scatter_sum(): lax.ppermute(sent.astype(jnp.bfloat16), axis, [(i, i ^ 2) for i in range(...  15.3 us
  transfers between devices with their start and end apart: 17, of which 15 were waited for; matrix products, arithmetic and copies ran while one was open for 4% of the time, Pallas kernels for 0%

profile of v2, /device:TPU:38, one launch (start us, length us, event | category | flops | bytes accessed | tf_op | source)
XLA Modules:
  0.0 361.2 jit_solution(5030252477663204898)
XLA Ops:
  15.4 4.7 %collective-permute-start.5 = (f32[]{:T(128)}, f32[]{:T(128)}, u32[]{:S(2)}, u32[]{:S(2)}) collective-permute-start(f32[]{:T(128)} %add.138), channel_id=1, source_target_pairs={{0,8},{4,12},{8,0},{12,4},{16,24},{20,28},{24,16},{28,20},{32,40},... | collective-permute-start | bytes 20 | tf_op jit(solution)/shard_map/ppermute | solution.py:23
  20.9 7.3 %collective-permute-start.6 = (f32[]{:T(128)}, f32[]{:T(128)}, u32[]{:S(2)}, u32[]{:S(2)}) collective-permute-start(f32[]{:T(128)} %add.139), channel_id=1, source_target_pairs={{0,16},{4,20},{8,24},{12,28},{16,0},{20,4},{24,8},{28,12},{32,48},... | collective-permute-start | bytes 20 | tf_op jit(solution)/shard_map/ppermute | solution.py:23
  29.2 4.6 %collective-permute-start.7 = (f32[]{:T(128)}, f32[]{:T(128)}, u32[]{:S(2)}, u32[]{:S(2)}) collective-permute-start(f32[]{:T(128)} %add.140), channel_id=1, source_target_pairs={{0,32},{4,36},{8,40},{12,44},{16,48},{20,52},{24,56},{28,60},{32,0... | collective-permute-start | bytes 20 | tf_op jit(solution)/shard_map/ppermute | solution.py:23
  39.4 2.8 collective-permute-start.9
  47.8 130.3 %all-gather.3.cloned.1.call-done = bf16[64,84,1024]{2,1,0:T(8,128)(2,1)} async-done(((bf16[1,84,1024]{2,1,0:T(8,128)(2,1)}), bf16[64,84,1024]{2,1,0:T(8,128)(2,1)}) %all-gather.3.cloned.1.call-update) | async-done | bytes 11010064 | tf_op jit(solution)/shard_map/all_gather | solution.py:146
  178.1 13.9 %reshape.223 = bf16[5376,1024]{1,0:T(8,128)(2,1)} reshape(bf16[64,84,1024]{2,1,0:T(8,128)(2,1)} %all-gather.3.cloned.1.call-done) | data formatting | bytes 22020096
  192.1 5.9 %convolution_bitcast_fusion.1 = f32[256,1024]{0,1:T(8,128)S(1)} fusion(bf16[5376,1024]{1,0:T(8,128)(2,1)} %reshape.223, bf16[256,5376]{1,0:T(8,128)(2,1)S(1)} %copy-done), kind=kOutput, calls=%fused_computation.20 | convolution fusion | flops 2818572288 | bytes 14811136 | tf_op jit(solution)/shard_map/dot_general | solution.py:149
  199.0 6.2 %collective-permute-start = (bf16[2,256,256]{1,2,0:T(8,128)(2,1)}, bf16[2,256,256]{1,2,0:T(8,128)(2,1)}, u32[]{:S(2)}, u32[]{:S(2)}) collective-permute-start(bf16[2,256,256]{1,2,0:T(8,128)(2,1)} %pad_maximum_fusion.1), channel_id=1, source_target_pairs={{0,16},{4,20},{8,24},{12,28},{16,32},{20,36},{24,40},{28,44},{32,4... | collective-permute-start | bytes 786440 | tf_op jit(solution)/shard_map/ppermute | solution.py:16
  205.2 3.9 %collective-permute-start.1 = (bf16[2,256,256]{1,2,0:T(8,128)(2,1)}, bf16[2,256,256]{1,2,0:T(8,128)(2,1)}, u32[]{:S(2)}, u32[]{:S(2)}) collective-permute-start(bf16[2,256,256]{1,2,0:T(8,128)(2,1)} %pad_maximum_fusion.1), channel_id=1, source_target_pairs={{0,12},{4,16},{8,20},{12,24},{16,28},{20,32},{24,36},{28,40},{32,4... | collective-permute-start | bytes 786440 | tf_op jit(solution)/shard_map/ppermute | solution.py:16
  209.1 3.6 %collective-permute-start.2 = (bf16[2,256,256]{1,2,0:T(8,128)(2,1)}, bf16[2,256,256]{1,2,0:T(8,128)(2,1)}, u32[]{:S(2)}, u32[]{:S(2)}) collective-permute-start(bf16[2,256,256]{1,2,0:T(8,128)(2,1)} %pad_maximum_fusion.1), channel_id=1, source_target_pairs={{0,8},{4,12},{8,16},{12,20},{16,24},{20,28},{24,32},{28,36},{32,40... | collective-permute-start | bytes 786440 | tf_op jit(solution)/shard_map/ppermute | solution.py:16
  212.7 3.9 %collective-permute-start.3 = (bf16[2,256,256]{1,2,0:T(8,128)(2,1)}, bf16[2,256,256]{1,2,0:T(8,128)(2,1)}, u32[]{:S(2)}, u32[]{:S(2)}) collective-permute-start(bf16[2,256,256]{1,2,0:T(8,128)(2,1)} %pad_maximum_fusion.1), channel_id=1, source_target_pairs={{0,4},{4,8},{8,12},{12,16},{16,20},{20,24},{24,28},{28,32},{32,36}... | collective-permute-start | bytes 786440 | tf_op jit(solution)/shard_map/ppermute | solution.py:16
  222.3 17.7 %collective-permute-done.1 = bf16[2,256,256]{1,2,0:T(8,128)(2,1)} collective-permute-done((bf16[2,256,256]{1,2,0:T(8,128)(2,1)}, bf16[2,256,256]{1,2,0:T(8,128)(2,1)}, u32[]{:S(2)}, u32[]{:S(2)}) %collective-permute-start.1) | collective-permute-done | bytes 262176 | tf_op jit(solution)/shard_map/ppermute | solution.py:16
  240.9 7.1 %collective-permute-done.2 = bf16[2,256,256]{1,2,0:T(8,128)(2,1)} collective-permute-done((bf16[2,256,256]{1,2,0:T(8,128)(2,1)}, bf16[2,256,256]{1,2,0:T(8,128)(2,1)}, u32[]{:S(2)}, u32[]{:S(2)}) %collective-permute-start.2) | collective-permute-done | bytes 262176 | tf_op jit(solution)/shard_map/ppermute | solution.py:16
  256.4 2.6 multiply_reduce_fusion.1
  260.9 3.1 fusion.1
  266.1 6.6 %collective-permute-start.10 = (bf16[2,256,256]{1,2,0:T(8,128)(2,1)S(1)}, bf16[2,256,256]{1,2,0:T(8,128)(2,1)S(1)}, u32[]{:S(2)}, u32[]{:S(2)}) collective-permute-start(bf16[2,256,256]{1,2,0:T(8,128)(2,1)S(1)} %get-tuple-element.8), channel_id=1, source_target_pairs={{4,0},{8,4},{12,8},{16,12},{20,16},{24,20},{28,24},{32,28},{36,32}... | collective-permute-start | bytes 786440 | tf_op jit(solution)/shard_map/ppermute | solution.py:16
  272.7 3.1 collective-permute-start.11
  277.8 6.7 %collective-permute-start.13 = (bf16[2,256,256]{1,2,0:T(8,128)(2,1)S(1)}, bf16[2,256,256]{1,2,0:T(8,128)(2,1)S(1)}, u32[]{:S(2)}, u32[]{:S(2)}) collective-permute-start(bf16[2,256,256]{1,2,0:T(8,128)(2,1)S(1)} %get-tuple-element.9), channel_id=1, source_target_pairs={{16,0},{20,4},{24,8},{28,12},{32,16},{36,20},{40,24},{44,28},{48,3... | collective-permute-start | bytes 786440 | tf_op jit(solution)/shard_map/ppermute | solution.py:16
  284.9 8.4 %collective-permute-done.11 = bf16[2,256,256]{1,2,0:T(8,128)(2,1)S(1)} collective-permute-done((bf16[2,256,256]{1,2,0:T(8,128)(2,1)S(1)}, bf16[2,256,256]{1,2,0:T(8,128)(2,1)S(1)}, u32[]{:S(2)}, u32[]{:S(2)}) %collective-permute-start.11) | collective-permute-done | bytes 262176 | tf_op jit(solution)/shard_map/ppermute | solution.py:16
  293.2 19.8 %collective-permute-done.12 = bf16[2,256,256]{1,2,0:T(8,128)(2,1)S(1)} collective-permute-done((bf16[2,256,256]{1,2,0:T(8,128)(2,1)S(1)}, bf16[2,256,256]{1,2,0:T(8,128)(2,1)S(1)}, u32[]{:S(2)}, u32[]{:S(2)}) %collective-permute-start.12) | collective-permute-done | bytes 262176 | tf_op jit(solution)/shard_map/ppermute | solution.py:16
  313.0 5.6 %collective-permute-done.13 = bf16[2,256,256]{1,2,0:T(8,128)(2,1)S(1)} collective-permute-done((bf16[2,256,256]{1,2,0:T(8,128)(2,1)S(1)}, bf16[2,256,256]{1,2,0:T(8,128)(2,1)S(1)}, u32[]{:S(2)}, u32[]{:S(2)}) %collective-permute-start.13) | collective-permute-done | bytes 262176 | tf_op jit(solution)/shard_map/ppermute | solution.py:16
  319.2 3.0 fusion.14
  325.9 3.5 collective-permute-done.14
  336.7 15.3 %collective-permute-done.15 = bf16[256,1344]{0,1:T(8,128)(2,1)S(1)} collective-permute-done((bf16[256,1344]{0,1:T(8,128)(2,1)}, bf16[256,1344]{0,1:T(8,128)(2,1)S(1)}, u32[]{:S(2)}, u32[]{:S(2)}) %collective-permute-start.15) | collective-permute-done | bytes 688160 | tf_op jit(solution)/shard_map/ppermute | solution.py:40
  (101 shorter events, 52.9 us)
Async XLA Ops:
  7.2 184.9 %copy-start = (bf16[256,5376]{1,0:T(8,128)(2,1)S(1)}, bf16[256,5376]{1,0:T(8,128)(2,1)}, u32[]{:S(2)}) copy-start(bf16[256,5376]{1,0:T(8,128)(2,1)} %param.10) | copy-start | bytes 8257540
  7.2 171.0 %all-gather.3.cloned.1.call-start = ((), (), s32[]{:S(2)}) async-start(), calls=%async_computation | async-start | bytes 11714560 | tf_op jit(solution)/shard_map/all_gather | solution.py:146
  10.3 3.8 %collective-permute-start.4 = (f32[]{:T(128)}, f32[]{:T(128)}, u32[]{:S(2)}, u32[]{:S(2)}) collective-permute-start(f32[]{:T(128)} %fusion.25), channel_id=1, source_target_pairs={{0,4},{4,0},{8,12},{12,8},{16,20},{20,16},{24,28},{28,24},{32,36},... | collective-permute-start | bytes 20 | tf_op jit(solution)/shard_map/ppermute | solution.py:23
  15.4 5.0 %collective-permute-start.5 = (f32[]{:T(128)}, f32[]{:T(128)}, u32[]{:S(2)}, u32[]{:S(2)}) collective-permute-start(f32[]{:T(128)} %add.138), channel_id=1, source_target_pairs={{0,8},{4,12},{8,0},{12,4},{16,24},{20,28},{24,16},{28,20},{32,40},... | collective-permute-start | bytes 20 | tf_op jit(solution)/shard_map/ppermute | solution.py:23
  20.9 7.7 %collective-permute-start.6 = (f32[]{:T(128)}, f32[]{:T(128)}, u32[]{:S(2)}, u32[]{:S(2)}) collective-permute-start(f32[]{:T(128)} %add.139), channel_id=1, source_target_pairs={{0,16},{4,20},{8,24},{12,28},{16,0},{20,4},{24,8},{28,12},{32,48},... | collective-permute-start | bytes 20 | tf_op jit(solution)/shard_map/ppermute | solution.py:23
  29.2 5.3 %collective-permute-start.7 = (f32[]{:T(128)}, f32[]{:T(128)}, u32[]{:S(2)}, u32[]{:S(2)}) collective-permute-start(f32[]{:T(128)} %add.140), channel_id=1, source_target_pairs={{0,32},{4,36},{8,40},{12,44},{16,48},{20,52},{24,56},{28,60},{32,0... | collective-permute-start | bytes 20 | tf_op jit(solution)/shard_map/ppermute | solution.py:23
  35.0 3.8 %collective-permute-start.8 = (f32[]{:T(128)}, f32[]{:T(128)}, u32[]{:S(2)}, u32[]{:S(2)}) collective-permute-start(f32[]{:T(128)} %add.141), channel_id=1, source_target_pairs={{0,64},{4,68},{8,72},{12,76},{16,80},{20,84},{24,88},{28,92},{32,9... | collective-permute-start | bytes 20 | tf_op jit(solution)/shard_map/ppermute | solution.py:23
  39.4 5.3 %collective-permute-start.9 = (f32[]{:T(128)}, f32[]{:T(128)}, u32[]{:S(2)}, u32[]{:S(2)}) collective-permute-start(f32[]{:T(128)} %add.142), channel_id=1, source_target_pairs={{0,128},{4,132},{8,136},{12,140},{16,144},{20,148},{24,152},{28,15... | collective-permute-start | bytes 20 | tf_op jit(solution)/shard_map/ppermute | solution.py:23
  199.0 22.1 %collective-permute-start = (bf16[2,256,256]{1,2,0:T(8,128)(2,1)}, bf16[2,256,256]{1,2,0:T(8,128)(2,1)}, u32[]{:S(2)}, u32[]{:S(2)}) collective-permute-start(bf16[2,256,256]{1,2,0:T(8,128)(2,1)} %pad_maximum_fusion.1), channel_id=1, source_target_pairs={{0,16},{4,20},{8,24},{12,28},{16,32},{20,36},{24,40},{28,44},{32,4... | collective-permute-start | bytes 786440 | tf_op jit(solution)/shard_map/ppermute | solution.py:16
  205.2 34.8 %collective-permute-start.1 = (bf16[2,256,256]{1,2,0:T(8,128)(2,1)}, bf16[2,256,256]{1,2,0:T(8,128)(2,1)}, u32[]{:S(2)}, u32[]{:S(2)}) collective-permute-start(bf16[2,256,256]{1,2,0:T(8,128)(2,1)} %pad_maximum_fusion.1), channel_id=1, source_target_pairs={{0,12},{4,16},{8,20},{12,24},{16,28},{20,32},{24,36},{28,40},{32,4... | collective-permute-start | bytes 786440 | tf_op jit(solution)/shard_map/ppermute | solution.py:16
  209.1 39.0 %collective-permute-start.2 = (bf16[2,256,256]{1,2,0:T(8,128)(2,1)}, bf16[2,256,256]{1,2,0:T(8,128)(2,1)}, u32[]{:S(2)}, u32[]{:S(2)}) collective-permute-start(bf16[2,256,256]{1,2,0:T(8,128)(2,1)} %pad_maximum_fusion.1), channel_id=1, source_target_pairs={{0,8},{4,12},{8,16},{12,20},{16,24},{20,28},{24,32},{28,36},{32,40... | collective-permute-start | bytes 786440 | tf_op jit(solution)/shard_map/ppermute | solution.py:16
  212.7 38.1 %collective-permute-start.3 = (bf16[2,256,256]{1,2,0:T(8,128)(2,1)}, bf16[2,256,256]{1,2,0:T(8,128)(2,1)}, u32[]{:S(2)}, u32[]{:S(2)}) collective-permute-start(bf16[2,256,256]{1,2,0:T(8,128)(2,1)} %pad_maximum_fusion.1), channel_id=1, source_target_pairs={{0,4},{4,8},{8,12},{12,16},{16,20},{20,24},{24,28},{28,32},{32,36}... | collective-permute-start | bytes 786440 | tf_op jit(solution)/shard_map/ppermute | solution.py:16
  221.1 30.8 %copy-start.4 = (s32[256,1280]{0,1:T(8,128)S(1)}, s32[256,1280]{0,1:T(8,128)}, u32[]{:S(2)}) copy-start(s32[256,1280]{0,1:T(8,128)} %broadcast_subtract_fusion) | copy-start | bytes 3932164
  221.1 30.8 %copy-start.6 = (bf16[256,4,64]{2,0,1:T(8,128)(2,1)S(1)}, bf16[256,4,64]{2,0,1:T(8,128)(2,1)}, u32[]{:S(2)}) copy-start(bf16[256,4,64]{2,0,1:T(8,128)(2,1)} %copy.39) | copy-start | bytes 393220
  221.1 30.8 %copy-start.7 = (bf16[256,4,64]{2,0,1:T(8,128)(2,1)S(1)}, bf16[256,4,64]{2,0,1:T(8,128)(2,1)}, u32[]{:S(2)}) copy-start(bf16[256,4,64]{2,0,1:T(8,128)(2,1)} %copy.40) | copy-start | bytes 393220
  264.6 54.6 %slice-start = ((s8[11010048]{0:T(1024)(128)(4,1)}), s8[4194304]{0:T(1024)(128)(4,1)S(1)}, s32[]{:S(2)}) async-start(s8[11010048]{0:T(1024)(128)(4,1)} %bitcast.96), calls=%async_computation.1 | async-start | bytes 8388608
  265.7 53.5 %slice-start.1 = ((s8[11010048]{0:T(1024)(128)(4,1)}), s8[4194304]{0:T(1024)(128)(4,1)S(1)}, s32[]{:S(2)}) async-start(s8[11010048]{0:T(1024)(128)(4,1)} %bitcast.96), calls=%async_computation.2 | async-start | bytes 8388608
  266.1 18.8 %collective-permute-start.10 = (bf16[2,256,256]{1,2,0:T(8,128)(2,1)S(1)}, bf16[2,256,256]{1,2,0:T(8,128)(2,1)S(1)}, u32[]{:S(2)}, u32[]{:S(2)}) collective-permute-start(bf16[2,256,256]{1,2,0:T(8,128)(2,1)S(1)} %get-tuple-element.8), channel_id=1, source_target_pairs={{4,0},{8,4},{12,8},{16,12},{20,16},{24,20},{28,24},{32,28},{36,32}... | collective-permute-start | bytes 786440 | tf_op jit(solution)/shard_map/ppermute | solution.py:16
  272.7 20.6 %collective-permute-start.11 = (bf16[2,256,256]{1,2,0:T(8,128)(2,1)S(1)}, bf16[2,256,256]{1,2,0:T(8,128)(2,1)S(1)}, u32[]{:S(2)}, u32[]{:S(2)}) collective-permute-start(bf16[2,256,256]{1,2,0:T(8,128)(2,1)S(1)} %get-tuple-element.11), channel_id=1, source_target_pairs={{8,0},{12,4},{16,8},{20,12},{24,16},{28,20},{32,24},{36,28},{40,32... | collective-permute-start | bytes 786440 | tf_op jit(solution)/shard_map/ppermute | solution.py:16
  275.8 37.2 %collective-permute-start.12 = (bf16[2,256,256]{1,2,0:T(8,128)(2,1)S(1)}, bf16[2,256,256]{1,2,0:T(8,128)(2,1)S(1)}, u32[]{:S(2)}, u32[]{:S(2)}) collective-permute-start(bf16[2,256,256]{1,2,0:T(8,128)(2,1)S(1)} %get-tuple-element.10), channel_id=1, source_target_pairs={{12,0},{16,4},{20,8},{24,12},{28,16},{32,20},{36,24},{40,28},{44,3... | collective-permute-start | bytes 786440 | tf_op jit(solution)/shard_map/ppermute | solution.py:16
  277.8 40.9 %collective-permute-start.13 = (bf16[2,256,256]{1,2,0:T(8,128)(2,1)S(1)}, bf16[2,256,256]{1,2,0:T(8,128)(2,1)S(1)}, u32[]{:S(2)}, u32[]{:S(2)}) collective-permute-start(bf16[2,256,256]{1,2,0:T(8,128)(2,1)S(1)} %get-tuple-element.9), channel_id=1, source_target_pairs={{16,0},{20,4},{24,8},{28,12},{32,16},{36,20},{40,24},{44,28},{48,3... | collective-permute-start | bytes 786440 | tf_op jit(solution)/shard_map/ppermute | solution.py:16
  284.7 34.5 %slice-start.2 = ((s8[11010048]{0:T(1024)(128)(4,1)}), s8[2621440]{0:T(1024)(128)(4,1)S(1)}, s32[]{:S(2)}) async-start(s8[11010048]{0:T(1024)(128)(4,1)} %bitcast.96), calls=%async_computation.3 | async-start | bytes 5242880
  325.9 3.5 collective-permute-start.14
  334.3 17.7 %collective-permute-start.15 = (bf16[256,1344]{0,1:T(8,128)(2,1)}, bf16[256,1344]{0,1:T(8,128)(2,1)S(1)}, u32[]{:S(2)}, u32[]{:S(2)}) collective-permute-start(bf16[256,1344]{0,1:T(8,128)(2,1)} %fusion.7), channel_id=1, source_target_pairs={{0,2},{1,3},{2,0},{3,1},{4,6},{5,7},{6,4},{7,5},{8,10},{9,11},{10,... | collective-permute-start | bytes 2064392 | tf_op jit(solution)/shard_map/ppermute | solution.py:40
  (7 other events, 68.6 us)
Sparse Core Ops, SparseCore 0:
  12.2 165.9 all-gather.2

commit v3 on v2

--- a/solution.py
+++ b/solution.py
@@ -143,10 +143,15 @@
     contract = (((1,), (1,)), ((), ()))
     q_cols = q_weight.shape[1]
     k_cols = k_weight.shape[1]
+    row_block = q_weight.shape[0]
+    seq_count = lax.axis_size("seq")
     joined_rows = lax.all_gather(
-        jnp.concatenate([q_weight, k_weight, v_weight], axis=1), "seq", axis=0, tiled=True
-    )
-    all_linear = jnp.dot(tokens, joined_rows, preferred_element_type=jnp.float32)
+        jnp.concatenate([q_weight, k_weight, v_weight], axis=1), "seq", axis=0, tiled=False
+    )
+    token_blocks = tokens.reshape(tok_rows, seq_count, row_block)
+    all_linear = jnp.einsum(
+        "tsr,src->tc", token_blocks, joined_rows, preferred_element_type=jnp.float32
+    )
     q_linear = all_linear[:, :q_cols]
     k_linear = all_linear[:, q_cols : q_cols + k_cols]
     v_linear = all_linear[:, q_cols + k_cols :]
@@ -192,12 +197,9 @@
     dk_lin = back_key(key_total)[0].astype(jnp.bfloat16).reshape(tok_rows, kv_heads * head_width)
     dv_lin = local_grads[1].astype(jnp.bfloat16)
     joined_grad = jnp.concatenate([dq_lin, dk_lin, dv_lin], axis=1)
-    partial_grad = lax.dot_general(
-        joined_grad,
-        joined_rows,
-        contract,
-        preferred_element_type=jnp.float32,
-    )
+    partial_grad = jnp.einsum(
+        "tc,src->tsr", joined_grad, joined_rows, preferred_element_type=jnp.float32
+    ).reshape(tok_rows, seq_count * row_block)
     grad_tokens = head_scatter_sum(partial_grad, "head")
     return (attended, grad_tokens)
 

time: 362 us -> 369 us (1.019)
  matrix products: 20.2 us -> 30.7 us
  waiting for transfers between devices: 216 us -> 212 us
    unnamed x34 -> x32, local copies, waits for them, and re-layouts: 23.7 us -> 9.41 us
    another operation x2 -> x6, local copies, waits for them, and re-layouts: 3.49 us -> 13.4 us  [the longest x1 6.79 us: head_scatter_sum(): parts = partial.reshape(rows, 2, 2, width // 4)]
    dot_general x2, matrix products: 8.89 us -> 16.9 us  [the longest x1 10 us: body(): jnp.einsum('tc,src->tsr', joined_grad, joined_rows, preferred_element_typ...]
  transfers between devices with their start and end apart: 17 -> 17, of which waited for: 15 -> 14; matrix products, arithmetic and copies ran while one was open for 4% -> 5% of each run, Pallas kernels for 0% -> 0%
where the time goes in v3:
time: 369 us; the launch traced here: 368 us
  waiting for transfers between devices  212 us (57%)
  starting transfers between devices  59.1 us (16%)
  local copies, waits for them, and re-layouts  31.5 us (9%)
  matrix products  30.7 us (8%)
  between operations  19 us (5%)
  other arithmetic  15.6 us (4%)
    all_gather x1, waiting for transfers between devices, body(): lax.all_gather(jnp.concatenate([q_weight, k_weight, v_weight], axis=1), '...  127 us
    ppermute x8, waiting for transfers between devices, passed_along(): return lax.ppermute(block, axis, route)  61.7 us
    ppermute x8, starting transfers between devices, passed_along(): return lax.ppermute(block, axis, route)  35.8 us
    ppermute x6, starting transfers between devices, butterfly_sum(): lax.ppermute(value, axis, [(i, i ^ step) for i in range(size)])  22.6 us
    ppermute x1, waiting for transfers between devices, head_scatter_sum(): lax.ppermute(sent.astype(jnp.bfloat16), axis, [(i, i ^ 2) for i in range(...  15.3 us
    dot_general x1, matrix products, body(): jnp.einsum('tc,src->tsr', joined_grad, joined_rows, preferred_element_typ...  10 us
    unnamed x32, local copies, waits for them, and re-layouts  9.41 us
  transfers between devices with their start and end apart: 17, of which 14 were waited for; matrix products, arithmetic and copies ran while one was open for 5% of the time, Pallas kernels for 0%

profile of v3, /device:TPU:38, one launch (start us, length us, event | category | flops | bytes accessed | tf_op | source)
XLA Modules:
  0.0 368.1 jit_solution(13042091298022686680)
XLA Ops:
  10.3 3.3 copy.51
  19.4 4.7 %collective-permute-start.5 = (f32[]{:T(128)}, f32[]{:T(128)}, u32[]{:S(2)}, u32[]{:S(2)}) collective-permute-start(f32[]{:T(128)} %add.138), channel_id=1, source_target_pairs={{0,8},{4,12},{8,0},{12,4},{16,24},{20,28},{24,16},{28,20},{32,40},... | collective-permute-start | bytes 20 | tf_op jit(solution)/shard_map/ppermute | solution.py:23
  24.8 8.2 %collective-permute-start.6 = (f32[]{:T(128)}, f32[]{:T(128)}, u32[]{:S(2)}, u32[]{:S(2)}) collective-permute-start(f32[]{:T(128)} %add.139), channel_id=1, source_target_pairs={{0,16},{4,20},{8,24},{12,28},{16,0},{20,4},{24,8},{28,12},{32,48},... | collective-permute-start | bytes 20 | tf_op jit(solution)/shard_map/ppermute | solution.py:23
  33.9 4.6 %collective-permute-start.7 = (f32[]{:T(128)}, f32[]{:T(128)}, u32[]{:S(2)}, u32[]{:S(2)}) collective-permute-start(f32[]{:T(128)} %add.140), channel_id=1, source_target_pairs={{0,32},{4,36},{8,40},{12,44},{16,48},{20,52},{24,56},{28,60},{32,0... | collective-permute-start | bytes 20 | tf_op jit(solution)/shard_map/ppermute | solution.py:23
  50.7 127.4 %all-gather.4.cloned.1.call-done = bf16[64,84,1024]{2,1,0:T(8,128)(2,1)} async-done(((bf16[1,84,1024]{2,1,0:T(8,128)(2,1)}), bf16[64,84,1024]{2,1,0:T(8,128)(2,1)}) %all-gather.4.cloned.1.call-update) | async-done | bytes 11010064 | tf_op jit(solution)/shard_map/all_gather | solution.py:148
  178.1 6.9 %convolution_bitcast_fusion.1 = f32[256,1024]{0,1:T(8,128)S(1)} fusion(bf16[64,84,1024]{2,1,0:T(8,128)(2,1)} %all-gather.4.cloned.1.call-done, bf16[256,64,84]{0,2,1:T(8,128)(2,1)} %reshape.215), kind=kOutput, calls=%fused_computation.20 | convolution fusion | flops 2818572288 | bytes 14811136 | tf_op jit(solution)/shard_map/tsr,src->tc/dot_general | solution.py:152
  186.0 6.2 %collective-permute-start = (bf16[2,256,256]{1,2,0:T(8,128)(2,1)}, bf16[2,256,256]{1,2,0:T(8,128)(2,1)}, u32[]{:S(2)}, u32[]{:S(2)}) collective-permute-start(bf16[2,256,256]{1,2,0:T(8,128)(2,1)} %pad_maximum_fusion.1), channel_id=1, source_target_pairs={{0,16},{4,20},{8,24},{12,28},{16,32},{20,36},{24,40},{28,44},{32,4... | collective-permute-start | bytes 786440 | tf_op jit(solution)/shard_map/ppermute | solution.py:16
  192.2 3.9 %collective-permute-start.1 = (bf16[2,256,256]{1,2,0:T(8,128)(2,1)}, bf16[2,256,256]{1,2,0:T(8,128)(2,1)}, u32[]{:S(2)}, u32[]{:S(2)}) collective-permute-start(bf16[2,256,256]{1,2,0:T(8,128)(2,1)} %pad_maximum_fusion.1), channel_id=1, source_target_pairs={{0,12},{4,16},{8,20},{12,24},{16,28},{20,32},{24,36},{28,40},{32,4... | collective-permute-start | bytes 786440 | tf_op jit(solution)/shard_map/ppermute | solution.py:16
  196.1 3.6 collective-permute-start.2
  199.7 3.9 %collective-permute-start.3 = (bf16[2,256,256]{1,2,0:T(8,128)(2,1)}, bf16[2,256,256]{1,2,0:T(8,128)(2,1)}, u32[]{:S(2)}, u32[]{:S(2)}) collective-permute-start(bf16[2,256,256]{1,2,0:T(8,128)(2,1)} %pad_maximum_fusion.1), channel_id=1, source_target_pairs={{0,4},{4,8},{8,12},{12,16},{16,20},{20,24},{24,28},{28,32},{32,36}... | collective-permute-start | bytes 786440 | tf_op jit(solution)/shard_map/ppermute | solution.py:16
  207.5 19.4 %collective-permute-done.1 = bf16[2,256,256]{1,2,0:T(8,128)(2,1)} collective-permute-done((bf16[2,256,256]{1,2,0:T(8,128)(2,1)}, bf16[2,256,256]{1,2,0:T(8,128)(2,1)}, u32[]{:S(2)}, u32[]{:S(2)}) %collective-permute-start.1) | collective-permute-done | bytes 262176 | tf_op jit(solution)/shard_map/ppermute | solution.py:16
  227.9 7.1 %collective-permute-done.2 = bf16[2,256,256]{1,2,0:T(8,128)(2,1)} collective-permute-done((bf16[2,256,256]{1,2,0:T(8,128)(2,1)}, bf16[2,256,256]{1,2,0:T(8,128)(2,1)}, u32[]{:S(2)}, u32[]{:S(2)}) %collective-permute-start.2) | collective-permute-done | bytes 262176 | tf_op jit(solution)/shard_map/ppermute | solution.py:16
  245.9 3.4 fusion.29
  249.3 3.1 fusion.1
  262.1 6.4 %collective-permute-start.10 = (bf16[2,256,256]{2,1,0:T(8,128)(2,1)}, bf16[2,256,256]{2,1,0:T(8,128)(2,1)S(1)}, u32[]{:S(2)}, u32[]{:S(2)}) collective-permute-start(bf16[2,256,256]{2,1,0:T(8,128)(2,1)} %get-tuple-element.8), channel_id=1, source_target_pairs={{4,0},{8,4},{12,8},{16,12},{20,16},{24,20},{28,24},{32,28},{36,32}... | collective-permute-start | bytes 786440 | tf_op jit(solution)/shard_map/ppermute | solution.py:16
  268.5 3.1 collective-permute-start.11
  273.6 6.7 %collective-permute-start.13 = (bf16[2,256,256]{2,1,0:T(8,128)(2,1)}, bf16[2,256,256]{2,1,0:T(8,128)(2,1)}, u32[]{:S(2)}, u32[]{:S(2)}) collective-permute-start(bf16[2,256,256]{2,1,0:T(8,128)(2,1)} %get-tuple-element.9), channel_id=1, source_target_pairs={{16,0},{20,4},{24,8},{28,12},{32,16},{36,20},{40,24},{44,28},{48,3... | collective-permute-start | bytes 786440 | tf_op jit(solution)/shard_map/ppermute | solution.py:16
  281.5 7.9 %collective-permute-done.11 = bf16[2,256,256]{2,1,0:T(8,128)(2,1)} collective-permute-done((bf16[2,256,256]{2,1,0:T(8,128)(2,1)}, bf16[2,256,256]{2,1,0:T(8,128)(2,1)}, u32[]{:S(2)}, u32[]{:S(2)}) %collective-permute-start.11) | collective-permute-done | bytes 262176 | tf_op jit(solution)/shard_map/ppermute | solution.py:16
  289.4 19.8 %collective-permute-done.12 = bf16[2,256,256]{2,1,0:T(8,128)(2,1)} collective-permute-done((bf16[2,256,256]{2,1,0:T(8,128)(2,1)}, bf16[2,256,256]{2,1,0:T(8,128)(2,1)}, u32[]{:S(2)}, u32[]{:S(2)}) %collective-permute-start.12) | collective-permute-done | bytes 262176 | tf_op jit(solution)/shard_map/ppermute | solution.py:16
  309.2 5.6 %collective-permute-done.13 = bf16[2,256,256]{2,1,0:T(8,128)(2,1)} collective-permute-done((bf16[2,256,256]{2,1,0:T(8,128)(2,1)}, bf16[2,256,256]{2,1,0:T(8,128)(2,1)}, u32[]{:S(2)}, u32[]{:S(2)}) %collective-permute-start.13) | collective-permute-done | bytes 262176 | tf_op jit(solution)/shard_map/ppermute | solution.py:16
  317.1 10.0 %fusion.14 = f32[256,64,84]{0,2,1:T(8,128)} fusion(bf16[64,84,1024]{2,1,0:T(8,128)(2,1)} %all-gather.4.cloned.1.call-done, bf16[256,256]{1,0:T(8,128)(2,1)S(1)} %fusion.21, bf16[256,256]{1,0:T(8,128)(2,1)S(1)} %copy.87, bf16[256,512]{1,0:T(8,128)(2,1)S(1)} %copy-done.3), kind=kOutput, calls=%fused_computation.34 | convolution fusion | flops 2820145152 | bytes 17039360 | tf_op jit(solution)/shard_map/tc,src->tsr/dot_general | solution.py:200
  327.1 6.8 %reshape_reshape.7 = f32[256,2,2,1344]{0,3,2,1:T(8,128)} reshape(f32[256,64,84]{0,2,1:T(8,128)} %fusion.14) | data formatting | bytes 11010048 | tf_op jit(solution)/shard_map/reshape;reshape | solution.py:31
  336.0 3.2 collective-permute-done.14
  345.0 15.3 %collective-permute-done.15 = bf16[256,1344]{0,1:T(8,128)(2,1)S(1)} collective-permute-done((bf16[256,1344]{0,1:T(8,128)(2,1)}, bf16[256,1344]{0,1:T(8,128)(2,1)S(1)}, u32[]{:S(2)}, u32[]{:S(2)}) %collective-permute-start.15) | collective-permute-done | bytes 688160 | tf_op jit(solution)/shard_map/ppermute | solution.py:40
  (105 shorter events, 58.5 us)
Async XLA Ops:
  7.2 170.9 %all-gather.4.cloned.1.call-start = ((), (), s32[]{:S(2)}) async-start(), calls=%async_computation | async-start | bytes 11714560 | tf_op jit(solution)/shard_map/all_gather | solution.py:148
  10.2 7.9 %collective-permute-start.4 = (f32[]{:T(128)}, f32[]{:T(128)}, u32[]{:S(2)}, u32[]{:S(2)}) collective-permute-start(f32[]{:T(128)} %fusion.24), channel_id=1, source_target_pairs={{0,4},{4,0},{8,12},{12,8},{16,20},{20,16},{24,28},{28,24},{32,36},... | collective-permute-start | bytes 20 | tf_op jit(solution)/shard_map/ppermute | solution.py:23
  13.6 36.1 %copy-start.9 = (f32[256]{0:T(256)S(1)}, f32[256]{0:T(256)}, u32[]{:S(2)}) copy-start(f32[256]{0:T(256)} %param.17) | copy-start | bytes 3076
  13.6 36.1 %copy-start.10 = (s32[256]{0:T(256)S(1)}, s32[256]{0:T(256)}, u32[]{:S(2)}) copy-start(s32[256]{0:T(256)} %param.18) | copy-start | bytes 3076
  13.6 36.1 %copy-start.1 = (bf16[256,512]{1,0:T(8,128)(2,1)S(1)}, bf16[256,512]{1,0:T(8,128)(2,1)}, u32[]{:S(2)}) copy-start(bf16[256,512]{1,0:T(8,128)(2,1)} %param.19) | copy-start | bytes 786436
  19.4 4.9 %collective-permute-start.5 = (f32[]{:T(128)}, f32[]{:T(128)}, u32[]{:S(2)}, u32[]{:S(2)}) collective-permute-start(f32[]{:T(128)} %add.138), channel_id=1, source_target_pairs={{0,8},{4,12},{8,0},{12,4},{16,24},{20,28},{24,16},{28,20},{32,40},... | collective-permute-start | bytes 20 | tf_op jit(solution)/shard_map/ppermute | solution.py:23
  24.8 8.4 %collective-permute-start.6 = (f32[]{:T(128)}, f32[]{:T(128)}, u32[]{:S(2)}, u32[]{:S(2)}) collective-permute-start(f32[]{:T(128)} %add.139), channel_id=1, source_target_pairs={{0,16},{4,20},{8,24},{12,28},{16,0},{20,4},{24,8},{28,12},{32,48},... | collective-permute-start | bytes 20 | tf_op jit(solution)/shard_map/ppermute | solution.py:23
  33.9 5.1 %collective-permute-start.7 = (f32[]{:T(128)}, f32[]{:T(128)}, u32[]{:S(2)}, u32[]{:S(2)}) collective-permute-start(f32[]{:T(128)} %add.140), channel_id=1, source_target_pairs={{0,32},{4,36},{8,40},{12,44},{16,48},{20,52},{24,56},{28,60},{32,0... | collective-permute-start | bytes 20 | tf_op jit(solution)/shard_map/ppermute | solution.py:23
  39.6 3.6 collective-permute-start.8
  43.9 5.1 %collective-permute-start.9 = (f32[]{:T(128)}, f32[]{:T(128)}, u32[]{:S(2)}, u32[]{:S(2)}) collective-permute-start(f32[]{:T(128)} %add.142), channel_id=1, source_target_pairs={{0,128},{4,132},{8,136},{12,140},{16,144},{20,148},{24,152},{28,15... | collective-permute-start | bytes 20 | tf_op jit(solution)/shard_map/ppermute | solution.py:23
  50.6 134.4 %copy-start.7 = (f32[128]{0:T(128)S(1)}, f32[128]{0:T(128)}, u32[]{:S(2)}) copy-start(f32[128]{0:T(128)} %param.15) | copy-start | bytes 1540
  186.0 20.5 %collective-permute-start = (bf16[2,256,256]{1,2,0:T(8,128)(2,1)}, bf16[2,256,256]{1,2,0:T(8,128)(2,1)}, u32[]{:S(2)}, u32[]{:S(2)}) collective-permute-start(bf16[2,256,256]{1,2,0:T(8,128)(2,1)} %pad_maximum_fusion.1), channel_id=1, source_target_pairs={{0,16},{4,20},{8,24},{12,28},{16,32},{20,36},{24,40},{28,44},{32,4... | collective-permute-start | bytes 786440 | tf_op jit(solution)/shard_map/ppermute | solution.py:16
  192.2 34.8 %collective-permute-start.1 = (bf16[2,256,256]{1,2,0:T(8,128)(2,1)}, bf16[2,256,256]{1,2,0:T(8,128)(2,1)}, u32[]{:S(2)}, u32[]{:S(2)}) collective-permute-start(bf16[2,256,256]{1,2,0:T(8,128)(2,1)} %pad_maximum_fusion.1), channel_id=1, source_target_pairs={{0,12},{4,16},{8,20},{12,24},{16,28},{20,32},{24,36},{28,40},{32,4... | collective-permute-start | bytes 786440 | tf_op jit(solution)/shard_map/ppermute | solution.py:16
  196.1 39.0 %collective-permute-start.2 = (bf16[2,256,256]{1,2,0:T(8,128)(2,1)}, bf16[2,256,256]{1,2,0:T(8,128)(2,1)}, u32[]{:S(2)}, u32[]{:S(2)}) collective-permute-start(bf16[2,256,256]{1,2,0:T(8,128)(2,1)} %pad_maximum_fusion.1), channel_id=1, source_target_pairs={{0,8},{4,12},{8,16},{12,20},{16,24},{20,28},{24,32},{28,36},{32,40... | collective-permute-start | bytes 786440 | tf_op jit(solution)/shard_map/ppermute | solution.py:16
  199.7 38.1 %collective-permute-start.3 = (bf16[2,256,256]{1,2,0:T(8,128)(2,1)}, bf16[2,256,256]{1,2,0:T(8,128)(2,1)}, u32[]{:S(2)}, u32[]{:S(2)}) collective-permute-start(bf16[2,256,256]{1,2,0:T(8,128)(2,1)} %pad_maximum_fusion.1), channel_id=1, source_target_pairs={{0,4},{4,8},{8,12},{12,16},{16,20},{20,24},{24,28},{28,32},{32,36}... | collective-permute-start | bytes 786440 | tf_op jit(solution)/shard_map/ppermute | solution.py:16
  206.5 32.4 %copy-start.4 = (pred[1280]{0:T(1024)(128)(4,1)S(1)}, pred[1280]{0:T(1024)(128)(4,1)}, u32[]{:S(2)}) copy-start(pred[1280]{0:T(1024)(128)(4,1)} %broadcast_compare_fusion.1) | copy-start | bytes 3844
  206.5 32.4 %copy-start.11 = (s32[2,2]{1,0:T(2,128)S(1)}, s32[2,2]{1,0:T(2,128)}, u32[]{:S(2)}) copy-start(s32[2,2]{1,0:T(2,128)} %lt.36) | copy-start | bytes 52
  262.1 19.4 %collective-permute-start.10 = (bf16[2,256,256]{2,1,0:T(8,128)(2,1)}, bf16[2,256,256]{2,1,0:T(8,128)(2,1)S(1)}, u32[]{:S(2)}, u32[]{:S(2)}) collective-permute-start(bf16[2,256,256]{2,1,0:T(8,128)(2,1)} %get-tuple-element.8), channel_id=1, source_target_pairs={{4,0},{8,4},{12,8},{16,12},{20,16},{24,20},{28,24},{32,28},{36,32}... | collective-permute-start | bytes 786440 | tf_op jit(solution)/shard_map/ppermute | solution.py:16
  268.5 20.9 %collective-permute-start.11 = (bf16[2,256,256]{2,1,0:T(8,128)(2,1)}, bf16[2,256,256]{2,1,0:T(8,128)(2,1)}, u32[]{:S(2)}, u32[]{:S(2)}) collective-permute-start(bf16[2,256,256]{2,1,0:T(8,128)(2,1)} %get-tuple-element.11), channel_id=1, source_target_pairs={{8,0},{12,4},{16,8},{20,12},{24,16},{28,20},{32,24},{36,28},{40,32... | collective-permute-start | bytes 786440 | tf_op jit(solution)/shard_map/ppermute | solution.py:16
  271.6 37.6 %collective-permute-start.12 = (bf16[2,256,256]{2,1,0:T(8,128)(2,1)}, bf16[2,256,256]{2,1,0:T(8,128)(2,1)}, u32[]{:S(2)}, u32[]{:S(2)}) collective-permute-start(bf16[2,256,256]{2,1,0:T(8,128)(2,1)} %get-tuple-element.10), channel_id=1, source_target_pairs={{12,0},{16,4},{20,8},{24,12},{28,16},{32,20},{36,24},{40,28},{44,3... | collective-permute-start | bytes 786440 | tf_op jit(solution)/shard_map/ppermute | solution.py:16
  273.6 41.2 %collective-permute-start.13 = (bf16[2,256,256]{2,1,0:T(8,128)(2,1)}, bf16[2,256,256]{2,1,0:T(8,128)(2,1)}, u32[]{:S(2)}, u32[]{:S(2)}) collective-permute-start(bf16[2,256,256]{2,1,0:T(8,128)(2,1)} %get-tuple-element.9), channel_id=1, source_target_pairs={{16,0},{20,4},{24,8},{28,12},{32,16},{36,20},{40,24},{44,28},{48,3... | collective-permute-start | bytes 786440 | tf_op jit(solution)/shard_map/ppermute | solution.py:16
  281.5 34.9 %copy-start.8 = (f32[128]{0:T(128)S(1)}, f32[128]{0:T(128)}, u32[]{:S(2)}) copy-start(f32[128]{0:T(128)} %param.15) | copy-start | bytes 1540
  335.8 3.3 collective-permute-start.14
  342.6 17.7 %collective-permute-start.15 = (bf16[256,1344]{0,1:T(8,128)(2,1)}, bf16[256,1344]{0,1:T(8,128)(2,1)S(1)}, u32[]{:S(2)}, u32[]{:S(2)}) collective-permute-start(bf16[256,1344]{0,1:T(8,128)(2,1)} %fusion.7), channel_id=1, source_target_pairs={{0,2},{1,3},{2,0},{3,1},{4,6},{5,7},{6,4},{7,5},{8,10},{9,11},{10,... | collective-permute-start | bytes 2064392 | tf_op jit(solution)/shard_map/ppermute | solution.py:40
  (6 other events, 77.5 us)
Sparse Core Ops, SparseCore 0:
  12.2 165.8 all-gather.3

commit v4 on v3

--- a/solution.py
+++ b/solution.py
@@ -197,9 +197,12 @@
     dk_lin = back_key(key_total)[0].astype(jnp.bfloat16).reshape(tok_rows, kv_heads * head_width)
     dv_lin = local_grads[1].astype(jnp.bfloat16)
     joined_grad = jnp.concatenate([dq_lin, dk_lin, dv_lin], axis=1)
-    partial_grad = jnp.einsum(
-        "tc,src->tsr", joined_grad, joined_rows, preferred_element_type=jnp.float32
-    ).reshape(tok_rows, seq_count * row_block)
+    partial_grad = lax.dot_general(
+        joined_grad,
+        joined_rows.reshape(seq_count * row_block, joined_rows.shape[-1]),
+        contract,
+        preferred_element_type=jnp.float32,
+    )
     grad_tokens = head_scatter_sum(partial_grad, "head")
     return (attended, grad_tokens)
 

time: 369 us -> 359 us (0.973)
  waiting for transfers between devices: 212 us -> 198 us
  local copies, waits for them, and re-layouts: 31.5 us -> 39.3 us
  matrix products: 30.7 us -> 26.6 us
    ppermute x8, waiting for transfers between devices: 61.7 us -> 47.7 us  [passed_along(): return lax.ppermute(block, axis, route)]
    dot_general x0 -> x1, local copies, waits for them, and re-layouts: none -> 13.9 us  [body(): lax.dot_general(joined_grad, joined_rows.reshape(seq_count * row_block, j...]
    another operation x3 -> x2, local copies, waits for them, and re-layouts: 8.72 us -> 1.94 us  [the longest x1 6.79 us: head_scatter_sum(): parts = partial.reshape(rows, 2, 2, width // 4)]
    dot_general x1, matrix products: 10 us -> 5.95 us  [body(): lax.dot_general(joined_grad, joined_rows.reshape(seq_count * row_block, j...]
    unnamed x32 -> x34, local copies, waits for them, and re-layouts: 9.41 us -> 11.8 us
  transfers between devices with their start and end apart: 17 -> 17, of which waited for: 14 -> 14; matrix products, arithmetic and copies ran while one was open for 5% -> 9% of each run, Pallas kernels for 0% -> 0%
where the time goes in v4:
time: 359 us; the launch traced here: 358 us
  waiting for transfers between devices  198 us (55%)
  starting transfers between devices  59.1 us (16%)
  local copies, waits for them, and re-layouts  39.3 us (11%)
  matrix products  26.6 us (7%)
  between operations  19.4 us (5%)
  other arithmetic  15.5 us (4%)
    all_gather x1, waiting for transfers between devices, body(): lax.all_gather(jnp.concatenate([q_weight, k_weight, v_weight], axis=1), '...  127 us
    ppermute x8, waiting for transfers between devices, passed_along(): return lax.ppermute(block, axis, route)  47.7 us
    ppermute x8, starting transfers between devices, passed_along(): return lax.ppermute(block, axis, route)  35.8 us
    ppermute x6, starting transfers between devices, butterfly_sum(): lax.ppermute(value, axis, [(i, i ^ step) for i in range(size)])  22.6 us
    ppermute x1, waiting for transfers between devices, head_scatter_sum(): lax.ppermute(sent.astype(jnp.bfloat16), axis, [(i, i ^ 2) for i in range(...  15.3 us
    dot_general x1, local copies, waits for them, and re-layouts, body(): lax.dot_general(joined_grad, joined_rows.reshape(seq_count * row_block, j...  13.9 us
    unnamed x34, local copies, waits for them, and re-layouts  11.8 us
  transfers between devices with their start and end apart: 17, of which 14 were waited for; matrix products, arithmetic and copies ran while one was open for 9% of the time, Pallas kernels for 0%

profile of v4, /device:TPU:38, one launch (start us, length us, event | category | flops | bytes accessed | tf_op | source)
XLA Modules:
  0.0 357.8 jit_solution(7203653957515040718)
XLA Ops:
  10.3 3.3 copy.50
  19.4 4.7 %collective-permute-start.5 = (f32[]{:T(128)}, f32[]{:T(128)}, u32[]{:S(2)}, u32[]{:S(2)}) collective-permute-start(f32[]{:T(128)} %add.138), channel_id=1, source_target_pairs={{0,8},{4,12},{8,0},{12,4},{16,24},{20,28},{24,16},{28,20},{32,40},... | collective-permute-start | bytes 20 | tf_op jit(solution)/shard_map/ppermute | solution.py:23
  24.9 8.2 %collective-permute-start.6 = (f32[]{:T(128)}, f32[]{:T(128)}, u32[]{:S(2)}, u32[]{:S(2)}) collective-permute-start(f32[]{:T(128)} %add.139), channel_id=1, source_target_pairs={{0,16},{4,20},{8,24},{12,28},{16,0},{20,4},{24,8},{28,12},{32,48},... | collective-permute-start | bytes 20 | tf_op jit(solution)/shard_map/ppermute | solution.py:23
  34.0 4.6 %collective-permute-start.7 = (f32[]{:T(128)}, f32[]{:T(128)}, u32[]{:S(2)}, u32[]{:S(2)}) collective-permute-start(f32[]{:T(128)} %add.140), channel_id=1, source_target_pairs={{0,32},{4,36},{8,40},{12,44},{16,48},{20,52},{24,56},{28,60},{32,0... | collective-permute-start | bytes 20 | tf_op jit(solution)/shard_map/ppermute | solution.py:23
  51.0 127.0 %all-gather.4.cloned.1.call-done = bf16[64,84,1024]{2,1,0:T(8,128)(2,1)} async-done(((bf16[1,84,1024]{2,1,0:T(8,128)(2,1)}), bf16[64,84,1024]{2,1,0:T(8,128)(2,1)}) %all-gather.4.cloned.1.call-update) | async-done | bytes 11010064 | tf_op jit(solution)/shard_map/all_gather | solution.py:148
  178.0 6.9 %convolution_bitcast_fusion.1 = f32[256,1024]{0,1:T(8,128)S(1)} fusion(bf16[64,84,1024]{2,1,0:T(8,128)(2,1)} %all-gather.4.cloned.1.call-done, bf16[256,64,84]{0,2,1:T(8,128)(2,1)} %reshape.219), kind=kOutput, calls=%fused_computation.20 | convolution fusion | flops 2818572288 | bytes 14811136 | tf_op jit(solution)/shard_map/tsr,src->tc/dot_general | solution.py:152
  185.9 6.2 %collective-permute-start = (bf16[2,256,256]{1,2,0:T(8,128)(2,1)}, bf16[2,256,256]{1,2,0:T(8,128)(2,1)}, u32[]{:S(2)}, u32[]{:S(2)}) collective-permute-start(bf16[2,256,256]{1,2,0:T(8,128)(2,1)} %pad_maximum_fusion.1), channel_id=1, source_target_pairs={{0,16},{4,20},{8,24},{12,28},{16,32},{20,36},{24,40},{28,44},{32,4... | collective-permute-start | bytes 786440 | tf_op jit(solution)/shard_map/ppermute | solution.py:16
  192.1 3.9 %collective-permute-start.1 = (bf16[2,256,256]{1,2,0:T(8,128)(2,1)}, bf16[2,256,256]{1,2,0:T(8,128)(2,1)}, u32[]{:S(2)}, u32[]{:S(2)}) collective-permute-start(bf16[2,256,256]{1,2,0:T(8,128)(2,1)} %pad_maximum_fusion.1), channel_id=1, source_target_pairs={{0,12},{4,16},{8,20},{12,24},{16,28},{20,32},{24,36},{28,40},{32,4... | collective-permute-start | bytes 786440 | tf_op jit(solution)/shard_map/ppermute | solution.py:16
  196.0 3.6 %collective-permute-start.2 = (bf16[2,256,256]{1,2,0:T(8,128)(2,1)}, bf16[2,256,256]{1,2,0:T(8,128)(2,1)}, u32[]{:S(2)}, u32[]{:S(2)}) collective-permute-start(bf16[2,256,256]{1,2,0:T(8,128)(2,1)} %pad_maximum_fusion.1), channel_id=1, source_target_pairs={{0,8},{4,12},{8,16},{12,20},{16,24},{20,28},{24,32},{28,36},{32,40... | collective-permute-start | bytes 786440 | tf_op jit(solution)/shard_map/ppermute | solution.py:16
  199.6 3.9 %collective-permute-start.3 = (bf16[2,256,256]{1,2,0:T(8,128)(2,1)}, bf16[2,256,256]{1,2,0:T(8,128)(2,1)}, u32[]{:S(2)}, u32[]{:S(2)}) collective-permute-start(bf16[2,256,256]{1,2,0:T(8,128)(2,1)} %pad_maximum_fusion.1), channel_id=1, source_target_pairs={{0,4},{4,8},{8,12},{12,16},{16,20},{20,24},{24,28},{28,32},{32,36}... | collective-permute-start | bytes 786440 | tf_op jit(solution)/shard_map/ppermute | solution.py:16
  206.4 13.9 %dot_general.36 = bf16[2,2,1344,1024]{3,2,1,0:T(8,128)(2,1)} reshape(bf16[64,84,1024]{2,1,0:T(8,128)(2,1)} %all-gather.4.cloned.1.call-done) | data formatting | bytes 22020096 | tf_op jit(solution)/shard_map/dot_general | solution.py:200
  221.4 5.5 %collective-permute-done.1 = bf16[2,256,256]{1,2,0:T(8,128)(2,1)} collective-permute-done((bf16[2,256,256]{1,2,0:T(8,128)(2,1)}, bf16[2,256,256]{1,2,0:T(8,128)(2,1)}, u32[]{:S(2)}, u32[]{:S(2)}) %collective-permute-start.1) | collective-permute-done | bytes 262176 | tf_op jit(solution)/shard_map/ppermute | solution.py:16
  227.9 7.1 %collective-permute-done.2 = bf16[2,256,256]{1,2,0:T(8,128)(2,1)} collective-permute-done((bf16[2,256,256]{1,2,0:T(8,128)(2,1)}, bf16[2,256,256]{1,2,0:T(8,128)(2,1)}, u32[]{:S(2)}, u32[]{:S(2)}) %collective-permute-start.2) | collective-permute-done | bytes 262176 | tf_op jit(solution)/shard_map/ppermute | solution.py:16
  245.8 3.4 fusion.29
  249.2 3.1 fusion.1
  262.1 6.3 %collective-permute-start.10 = (bf16[2,256,256]{2,1,0:T(8,128)(2,1)}, bf16[2,256,256]{2,1,0:T(8,128)(2,1)S(1)}, u32[]{:S(2)}, u32[]{:S(2)}) collective-permute-start(bf16[2,256,256]{2,1,0:T(8,128)(2,1)} %get-tuple-element.8), channel_id=1, source_target_pairs={{4,0},{8,4},{12,8},{16,12},{20,16},{24,20},{28,24},{32,28},{36,32}... | collective-permute-start | bytes 786440 | tf_op jit(solution)/shard_map/ppermute | solution.py:16
  268.4 3.1 collective-permute-start.11
  273.6 6.7 %collective-permute-start.13 = (bf16[2,256,256]{2,1,0:T(8,128)(2,1)}, bf16[2,256,256]{2,1,0:T(8,128)(2,1)}, u32[]{:S(2)}, u32[]{:S(2)}) collective-permute-start(bf16[2,256,256]{2,1,0:T(8,128)(2,1)} %get-tuple-element.9), channel_id=1, source_target_pairs={{16,0},{20,4},{24,8},{28,12},{32,16},{36,20},{40,24},{44,28},{48,3... | collective-permute-start | bytes 786440 | tf_op jit(solution)/shard_map/ppermute | solution.py:16
  281.5 7.8 %collective-permute-done.11 = bf16[2,256,256]{2,1,0:T(8,128)(2,1)} collective-permute-done((bf16[2,256,256]{2,1,0:T(8,128)(2,1)}, bf16[2,256,256]{2,1,0:T(8,128)(2,1)}, u32[]{:S(2)}, u32[]{:S(2)}) %collective-permute-start.11) | collective-permute-done | bytes 262176 | tf_op jit(solution)/shard_map/ppermute | solution.py:16
  289.3 19.8 %collective-permute-done.12 = bf16[2,256,256]{2,1,0:T(8,128)(2,1)} collective-permute-done((bf16[2,256,256]{2,1,0:T(8,128)(2,1)}, bf16[2,256,256]{2,1,0:T(8,128)(2,1)}, u32[]{:S(2)}, u32[]{:S(2)}) %collective-permute-start.12) | collective-permute-done | bytes 262176 | tf_op jit(solution)/shard_map/ppermute | solution.py:16
  309.1 5.6 %collective-permute-done.13 = bf16[2,256,256]{2,1,0:T(8,128)(2,1)} collective-permute-done((bf16[2,256,256]{2,1,0:T(8,128)(2,1)}, bf16[2,256,256]{2,1,0:T(8,128)(2,1)}, u32[]{:S(2)}, u32[]{:S(2)}) %collective-permute-start.13) | collective-permute-done | bytes 262176 | tf_op jit(solution)/shard_map/ppermute | solution.py:16
  317.0 5.9 %fusion.14 = f32[256,2,2,1344]{0,3,2,1:T(8,128)S(1)} fusion(bf16[2,2,1344,1024]{3,2,1,0:T(8,128)(2,1)} %dot_general.36, bf16[256,256]{1,0:T(8,128)(2,1)S(1)} %fusion.21, bf16[256,256]{1,0:T(8,128)(2,1)S(1)} %copy.87, bf16[256,512]{1,0:T(8,128)(2,1)S(1)} %copy-done.4), kind=kOutput, calls=%fused_computation.34 | convolution fusion | flops 2820145152 | bytes 17039360 | tf_op jit(solution)/shard_map/dot_general | solution.py:200
  325.7 3.2 collective-permute-done.14
  334.7 15.3 %collective-permute-done.15 = bf16[256,1344]{0,1:T(8,128)(2,1)S(1)} collective-permute-done((bf16[256,1344]{0,1:T(8,128)(2,1)}, bf16[256,1344]{0,1:T(8,128)(2,1)S(1)}, u32[]{:S(2)}, u32[]{:S(2)}) %collective-permute-start.15) | collective-permute-done | bytes 688160 | tf_op jit(solution)/shard_map/ppermute | solution.py:40
  (107 shorter events, 59.2 us)
Async XLA Ops:
  7.2 170.8 %all-gather.4.cloned.1.call-start = ((), (), s32[]{:S(2)}) async-start(), calls=%async_computation | async-start | bytes 11714560 | tf_op jit(solution)/shard_map/all_gather | solution.py:148
  10.2 7.8 %collective-permute-start.4 = (f32[]{:T(128)}, f32[]{:T(128)}, u32[]{:S(2)}, u32[]{:S(2)}) collective-permute-start(f32[]{:T(128)} %fusion.24), channel_id=1, source_target_pairs={{0,4},{4,0},{8,12},{12,8},{16,20},{20,16},{24,28},{28,24},{32,36},... | collective-permute-start | bytes 20 | tf_op jit(solution)/shard_map/ppermute | solution.py:23
  13.6 36.4 %copy-start.10 = (f32[256]{0:T(256)S(1)}, f32[256]{0:T(256)}, u32[]{:S(2)}) copy-start(f32[256]{0:T(256)} %param.17) | copy-start | bytes 3076
  13.6 36.4 %copy-start.11 = (s32[256]{0:T(256)S(1)}, s32[256]{0:T(256)}, u32[]{:S(2)}) copy-start(s32[256]{0:T(256)} %param.18) | copy-start | bytes 3076
  13.6 36.4 %copy-start.2 = (bf16[256,512]{1,0:T(8,128)(2,1)S(1)}, bf16[256,512]{1,0:T(8,128)(2,1)}, u32[]{:S(2)}) copy-start(bf16[256,512]{1,0:T(8,128)(2,1)} %param.19) | copy-start | bytes 786436
  19.4 4.9 %collective-permute-start.5 = (f32[]{:T(128)}, f32[]{:T(128)}, u32[]{:S(2)}, u32[]{:S(2)}) collective-permute-start(f32[]{:T(128)} %add.138), channel_id=1, source_target_pairs={{0,8},{4,12},{8,0},{12,4},{16,24},{20,28},{24,16},{28,20},{32,40},... | collective-permute-start | bytes 20 | tf_op jit(solution)/shard_map/ppermute | solution.py:23
  24.9 8.4 %collective-permute-start.6 = (f32[]{:T(128)}, f32[]{:T(128)}, u32[]{:S(2)}, u32[]{:S(2)}) collective-permute-start(f32[]{:T(128)} %add.139), channel_id=1, source_target_pairs={{0,16},{4,20},{8,24},{12,28},{16,0},{20,4},{24,8},{28,12},{32,48},... | collective-permute-start | bytes 20 | tf_op jit(solution)/shard_map/ppermute | solution.py:23
  34.0 5.1 %collective-permute-start.7 = (f32[]{:T(128)}, f32[]{:T(128)}, u32[]{:S(2)}, u32[]{:S(2)}) collective-permute-start(f32[]{:T(128)} %add.140), channel_id=1, source_target_pairs={{0,32},{4,36},{8,40},{12,44},{16,48},{20,52},{24,56},{28,60},{32,0... | collective-permute-start | bytes 20 | tf_op jit(solution)/shard_map/ppermute | solution.py:23
  39.8 3.6 %collective-permute-start.8 = (f32[]{:T(128)}, f32[]{:T(128)}, u32[]{:S(2)}, u32[]{:S(2)}) collective-permute-start(f32[]{:T(128)} %add.141), channel_id=1, source_target_pairs={{0,64},{4,68},{8,72},{12,76},{16,80},{20,84},{24,88},{28,92},{32,9... | collective-permute-start | bytes 20 | tf_op jit(solution)/shard_map/ppermute | solution.py:23
  44.1 5.1 %collective-permute-start.9 = (f32[]{:T(128)}, f32[]{:T(128)}, u32[]{:S(2)}, u32[]{:S(2)}) collective-permute-start(f32[]{:T(128)} %add.142), channel_id=1, source_target_pairs={{0,128},{4,132},{8,136},{12,140},{16,144},{20,148},{24,152},{28,15... | collective-permute-start | bytes 20 | tf_op jit(solution)/shard_map/ppermute | solution.py:23
  51.0 134.0 %copy-start.8 = (f32[128]{0:T(128)S(1)}, f32[128]{0:T(128)}, u32[]{:S(2)}) copy-start(f32[128]{0:T(128)} %param.15) | copy-start | bytes 1540
  184.9 18.7 %copy-start.6 = (f32[128]{0:T(128)S(1)}, f32[128]{0:T(128)}, u32[]{:S(2)}) copy-start(f32[128]{0:T(128)} %param.14) | copy-start | bytes 1540
  185.9 34.5 %collective-permute-start = (bf16[2,256,256]{1,2,0:T(8,128)(2,1)}, bf16[2,256,256]{1,2,0:T(8,128)(2,1)}, u32[]{:S(2)}, u32[]{:S(2)}) collective-permute-start(bf16[2,256,256]{1,2,0:T(8,128)(2,1)} %pad_maximum_fusion.1), channel_id=1, source_target_pairs={{0,16},{4,20},{8,24},{12,28},{16,32},{20,36},{24,40},{28,44},{32,4... | collective-permute-start | bytes 786440 | tf_op jit(solution)/shard_map/ppermute | solution.py:16
  192.1 34.8 %collective-permute-start.1 = (bf16[2,256,256]{1,2,0:T(8,128)(2,1)}, bf16[2,256,256]{1,2,0:T(8,128)(2,1)}, u32[]{:S(2)}, u32[]{:S(2)}) collective-permute-start(bf16[2,256,256]{1,2,0:T(8,128)(2,1)} %pad_maximum_fusion.1), channel_id=1, source_target_pairs={{0,12},{4,16},{8,20},{12,24},{16,28},{20,32},{24,36},{28,40},{32,4... | collective-permute-start | bytes 786440 | tf_op jit(solution)/shard_map/ppermute | solution.py:16
  196.0 39.0 %collective-permute-start.2 = (bf16[2,256,256]{1,2,0:T(8,128)(2,1)}, bf16[2,256,256]{1,2,0:T(8,128)(2,1)}, u32[]{:S(2)}, u32[]{:S(2)}) collective-permute-start(bf16[2,256,256]{1,2,0:T(8,128)(2,1)} %pad_maximum_fusion.1), channel_id=1, source_target_pairs={{0,8},{4,12},{8,16},{12,20},{16,24},{20,28},{24,32},{28,36},{32,40... | collective-permute-start | bytes 786440 | tf_op jit(solution)/shard_map/ppermute | solution.py:16
  199.6 38.1 %collective-permute-start.3 = (bf16[2,256,256]{1,2,0:T(8,128)(2,1)}, bf16[2,256,256]{1,2,0:T(8,128)(2,1)}, u32[]{:S(2)}, u32[]{:S(2)}) collective-permute-start(bf16[2,256,256]{1,2,0:T(8,128)(2,1)} %pad_maximum_fusion.1), channel_id=1, source_target_pairs={{0,4},{4,8},{8,12},{12,16},{16,20},{20,24},{24,28},{28,32},{32,36}... | collective-permute-start | bytes 786440 | tf_op jit(solution)/shard_map/ppermute | solution.py:16
  259.6 20.7 %copy-start.7 = (f32[128]{0:T(128)S(1)}, f32[128]{0:T(128)}, u32[]{:S(2)}) copy-start(f32[128]{0:T(128)} %param.14) | copy-start | bytes 1540
  262.1 19.4 %collective-permute-start.10 = (bf16[2,256,256]{2,1,0:T(8,128)(2,1)}, bf16[2,256,256]{2,1,0:T(8,128)(2,1)S(1)}, u32[]{:S(2)}, u32[]{:S(2)}) collective-permute-start(bf16[2,256,256]{2,1,0:T(8,128)(2,1)} %get-tuple-element.8), channel_id=1, source_target_pairs={{4,0},{8,4},{12,8},{16,12},{20,16},{24,20},{28,24},{32,28},{36,32}... | collective-permute-start | bytes 786440 | tf_op jit(solution)/shard_map/ppermute | solution.py:16
  268.4 20.9 %collective-permute-start.11 = (bf16[2,256,256]{2,1,0:T(8,128)(2,1)}, bf16[2,256,256]{2,1,0:T(8,128)(2,1)}, u32[]{:S(2)}, u32[]{:S(2)}) collective-permute-start(bf16[2,256,256]{2,1,0:T(8,128)(2,1)} %get-tuple-element.11), channel_id=1, source_target_pairs={{8,0},{12,4},{16,8},{20,12},{24,16},{28,20},{32,24},{36,28},{40,32... | collective-permute-start | bytes 786440 | tf_op jit(solution)/shard_map/ppermute | solution.py:16
  271.6 37.5 %collective-permute-start.12 = (bf16[2,256,256]{2,1,0:T(8,128)(2,1)}, bf16[2,256,256]{2,1,0:T(8,128)(2,1)}, u32[]{:S(2)}, u32[]{:S(2)}) collective-permute-start(bf16[2,256,256]{2,1,0:T(8,128)(2,1)} %get-tuple-element.10), channel_id=1, source_target_pairs={{12,0},{16,4},{20,8},{24,12},{28,16},{32,20},{36,24},{40,28},{44,3... | collective-permute-start | bytes 786440 | tf_op jit(solution)/shard_map/ppermute | solution.py:16
  273.6 41.2 %collective-permute-start.13 = (bf16[2,256,256]{2,1,0:T(8,128)(2,1)}, bf16[2,256,256]{2,1,0:T(8,128)(2,1)}, u32[]{:S(2)}, u32[]{:S(2)}) collective-permute-start(bf16[2,256,256]{2,1,0:T(8,128)(2,1)} %get-tuple-element.9), channel_id=1, source_target_pairs={{16,0},{20,4},{24,8},{28,12},{32,16},{36,20},{40,24},{44,28},{48,3... | collective-permute-start | bytes 786440 | tf_op jit(solution)/shard_map/ppermute | solution.py:16
  281.5 34.8 %copy-start.9 = (f32[128]{0:T(128)S(1)}, f32[128]{0:T(128)}, u32[]{:S(2)}) copy-start(f32[128]{0:T(128)} %param.15) | copy-start | bytes 1540
  325.5 3.3 collective-permute-start.14
  332.3 17.7 %collective-permute-start.15 = (bf16[256,1344]{0,1:T(8,128)(2,1)}, bf16[256,1344]{0,1:T(8,128)(2,1)S(1)}, u32[]{:S(2)}, u32[]{:S(2)}) collective-permute-start(bf16[256,1344]{0,1:T(8,128)(2,1)} %fusion.7), channel_id=1, source_target_pairs={{0,2},{1,3},{2,0},{3,1},{4,6},{5,7},{6,4},{7,5},{8,10},{9,11},{10,... | collective-permute-start | bytes 2064392 | tf_op jit(solution)/shard_map/ppermute | solution.py:40
  (7 other events, 63.5 us)
Sparse Core Ops, SparseCore 0:
  12.2 165.7 all-gather.3

commit v5 on v4

--- a/solution.py
+++ b/solution.py
@@ -162,10 +162,16 @@
     q_rot = norm_rotate(q_linear, q_gain, cosine, sine_table).astype(jnp.bfloat16)
     k_rot = norm_rotate(k_linear, k_gain, cosine, sine_table).astype(jnp.bfloat16)
     stacked = jnp.stack([k_rot.reshape(tok_rows, kv_heads * head_width), values])
-    received = []
-    for offset in range(1, pred_count + 1):
-        received.append(passed_along(stacked, "seq", offset))
-    extended = jnp.concatenate(received[::-1] + [stacked], axis=1)
+    if pred_count == 4:
+        near_one = passed_along(stacked, "seq", 1)
+        near_two = passed_along(stacked, "seq", 2)
+        far_pair = passed_along(jnp.concatenate([near_two, near_one], axis=1), "seq", 2)
+        extended = jnp.concatenate([far_pair, near_two, near_one, stacked], axis=1)
+    else:
+        received = []
+        for offset in range(1, pred_count + 1):
+            received.append(passed_along(stacked, "seq", offset))
+        extended = jnp.concatenate(received[::-1] + [stacked], axis=1)
     key_rows = extended[0].reshape(key_span, kv_heads, head_width)
     value_rows = extended[1].reshape(key_span, kv_heads, head_width)
     attended, dquery, key_grads, dvalues = block_grad(
@@ -178,14 +184,29 @@
         ]
     )
     local_grads = stacked_grads[:, pred_count * tok_rows :]
-    for offset in range(1, pred_count + 1):
-        local_grads = local_grads + passed_along(
-            stacked_grads[
-                :, (pred_count - offset) * tok_rows : (pred_count - offset + 1) * tok_rows
-            ].astype(jnp.bfloat16),
-            "seq",
-            -offset,
+    if pred_count == 4:
+        far_back = passed_along(
+            stacked_grads[:, : 2 * tok_rows].astype(jnp.bfloat16), "seq", -2
         ).astype(jnp.float32)
+        near_sums = stacked_grads[:, 2 * tok_rows : 4 * tok_rows] + far_back
+        local_grads = (
+            local_grads
+            + passed_along(near_sums[:, :tok_rows].astype(jnp.bfloat16), "seq", -2).astype(
+                jnp.float32
+            )
+            + passed_along(near_sums[:, tok_rows:].astype(jnp.bfloat16), "seq", -1).astype(
+                jnp.float32
+            )
+        )
+    else:
+        for offset in range(1, pred_count + 1):
+            local_grads = local_grads + passed_along(
+                stacked_grads[
+                    :, (pred_count - offset) * tok_rows : (pred_count - offset + 1) * tok_rows
+                ].astype(jnp.bfloat16),
+                "seq",
+                -offset,
+            ).astype(jnp.float32)
     key_total = local_grads[0].reshape(tok_rows, kv_heads, head_width)
     _, back_query = jax.vjp(
         lambda linear_in: norm_rotate(linear_in, q_gain, cosine, sine_table), q_linear

time: 359 us -> 353 us (0.983)
  starting transfers between devices: 59.1 us -> 42.3 us
  waiting for transfers between devices: 198 us -> 208 us
  local copies, waits for them, and re-layouts: 39.3 us -> 34.1 us
    ppermute x8 -> x6, starting transfers between devices: 35.8 us -> 19.6 us  [passed_along(): return lax.ppermute(block, axis, route)]
    ppermute x8 -> x6, waiting for transfers between devices: 47.7 us -> 57 us  [passed_along(): return lax.ppermute(block, axis, route)]
    unnamed x34 -> x46, local copies, waits for them, and re-layouts: 11.8 us -> 8.26 us
  transfers between devices with their start and end apart: 17 -> 15, of which waited for: 14 -> 13; matrix products, arithmetic and copies ran while one was open for 9% -> 9% of each run, Pallas kernels for 0% -> 0%
where the time goes in v5:
time: 353 us; the launch traced here: 352 us
  waiting for transfers between devices  208 us (59%)
  starting transfers between devices  42.3 us (12%)
  local copies, waits for them, and re-layouts  34.1 us (10%)
  matrix products  29.4 us (8%)
  between operations  19.1 us (5%)
  other arithmetic  18.7 us (5%)
    all_gather x1, waiting for transfers between devices, body(): lax.all_gather(jnp.concatenate([q_weight, k_weight, v_weight], axis=1), '...  128 us
    ppermute x6, waiting for transfers between devices, passed_along(): return lax.ppermute(block, axis, route)  57 us
    ppermute x6, starting transfers between devices, butterfly_sum(): lax.ppermute(value, axis, [(i, i ^ step) for i in range(size)])  22.6 us
    ppermute x6, starting transfers between devices, passed_along(): return lax.ppermute(block, axis, route)  19.6 us
    ppermute x1, waiting for transfers between devices, head_scatter_sum(): lax.ppermute(sent.astype(jnp.bfloat16), axis, [(i, i ^ 2) for i in range(...  15.9 us
    dot_general x1, local copies, waits for them, and re-layouts, body(): lax.dot_general(joined_grad, joined_rows.reshape(seq_count * row_block, j...  14.2 us
    unnamed x46, local copies, waits for them, and re-layouts  8.26 us
  transfers between devices with their start and end apart: 15, of which 13 were waited for; matrix products, arithmetic and copies ran while one was open for 9% of the time, Pallas kernels for 0%

profile of v5, /device:TPU:38, one launch (start us, length us, event | category | flops | bytes accessed | tf_op | source)
XLA Modules:
  0.0 352.1 jit_solution(730022034148744854)
XLA Ops:
  10.3 3.3 copy.50
  20.0 4.7 %collective-permute-start.4 = (f32[]{:T(128)}, f32[]{:T(128)}, u32[]{:S(2)}, u32[]{:S(2)}) collective-permute-start(f32[]{:T(128)} %add.135), channel_id=1, source_target_pairs={{0,8},{4,12},{8,0},{12,4},{16,24},{20,28},{24,16},{28,20},{32,40},... | collective-permute-start | bytes 20 | tf_op jit(solution)/shard_map/ppermute | solution.py:23
  25.5 8.2 %collective-permute-start.5 = (f32[]{:T(128)}, f32[]{:T(128)}, u32[]{:S(2)}, u32[]{:S(2)}) collective-permute-start(f32[]{:T(128)} %add.136), channel_id=1, source_target_pairs={{0,16},{4,20},{8,24},{12,28},{16,0},{20,4},{24,8},{28,12},{32,48},... | collective-permute-start | bytes 20 | tf_op jit(solution)/shard_map/ppermute | solution.py:23
  34.6 4.6 %collective-permute-start.6 = (f32[]{:T(128)}, f32[]{:T(128)}, u32[]{:S(2)}, u32[]{:S(2)}) collective-permute-start(f32[]{:T(128)} %add.137), channel_id=1, source_target_pairs={{0,32},{4,36},{8,40},{12,44},{16,48},{20,52},{24,56},{28,60},{32,0... | collective-permute-start | bytes 20 | tf_op jit(solution)/shard_map/ppermute | solution.py:23
  44.6 2.8 collective-permute-start.8
  50.4 127.6 %all-gather.4.cloned.1.call-done = bf16[64,84,1024]{2,1,0:T(8,128)(2,1)} async-done(((bf16[1,84,1024]{2,1,0:T(8,128)(2,1)}), bf16[64,84,1024]{2,1,0:T(8,128)(2,1)}) %all-gather.4.cloned.1.call-update) | async-done | bytes 11010064 | tf_op jit(solution)/shard_map/all_gather | solution.py:148
  178.0 6.9 %convolution_bitcast_fusion.1 = f32[256,1024]{0,1:T(8,128)S(1)} fusion(bf16[64,84,1024]{2,1,0:T(8,128)(2,1)} %all-gather.4.cloned.1.call-done, bf16[256,64,84]{0,2,1:T(8,128)(2,1)} %reshape.219), kind=kOutput, calls=%fused_computation.20 | convolution fusion | flops 2818572288 | bytes 14811136 | tf_op jit(solution)/shard_map/tsr,src->tc/dot_general | solution.py:152
  186.0 5.3 %collective-permute-start = (bf16[2,256,256]{1,2,0:T(8,128)(2,1)}, bf16[2,256,256]{1,2,0:T(8,128)(2,1)S(1)}, u32[]{:S(2)}, u32[]{:S(2)}) collective-permute-start(bf16[2,256,256]{1,2,0:T(8,128)(2,1)} %pad_maximum_fusion.2), channel_id=1, source_target_pairs={{0,8},{4,12},{8,16},{12,20},{16,24},{20,28},{24,32},{28,36},{32,40... | collective-permute-start | bytes 786440 | tf_op jit(solution)/shard_map/ppermute | solution.py:16
  191.3 2.6 collective-permute-start.1
  196.5 10.8 %collective-permute-done = bf16[2,256,256]{1,2,0:T(8,128)(2,1)S(1)} collective-permute-done((bf16[2,256,256]{1,2,0:T(8,128)(2,1)}, bf16[2,256,256]{1,2,0:T(8,128)(2,1)S(1)}, u32[]{:S(2)}, u32[]{:S(2)}) %collective-permute-start) | collective-permute-done | bytes 262176 | tf_op jit(solution)/shard_map/ppermute | solution.py:16
  208.2 4.9 %collective-permute-start.2 = (bf16[2,512,256]{1,2,0:T(8,128)(2,1)}, bf16[2,512,256]{1,2,0:T(8,128)(2,1)}, u32[]{:S(2)}, u32[]{:S(2)}) collective-permute-start(bf16[2,512,256]{1,2,0:T(8,128)(2,1)} %pad_maximum_fusion.1), channel_id=1, source_target_pairs={{0,8},{4,12},{8,16},{12,20},{16,24},{20,28},{24,32},{28,36},{32,40... | collective-permute-start | bytes 1572872 | tf_op jit(solution)/shard_map/ppermute | solution.py:16
  213.7 14.2 %dot_general.36 = bf16[2,2,1344,1024]{3,2,1,0:T(8,128)(2,1)} reshape(bf16[64,84,1024]{2,1,0:T(8,128)(2,1)} %all-gather.4.cloned.1.call-done) | data formatting | bytes 22020096 | tf_op jit(solution)/shard_map/dot_general | solution.py:221
  227.9 12.1 %collective-permute-done.2 = bf16[2,512,256]{1,2,0:T(8,128)(2,1)} collective-permute-done((bf16[2,512,256]{1,2,0:T(8,128)(2,1)}, bf16[2,512,256]{1,2,0:T(8,128)(2,1)}, u32[]{:S(2)}, u32[]{:S(2)}) %collective-permute-start.2) | collective-permute-done | bytes 524320 | tf_op jit(solution)/shard_map/ppermute | solution.py:16
  245.6 2.6 multiply_reduce_fusion.1
  248.2 3.4 fusion.30
  251.6 4.1 %fusion.1 = bf16[2,2,256,1280]{2,3,1,0:T(8,128)(2,1)} fusion(bf16[1280,2,128,1]{0,2,3,1:T(8,128)(2,1)S(1)} %bitcast.116, bf16[256,2,2,128]{0,3,2,1:T(8,128)(2,1)S(1)} %bitcast.120, f32[2,2,256,1280]{2,3,1,0:T(8,128)S(1)} %get-tuple-element.23, f32[2,2,256]{2,1,0:T(2,128)S(1)} %bitcast.121, f32[2,2,256]{2,1,0:T(2,128)S(1)} %log_add_fusion, ...), kind=kOutput, calls=%fused_computation.2 | convolution fusion | flops 346030080 | bytes 10429712 | tf_op jit(solution)/shard_map/tgjd,sgd->gjts/dot_general | solution.py:94
  257.5 3.8 %fusion.3 = f32[2,128,1280]{2,1,0:T(8,128)} fusion(bf16[2,2,256,1280]{2,3,1,0:T(8,128)(2,1)} %fusion.1, bf16[256,2,2,64]{3,0,2,1:T(8,128)(2,1)S(1)} %bitcast.112, bf16[256,2,2,64]{3,0,2,1:T(8,128)(2,1)S(1)} %bitcast.110), kind=kOutput, calls=%fused_computation.15 | convolution fusion | flops 336396288 | bytes 4194304 | tf_op jit(solution)/shard_map/gjts,tgjd->sgd/dot_general | solution.py:101
  263.2 2.8 collective-permute-start.9
  266.8 27.6 %collective-permute-done.9 = bf16[2,512,256]{2,1,0:T(8,128)(2,1)S(1)} collective-permute-done((bf16[2,512,256]{2,1,0:T(8,128)(2,1)S(1)}, bf16[2,512,256]{2,1,0:T(8,128)(2,1)S(1)}, u32[]{:S(2)}, u32[]{:S(2)}) %collective-permute-start.9) | collective-permute-done | bytes 524320 | tf_op jit(solution)/shard_map/ppermute | solution.py:16
  300.4 4.4 %collective-permute-done.10 = bf16[2,256,256]{2,1,0:T(8,128)(2,1)S(1)} collective-permute-done((bf16[2,256,256]{2,1,0:T(8,128)(2,1)}, bf16[2,256,256]{2,1,0:T(8,128)(2,1)S(1)}, u32[]{:S(2)}, u32[]{:S(2)}) %collective-permute-start.10) | collective-permute-done | bytes 262176 | tf_op jit(solution)/shard_map/ppermute | solution.py:16
  311.3 6.0 %fusion.15 = f32[256,2,2,1344]{0,3,2,1:T(8,128)S(1)} fusion(bf16[2,2,1344,1024]{3,2,1,0:T(8,128)(2,1)} %dot_general.36, bf16[256,256]{1,0:T(8,128)(2,1)S(1)} %fusion.22, bf16[256,256]{1,0:T(8,128)(2,1)S(1)} %copy.87, bf16[256,512]{1,0:T(8,128)(2,1)S(1)} %copy-done.12), kind=kOutput, calls=%fused_computation.39 | convolution fusion | flops 2820145152 | bytes 17039360 | tf_op jit(solution)/shard_map/dot_general | solution.py:221
  319.9 3.2 collective-permute-done.12
  323.1 2.5 bitcast_add_fusion
  328.3 15.9 %collective-permute-done.13 = bf16[256,1344]{0,1:T(8,128)(2,1)S(1)} collective-permute-done((bf16[256,1344]{0,1:T(8,128)(2,1)}, bf16[256,1344]{0,1:T(8,128)(2,1)S(1)}, u32[]{:S(2)}, u32[]{:S(2)}) %collective-permute-start.13) | collective-permute-done | bytes 688160 | tf_op jit(solution)/shard_map/ppermute | solution.py:40
  (117 shorter events, 48.7 us)
Async XLA Ops:
  7.2 170.9 %all-gather.4.cloned.1.call-start = ((), (), s32[]{:S(2)}) async-start(), calls=%async_computation | async-start | bytes 11714560 | tf_op jit(solution)/shard_map/all_gather | solution.py:148
  10.2 8.6 %collective-permute-start.3 = (f32[]{:T(128)}, f32[]{:T(128)}, u32[]{:S(2)}, u32[]{:S(2)}) collective-permute-start(f32[]{:T(128)} %fusion.25), channel_id=1, source_target_pairs={{0,4},{4,0},{8,12},{12,8},{16,20},{20,16},{24,28},{28,24},{32,36},... | collective-permute-start | bytes 20 | tf_op jit(solution)/shard_map/ppermute | solution.py:23
  13.6 36.7 %copy-start.18 = (f32[256]{0:T(256)S(1)}, f32[256]{0:T(256)}, u32[]{:S(2)}) copy-start(f32[256]{0:T(256)} %param.17) | copy-start | bytes 3076
  13.6 36.7 %copy-start.19 = (s32[256]{0:T(256)S(1)}, s32[256]{0:T(256)}, u32[]{:S(2)}) copy-start(s32[256]{0:T(256)} %param.18) | copy-start | bytes 3076
  20.0 4.9 %collective-permute-start.4 = (f32[]{:T(128)}, f32[]{:T(128)}, u32[]{:S(2)}, u32[]{:S(2)}) collective-permute-start(f32[]{:T(128)} %add.135), channel_id=1, source_target_pairs={{0,8},{4,12},{8,0},{12,4},{16,24},{20,28},{24,16},{28,20},{32,40},... | collective-permute-start | bytes 20 | tf_op jit(solution)/shard_map/ppermute | solution.py:23
  25.5 8.4 %collective-permute-start.5 = (f32[]{:T(128)}, f32[]{:T(128)}, u32[]{:S(2)}, u32[]{:S(2)}) collective-permute-start(f32[]{:T(128)} %add.136), channel_id=1, source_target_pairs={{0,16},{4,20},{8,24},{12,28},{16,0},{20,4},{24,8},{28,12},{32,48},... | collective-permute-start | bytes 20 | tf_op jit(solution)/shard_map/ppermute | solution.py:23
  34.6 5.1 %collective-permute-start.6 = (f32[]{:T(128)}, f32[]{:T(128)}, u32[]{:S(2)}, u32[]{:S(2)}) collective-permute-start(f32[]{:T(128)} %add.137), channel_id=1, source_target_pairs={{0,32},{4,36},{8,40},{12,44},{16,48},{20,52},{24,56},{28,60},{32,0... | collective-permute-start | bytes 20 | tf_op jit(solution)/shard_map/ppermute | solution.py:23
  40.3 3.6 %collective-permute-start.7 = (f32[]{:T(128)}, f32[]{:T(128)}, u32[]{:S(2)}, u32[]{:S(2)}) collective-permute-start(f32[]{:T(128)} %add.138), channel_id=1, source_target_pairs={{0,64},{4,68},{8,72},{12,76},{16,80},{20,84},{24,88},{28,92},{32,9... | collective-permute-start | bytes 20 | tf_op jit(solution)/shard_map/ppermute | solution.py:23
  44.6 5.1 %collective-permute-start.8 = (f32[]{:T(128)}, f32[]{:T(128)}, u32[]{:S(2)}, u32[]{:S(2)}) collective-permute-start(f32[]{:T(128)} %add.139), channel_id=1, source_target_pairs={{0,128},{4,132},{8,136},{12,140},{16,144},{20,148},{24,152},{28,15... | collective-permute-start | bytes 20 | tf_op jit(solution)/shard_map/ppermute | solution.py:23
  50.4 134.7 %copy-start.16 = (f32[128]{0:T(128)S(1)}, f32[128]{0:T(128)}, u32[]{:S(2)}) copy-start(f32[128]{0:T(128)} %param.15) | copy-start | bytes 1540
  178.0 15.9 %copy-start.10 = (bf16[256,512]{1,0:T(8,128)(2,1)S(1)}, bf16[256,512]{1,0:T(8,128)(2,1)}, u32[]{:S(2)}) copy-start(bf16[256,512]{1,0:T(8,128)(2,1)} %param.19) | copy-start | bytes 786436
  185.0 28.3 %copy-start = (f32[256,1024]{0,1:T(8,128)}, f32[256,1024]{0,1:T(8,128)S(1)}, u32[]{:S(2)}) copy-start(f32[256,1024]{0,1:T(8,128)S(1)} %convolution_bitcast_fusion.1) | copy-start | bytes 3145732
  185.0 28.1 %copy-start.14 = (f32[128]{0:T(128)S(1)}, f32[128]{0:T(128)}, u32[]{:S(2)}) copy-start(f32[128]{0:T(128)} %param.14) | copy-start | bytes 1540
  186.0 21.3 %collective-permute-start = (bf16[2,256,256]{1,2,0:T(8,128)(2,1)}, bf16[2,256,256]{1,2,0:T(8,128)(2,1)S(1)}, u32[]{:S(2)}, u32[]{:S(2)}) collective-permute-start(bf16[2,256,256]{1,2,0:T(8,128)(2,1)} %pad_maximum_fusion.2), channel_id=1, source_target_pairs={{0,8},{4,12},{8,16},{12,20},{16,24},{20,28},{24,32},{28,36},{32,40... | collective-permute-start | bytes 786440 | tf_op jit(solution)/shard_map/ppermute | solution.py:16
  191.3 16.1 %collective-permute-start.1 = (bf16[2,256,256]{1,2,0:T(8,128)(2,1)}, bf16[2,256,256]{1,2,0:T(8,128)(2,1)S(1)}, u32[]{:S(2)}, u32[]{:S(2)}) collective-permute-start(bf16[2,256,256]{1,2,0:T(8,128)(2,1)} %pad_maximum_fusion.2), channel_id=1, source_target_pairs={{0,4},{4,8},{8,12},{12,16},{16,20},{20,24},{24,28},{28,32},{32,36}... | collective-permute-start | bytes 786440 | tf_op jit(solution)/shard_map/ppermute | solution.py:16
  208.2 31.8 %collective-permute-start.2 = (bf16[2,512,256]{1,2,0:T(8,128)(2,1)}, bf16[2,512,256]{1,2,0:T(8,128)(2,1)}, u32[]{:S(2)}, u32[]{:S(2)}) collective-permute-start(bf16[2,512,256]{1,2,0:T(8,128)(2,1)} %pad_maximum_fusion.1), channel_id=1, source_target_pairs={{0,8},{4,12},{8,16},{12,20},{16,24},{20,28},{24,32},{28,36},{32,40... | collective-permute-start | bytes 1572872 | tf_op jit(solution)/shard_map/ppermute | solution.py:16
  213.5 27.7 %copy-start.5 = (bf16[256,4,64]{2,0,1:T(8,128)(2,1)}, bf16[256,4,64]{2,0,1:T(8,128)(2,1)S(1)}, u32[]{:S(2)}) copy-start(bf16[256,4,64]{2,0,1:T(8,128)(2,1)S(1)} %copy.51) | copy-start | bytes 393220
  213.7 27.5 %copy-start.7 = (bf16[256,4,64]{2,0,1:T(8,128)(2,1)}, bf16[256,4,64]{2,0,1:T(8,128)(2,1)S(1)}, u32[]{:S(2)}) copy-start(bf16[256,4,64]{2,0,1:T(8,128)(2,1)S(1)} %copy.52) | copy-start | bytes 393220
  227.9 13.4 %copy-start.20 = (s32[2,2]{1,0:T(2,128)S(1)}, s32[2,2]{1,0:T(2,128)}, u32[]{:S(2)}) copy-start(s32[2,2]{1,0:T(2,128)} %lt.36) | copy-start | bytes 52
  263.2 31.2 %collective-permute-start.9 = (bf16[2,512,256]{2,1,0:T(8,128)(2,1)S(1)}, bf16[2,512,256]{2,1,0:T(8,128)(2,1)S(1)}, u32[]{:S(2)}, u32[]{:S(2)}) collective-permute-start(bf16[2,512,256]{2,1,0:T(8,128)(2,1)S(1)} %fusion.9), channel_id=1, source_target_pairs={{8,0},{12,4},{16,8},{20,12},{24,16},{28,20},{32,24},{36,28},{40,32... | collective-permute-start | bytes 1572872 | tf_op jit(solution)/shard_map/ppermute | solution.py:16
  295.4 9.5 %collective-permute-start.10 = (bf16[2,256,256]{2,1,0:T(8,128)(2,1)}, bf16[2,256,256]{2,1,0:T(8,128)(2,1)S(1)}, u32[]{:S(2)}, u32[]{:S(2)}) collective-permute-start(bf16[2,256,256]{2,1,0:T(8,128)(2,1)} %get-tuple-element.14), channel_id=1, source_target_pairs={{8,0},{12,4},{16,8},{20,12},{24,16},{28,20},{32,24},{36,28},{40,32... | collective-permute-start | bytes 786440 | tf_op jit(solution)/shard_map/ppermute | solution.py:16
  297.3 10.4 %collective-permute-start.11 = (bf16[2,256,256]{2,1,0:T(8,128)(2,1)}, bf16[2,256,256]{2,1,0:T(8,128)(2,1)}, u32[]{:S(2)}, u32[]{:S(2)}) collective-permute-start(bf16[2,256,256]{2,1,0:T(8,128)(2,1)} %get-tuple-element.15), channel_id=1, source_target_pairs={{4,0},{8,4},{12,8},{16,12},{20,16},{24,20},{28,24},{32,28},{36,32}... | collective-permute-start | bytes 786440 | tf_op jit(solution)/shard_map/ppermute | solution.py:16
  319.8 3.3 collective-permute-start.12
  326.5 17.7 %collective-permute-start.13 = (bf16[256,1344]{0,1:T(8,128)(2,1)}, bf16[256,1344]{0,1:T(8,128)(2,1)S(1)}, u32[]{:S(2)}, u32[]{:S(2)}) collective-permute-start(bf16[256,1344]{0,1:T(8,128)(2,1)} %fusion.10), channel_id=1, source_target_pairs={{0,2},{1,3},{2,0},{3,1},{4,6},{5,7},{6,4},{7,5},{8,10},{9,11},{10,... | collective-permute-start | bytes 2064392 | tf_op jit(solution)/shard_map/ppermute | solution.py:40
  (13 other events, 59.0 us)
Sparse Core Ops, SparseCore 0:
  12.2 165.8 all-gather.3

commit v6 on v4

--- a/solution.py
+++ b/solution.py
@@ -162,10 +162,16 @@
     q_rot = norm_rotate(q_linear, q_gain, cosine, sine_table).astype(jnp.bfloat16)
     k_rot = norm_rotate(k_linear, k_gain, cosine, sine_table).astype(jnp.bfloat16)
     stacked = jnp.stack([k_rot.reshape(tok_rows, kv_heads * head_width), values])
-    received = []
-    for offset in range(1, pred_count + 1):
-        received.append(passed_along(stacked, "seq", offset))
-    extended = jnp.concatenate(received[::-1] + [stacked], axis=1)
+    if pred_count == 4:
+        near_one = passed_along(stacked, "seq", 1)
+        near_two = passed_along(stacked, "seq", 2)
+        far_pair = passed_along(jnp.concatenate([near_two, near_one], axis=1), "seq", 2)
+        extended = jnp.concatenate([far_pair, near_two, near_one, stacked], axis=1)
+    else:
+        received = []
+        for offset in range(1, pred_count + 1):
+            received.append(passed_along(stacked, "seq", offset))
+        extended = jnp.concatenate(received[::-1] + [stacked], axis=1)
     key_rows = extended[0].reshape(key_span, kv_heads, head_width)
     value_rows = extended[1].reshape(key_span, kv_heads, head_width)
     attended, dquery, key_grads, dvalues = block_grad(

time: 359 us -> 356 us (level)
  starting transfers between devices: 59.1 us -> 49.9 us
  waiting for transfers between devices: 198 us -> 202 us
  other arithmetic: 15.5 us -> 19.4 us
    ppermute x8 -> x7, starting transfers between devices: 35.8 us -> 27.2 us  [passed_along(): return lax.ppermute(block, axis, route)]
    unnamed x34 -> x32, local copies, waits for them, and re-layouts: 11.8 us -> 7.9 us
    ppermute x8 -> x7, waiting for transfers between devices: 47.7 us -> 49.8 us  [passed_along(): return lax.ppermute(block, axis, route)]
  transfers between devices with their start and end apart: 17 -> 16, of which waited for: 14 -> 14; matrix products, arithmetic and copies ran while one was open for 9% -> 9% of each run, Pallas kernels for 0% -> 0%
where the time goes in v6:
time: 356 us; the launch traced here: 353 us
  waiting for transfers between devices  202 us (57%)
  starting transfers between devices  49.9 us (14%)
  local copies, waits for them, and re-layouts  36.3 us (10%)
  matrix products  26.6 us (7%)
  other arithmetic  19.4 us (5%)
  between operations  19.4 us (5%)
    all_gather x1, waiting for transfers between devices, body(): lax.all_gather(jnp.concatenate([q_weight, k_weight, v_weight], axis=1), '...  128 us
    ppermute x7, waiting for transfers between devices, passed_along(): return lax.ppermute(block, axis, route)  49.8 us
    ppermute x7, starting transfers between devices, passed_along(): return lax.ppermute(block, axis, route)  27.2 us
    ppermute x6, starting transfers between devices, butterfly_sum(): lax.ppermute(value, axis, [(i, i ^ step) for i in range(size)])  22.6 us
    ppermute x1, waiting for transfers between devices, head_scatter_sum(): lax.ppermute(sent.astype(jnp.bfloat16), axis, [(i, i ^ 2) for i in range(...  15.9 us
    dot_general x1, local copies, waits for them, and re-layouts, body(): lax.dot_general(joined_grad, joined_rows.reshape(seq_count * row_block, j...  13.9 us
    unnamed x32, local copies, waits for them, and re-layouts  7.9 us
  transfers between devices with their start and end apart: 16, of which 14 were waited for; matrix products, arithmetic and copies ran while one was open for 9% of the time, Pallas kernels for 0%

profile of v6, /device:TPU:38, one launch (start us, length us, event | category | flops | bytes accessed | tf_op | source)
XLA Modules:
  0.0 353.3 jit_solution(7687356322732473065)
XLA Ops:
  10.3 3.3 copy.50
  19.3 4.7 %collective-permute-start.4 = (f32[]{:T(128)}, f32[]{:T(128)}, u32[]{:S(2)}, u32[]{:S(2)}) collective-permute-start(f32[]{:T(128)} %add.138), channel_id=1, source_target_pairs={{0,8},{4,12},{8,0},{12,4},{16,24},{20,28},{24,16},{28,20},{32,40},... | collective-permute-start | bytes 20 | tf_op jit(solution)/shard_map/ppermute | solution.py:23
  24.9 8.2 %collective-permute-start.5 = (f32[]{:T(128)}, f32[]{:T(128)}, u32[]{:S(2)}, u32[]{:S(2)}) collective-permute-start(f32[]{:T(128)} %add.139), channel_id=1, source_target_pairs={{0,16},{4,20},{8,24},{12,28},{16,0},{20,4},{24,8},{28,12},{32,48},... | collective-permute-start | bytes 20 | tf_op jit(solution)/shard_map/ppermute | solution.py:23
  34.0 4.6 %collective-permute-start.6 = (f32[]{:T(128)}, f32[]{:T(128)}, u32[]{:S(2)}, u32[]{:S(2)}) collective-permute-start(f32[]{:T(128)} %add.140), channel_id=1, source_target_pairs={{0,32},{4,36},{8,40},{12,44},{16,48},{20,52},{24,56},{28,60},{32,0... | collective-permute-start | bytes 20 | tf_op jit(solution)/shard_map/ppermute | solution.py:23
  44.1 2.8 collective-permute-start.8
  50.0 128.0 %all-gather.4.cloned.1.call-done = bf16[64,84,1024]{2,1,0:T(8,128)(2,1)} async-done(((bf16[1,84,1024]{2,1,0:T(8,128)(2,1)}), bf16[64,84,1024]{2,1,0:T(8,128)(2,1)}) %all-gather.4.cloned.1.call-update) | async-done | bytes 11010064 | tf_op jit(solution)/shard_map/all_gather | solution.py:148
  178.0 6.9 %convolution_bitcast_fusion.1 = f32[256,1024]{0,1:T(8,128)S(1)} fusion(bf16[64,84,1024]{2,1,0:T(8,128)(2,1)} %all-gather.4.cloned.1.call-done, bf16[256,64,84]{0,2,1:T(8,128)(2,1)} %reshape.219), kind=kOutput, calls=%fused_computation.20 | convolution fusion | flops 2818572288 | bytes 14811136 | tf_op jit(solution)/shard_map/tsr,src->tc/dot_general | solution.py:152
  185.9 5.3 %collective-permute-start = (bf16[2,256,256]{1,2,0:T(8,128)(2,1)}, bf16[2,256,256]{1,2,0:T(8,128)(2,1)S(1)}, u32[]{:S(2)}, u32[]{:S(2)}) collective-permute-start(bf16[2,256,256]{1,2,0:T(8,128)(2,1)} %pad_maximum_fusion.2), channel_id=1, source_target_pairs={{0,8},{4,12},{8,16},{12,20},{16,24},{20,28},{24,32},{28,36},{32,40... | collective-permute-start | bytes 786440 | tf_op jit(solution)/shard_map/ppermute | solution.py:16
  196.5 10.8 %collective-permute-done = bf16[2,256,256]{1,2,0:T(8,128)(2,1)S(1)} collective-permute-done((bf16[2,256,256]{1,2,0:T(8,128)(2,1)}, bf16[2,256,256]{1,2,0:T(8,128)(2,1)S(1)}, u32[]{:S(2)}, u32[]{:S(2)}) %collective-permute-start) | collective-permute-done | bytes 262176 | tf_op jit(solution)/shard_map/ppermute | solution.py:16
  209.2 4.9 %collective-permute-start.2 = (bf16[2,512,256]{1,2,0:T(8,128)(2,1)}, bf16[2,512,256]{1,2,0:T(8,128)(2,1)}, u32[]{:S(2)}, u32[]{:S(2)}) collective-permute-start(bf16[2,512,256]{1,2,0:T(8,128)(2,1)} %pad_maximum_fusion.1), channel_id=1, source_target_pairs={{0,8},{4,12},{8,16},{12,20},{16,24},{20,28},{24,32},{28,36},{32,40... | collective-permute-start | bytes 1572872 | tf_op jit(solution)/shard_map/ppermute | solution.py:16
  216.9 13.9 %dot_general.36 = bf16[2,2,1344,1024]{3,2,1,0:T(8,128)(2,1)} reshape(bf16[64,84,1024]{2,1,0:T(8,128)(2,1)} %all-gather.4.cloned.1.call-done) | data formatting | bytes 22020096 | tf_op jit(solution)/shard_map/dot_general | solution.py:206
  230.8 10.2 %collective-permute-done.2 = bf16[2,512,256]{1,2,0:T(8,128)(2,1)} collective-permute-done((bf16[2,512,256]{1,2,0:T(8,128)(2,1)}, bf16[2,512,256]{1,2,0:T(8,128)(2,1)}, u32[]{:S(2)}, u32[]{:S(2)}) %collective-permute-start.2) | collective-permute-done | bytes 524320 | tf_op jit(solution)/shard_map/ppermute | solution.py:16
  249.4 3.4 fusion.29
  252.8 3.1 fusion.1
  260.3 2.8 copy.63
  268.2 4.5 %collective-permute-start.11 = (bf16[2,256,256]{2,1,0:T(8,128)(2,1)}, bf16[2,256,256]{2,1,0:T(8,128)(2,1)}, u32[]{:S(2)}, u32[]{:S(2)}) collective-permute-start(bf16[2,256,256]{2,1,0:T(8,128)(2,1)} %get-tuple-element.10), channel_id=1, source_target_pairs={{12,0},{16,4},{20,8},{24,12},{28,16},{32,20},{36,24},{40,28},{44,3... | collective-permute-start | bytes 786440 | tf_op jit(solution)/shard_map/ppermute | solution.py:16
  272.7 5.3 %collective-permute-start.12 = (bf16[2,256,256]{2,1,0:T(8,128)(2,1)}, bf16[2,256,256]{2,1,0:T(8,128)(2,1)}, u32[]{:S(2)}, u32[]{:S(2)}) collective-permute-start(bf16[2,256,256]{2,1,0:T(8,128)(2,1)} %get-tuple-element.9), channel_id=1, source_target_pairs={{16,0},{20,4},{24,8},{28,12},{32,16},{36,20},{40,24},{44,28},{48,3... | collective-permute-start | bytes 786440 | tf_op jit(solution)/shard_map/ppermute | solution.py:16
  281.4 5.8 %collective-permute-done.10 = bf16[2,256,256]{2,1,0:T(8,128)(2,1)S(1)} collective-permute-done((bf16[2,256,256]{2,1,0:T(8,128)(2,1)}, bf16[2,256,256]{2,1,0:T(8,128)(2,1)S(1)}, u32[]{:S(2)}, u32[]{:S(2)}) %collective-permute-start.10) | collective-permute-done | bytes 262176 | tf_op jit(solution)/shard_map/ppermute | solution.py:16
  287.2 5.3 %collective-permute-done.11 = bf16[2,256,256]{2,1,0:T(8,128)(2,1)} collective-permute-done((bf16[2,256,256]{2,1,0:T(8,128)(2,1)}, bf16[2,256,256]{2,1,0:T(8,128)(2,1)}, u32[]{:S(2)}, u32[]{:S(2)}) %collective-permute-start.11) | collective-permute-done | bytes 262176 | tf_op jit(solution)/shard_map/ppermute | solution.py:16
  292.5 12.2 %collective-permute-done.12 = bf16[2,256,256]{2,1,0:T(8,128)(2,1)} collective-permute-done((bf16[2,256,256]{2,1,0:T(8,128)(2,1)}, bf16[2,256,256]{2,1,0:T(8,128)(2,1)}, u32[]{:S(2)}, u32[]{:S(2)}) %collective-permute-start.12) | collective-permute-done | bytes 262176 | tf_op jit(solution)/shard_map/ppermute | solution.py:16
  304.6 5.6 %collective-permute-done.9 = bf16[2,256,256]{2,1,0:T(8,128)(2,1)} collective-permute-done((bf16[2,256,256]{2,1,0:T(8,128)(2,1)}, bf16[2,256,256]{2,1,0:T(8,128)(2,1)}, u32[]{:S(2)}, u32[]{:S(2)}) %collective-permute-start.9) | collective-permute-done | bytes 262176 | tf_op jit(solution)/shard_map/ppermute | solution.py:16
  312.5 5.9 %fusion.14 = f32[256,2,2,1344]{0,3,2,1:T(8,128)S(1)} fusion(bf16[2,2,1344,1024]{3,2,1,0:T(8,128)(2,1)} %dot_general.36, bf16[256,256]{1,0:T(8,128)(2,1)S(1)} %fusion.21, bf16[256,256]{1,0:T(8,128)(2,1)S(1)} %copy.87, bf16[256,512]{1,0:T(8,128)(2,1)S(1)} %copy-done.5), kind=kOutput, calls=%fused_computation.36 | convolution fusion | flops 2820145152 | bytes 17039360 | tf_op jit(solution)/shard_map/dot_general | solution.py:206
  321.1 3.2 collective-permute-done.13
  329.5 15.9 %collective-permute-done.14 = bf16[256,1344]{0,1:T(8,128)(2,1)S(1)} collective-permute-done((bf16[256,1344]{0,1:T(8,128)(2,1)}, bf16[256,1344]{0,1:T(8,128)(2,1)S(1)}, u32[]{:S(2)}, u32[]{:S(2)}) %collective-permute-start.14) | collective-permute-done | bytes 688160 | tf_op jit(solution)/shard_map/ppermute | solution.py:40
  (104 shorter events, 57.4 us)
Async XLA Ops:
  7.2 170.8 %all-gather.4.cloned.1.call-start = ((), (), s32[]{:S(2)}) async-start(), calls=%async_computation | async-start | bytes 11714560 | tf_op jit(solution)/shard_map/all_gather | solution.py:148
  10.2 7.8 %collective-permute-start.3 = (f32[]{:T(128)}, f32[]{:T(128)}, u32[]{:S(2)}, u32[]{:S(2)}) collective-permute-start(f32[]{:T(128)} %fusion.24), channel_id=1, source_target_pairs={{0,4},{4,0},{8,12},{12,8},{16,20},{20,16},{24,28},{28,24},{32,36},... | collective-permute-start | bytes 20 | tf_op jit(solution)/shard_map/ppermute | solution.py:23
  13.6 36.4 %copy-start.11 = (f32[256]{0:T(256)S(1)}, f32[256]{0:T(256)}, u32[]{:S(2)}) copy-start(f32[256]{0:T(256)} %param.17) | copy-start | bytes 3076
  13.6 36.4 %copy-start.12 = (s32[256]{0:T(256)S(1)}, s32[256]{0:T(256)}, u32[]{:S(2)}) copy-start(s32[256]{0:T(256)} %param.18) | copy-start | bytes 3076
  19.3 4.9 %collective-permute-start.4 = (f32[]{:T(128)}, f32[]{:T(128)}, u32[]{:S(2)}, u32[]{:S(2)}) collective-permute-start(f32[]{:T(128)} %add.138), channel_id=1, source_target_pairs={{0,8},{4,12},{8,0},{12,4},{16,24},{20,28},{24,16},{28,20},{32,40},... | collective-permute-start | bytes 20 | tf_op jit(solution)/shard_map/ppermute | solution.py:23
  24.9 8.4 %collective-permute-start.5 = (f32[]{:T(128)}, f32[]{:T(128)}, u32[]{:S(2)}, u32[]{:S(2)}) collective-permute-start(f32[]{:T(128)} %add.139), channel_id=1, source_target_pairs={{0,16},{4,20},{8,24},{12,28},{16,0},{20,4},{24,8},{28,12},{32,48},... | collective-permute-start | bytes 20 | tf_op jit(solution)/shard_map/ppermute | solution.py:23
  34.0 5.1 %collective-permute-start.6 = (f32[]{:T(128)}, f32[]{:T(128)}, u32[]{:S(2)}, u32[]{:S(2)}) collective-permute-start(f32[]{:T(128)} %add.140), channel_id=1, source_target_pairs={{0,32},{4,36},{8,40},{12,44},{16,48},{20,52},{24,56},{28,60},{32,0... | collective-permute-start | bytes 20 | tf_op jit(solution)/shard_map/ppermute | solution.py:23
  39.8 3.6 %collective-permute-start.7 = (f32[]{:T(128)}, f32[]{:T(128)}, u32[]{:S(2)}, u32[]{:S(2)}) collective-permute-start(f32[]{:T(128)} %add.141), channel_id=1, source_target_pairs={{0,64},{4,68},{8,72},{12,76},{16,80},{20,84},{24,88},{28,92},{32,9... | collective-permute-start | bytes 20 | tf_op jit(solution)/shard_map/ppermute | solution.py:23
  44.1 5.1 %collective-permute-start.8 = (f32[]{:T(128)}, f32[]{:T(128)}, u32[]{:S(2)}, u32[]{:S(2)}) collective-permute-start(f32[]{:T(128)} %add.142), channel_id=1, source_target_pairs={{0,128},{4,132},{8,136},{12,140},{16,144},{20,148},{24,152},{28,15... | collective-permute-start | bytes 20 | tf_op jit(solution)/shard_map/ppermute | solution.py:23
  50.0 135.0 %copy-start.9 = (f32[128]{0:T(128)S(1)}, f32[128]{0:T(128)}, u32[]{:S(2)}) copy-start(f32[128]{0:T(128)} %param.15) | copy-start | bytes 1540
  178.0 15.8 %copy-start.3 = (bf16[256,512]{1,0:T(8,128)(2,1)S(1)}, bf16[256,512]{1,0:T(8,128)(2,1)}, u32[]{:S(2)}) copy-start(bf16[256,512]{1,0:T(8,128)(2,1)} %param.19) | copy-start | bytes 786436
  185.0 29.1 %copy-start.7 = (f32[128]{0:T(128)S(1)}, f32[128]{0:T(128)}, u32[]{:S(2)}) copy-start(f32[128]{0:T(128)} %param.14) | copy-start | bytes 1540
  185.9 21.4 %collective-permute-start = (bf16[2,256,256]{1,2,0:T(8,128)(2,1)}, bf16[2,256,256]{1,2,0:T(8,128)(2,1)S(1)}, u32[]{:S(2)}, u32[]{:S(2)}) collective-permute-start(bf16[2,256,256]{1,2,0:T(8,128)(2,1)} %pad_maximum_fusion.2), channel_id=1, source_target_pairs={{0,8},{4,12},{8,16},{12,20},{16,24},{20,28},{24,32},{28,36},{32,40... | collective-permute-start | bytes 786440 | tf_op jit(solution)/shard_map/ppermute | solution.py:16
  191.2 16.1 %collective-permute-start.1 = (bf16[2,256,256]{1,2,0:T(8,128)(2,1)}, bf16[2,256,256]{1,2,0:T(8,128)(2,1)}, u32[]{:S(2)}, u32[]{:S(2)}) collective-permute-start(bf16[2,256,256]{1,2,0:T(8,128)(2,1)} %pad_maximum_fusion.2), channel_id=1, source_target_pairs={{0,4},{4,8},{8,12},{12,16},{16,20},{20,24},{24,28},{28,32},{32,36}... | collective-permute-start | bytes 786440 | tf_op jit(solution)/shard_map/ppermute | solution.py:16
  209.2 31.8 %collective-permute-start.2 = (bf16[2,512,256]{1,2,0:T(8,128)(2,1)}, bf16[2,512,256]{1,2,0:T(8,128)(2,1)}, u32[]{:S(2)}, u32[]{:S(2)}) collective-permute-start(bf16[2,512,256]{1,2,0:T(8,128)(2,1)} %pad_maximum_fusion.1), channel_id=1, source_target_pairs={{0,8},{4,12},{8,16},{12,20},{16,24},{20,28},{24,32},{28,36},{32,40... | collective-permute-start | bytes 1572872 | tf_op jit(solution)/shard_map/ppermute | solution.py:16
  230.8 11.6 %copy-start.13 = (s32[2,2]{1,0:T(2,128)S(1)}, s32[2,2]{1,0:T(2,128)}, u32[]{:S(2)}) copy-start(s32[2,2]{1,0:T(2,128)} %lt.36) | copy-start | bytes 52
  263.1 17.0 %copy-start.8 = (f32[128]{0:T(128)S(1)}, f32[128]{0:T(128)}, u32[]{:S(2)}) copy-start(f32[128]{0:T(128)} %param.14) | copy-start | bytes 1540
  265.6 21.5 %collective-permute-start.10 = (bf16[2,256,256]{2,1,0:T(8,128)(2,1)}, bf16[2,256,256]{2,1,0:T(8,128)(2,1)S(1)}, u32[]{:S(2)}, u32[]{:S(2)}) collective-permute-start(bf16[2,256,256]{2,1,0:T(8,128)(2,1)} %get-tuple-element.11), channel_id=1, source_target_pairs={{8,0},{12,4},{16,8},{20,12},{24,16},{28,20},{32,24},{36,28},{40,32... | collective-permute-start | bytes 786440 | tf_op jit(solution)/shard_map/ppermute | solution.py:16
  268.2 24.3 %collective-permute-start.11 = (bf16[2,256,256]{2,1,0:T(8,128)(2,1)}, bf16[2,256,256]{2,1,0:T(8,128)(2,1)}, u32[]{:S(2)}, u32[]{:S(2)}) collective-permute-start(bf16[2,256,256]{2,1,0:T(8,128)(2,1)} %get-tuple-element.10), channel_id=1, source_target_pairs={{12,0},{16,4},{20,8},{24,12},{28,16},{32,20},{36,24},{40,28},{44,3... | collective-permute-start | bytes 786440 | tf_op jit(solution)/shard_map/ppermute | solution.py:16
  272.7 31.9 %collective-permute-start.12 = (bf16[2,256,256]{2,1,0:T(8,128)(2,1)}, bf16[2,256,256]{2,1,0:T(8,128)(2,1)}, u32[]{:S(2)}, u32[]{:S(2)}) collective-permute-start(bf16[2,256,256]{2,1,0:T(8,128)(2,1)} %get-tuple-element.9), channel_id=1, source_target_pairs={{16,0},{20,4},{24,8},{28,12},{32,16},{36,20},{40,24},{44,28},{48,3... | collective-permute-start | bytes 786440 | tf_op jit(solution)/shard_map/ppermute | solution.py:16
  278.0 32.2 %collective-permute-start.9 = (bf16[2,256,256]{2,1,0:T(8,128)(2,1)}, bf16[2,256,256]{2,1,0:T(8,128)(2,1)}, u32[]{:S(2)}, u32[]{:S(2)}) collective-permute-start(bf16[2,256,256]{2,1,0:T(8,128)(2,1)} %get-tuple-element.8), channel_id=1, source_target_pairs={{4,0},{8,4},{12,8},{16,12},{20,16},{24,20},{28,24},{32,28},{36,32}... | collective-permute-start | bytes 786440 | tf_op jit(solution)/shard_map/ppermute | solution.py:16
  281.4 30.4 %copy-start.10 = (f32[128]{0:T(128)S(1)}, f32[128]{0:T(128)}, u32[]{:S(2)}) copy-start(f32[128]{0:T(128)} %param.15) | copy-start | bytes 1540
  321.0 3.3 collective-permute-start.13
  327.7 17.7 %collective-permute-start.14 = (bf16[256,1344]{0,1:T(8,128)(2,1)}, bf16[256,1344]{0,1:T(8,128)(2,1)S(1)}, u32[]{:S(2)}, u32[]{:S(2)}) collective-permute-start(bf16[256,1344]{0,1:T(8,128)(2,1)} %fusion.7), channel_id=1, source_target_pairs={{0,2},{1,3},{2,0},{3,1},{4,6},{5,7},{6,4},{7,5},{8,10},{9,11},{10,... | collective-permute-start | bytes 2064392 | tf_op jit(solution)/shard_map/ppermute | solution.py:40
  (7 other events, 38.8 us)
Sparse Core Ops, SparseCore 0:
  12.2 165.7 all-gather.3

commit v7 on v5

--- a/solution.py
+++ b/solution.py
@@ -26,9 +26,8 @@
 
 
 def head_scatter_sum(partial, axis):
-    rows, width = partial.shape
     index = lax.axis_index(axis)
-    parts = partial.reshape(rows, 2, 2, width // 4)
+    parts = partial
     low_bit = index % 2
     high_bit = index // 2
     kept = lax.dynamic_index_in_dim(parts, low_bit, axis=2, keepdims=False)
@@ -149,12 +148,14 @@
         jnp.concatenate([q_weight, k_weight, v_weight], axis=1), "seq", axis=0, tiled=False
     )
     token_blocks = tokens.reshape(tok_rows, seq_count, row_block)
-    all_linear = jnp.einsum(
-        "tsr,src->tc", token_blocks, joined_rows, preferred_element_type=jnp.float32
-    )
-    q_linear = all_linear[:, :q_cols]
-    k_linear = all_linear[:, q_cols : q_cols + k_cols]
-    v_linear = all_linear[:, q_cols + k_cols :]
+    kv_linear = jnp.einsum(
+        "tsr,src->tc", token_blocks, joined_rows[:, :, q_cols:], preferred_element_type=jnp.float32
+    )
+    q_linear = jnp.einsum(
+        "tsr,src->tc", token_blocks, joined_rows[:, :, :q_cols], preferred_element_type=jnp.float32
+    )
+    k_linear = kv_linear[:, :k_cols]
+    v_linear = kv_linear[:, k_cols:]
     q_linear = q_linear.reshape(tok_rows, q_heads, head_width)
     k_linear = k_linear.reshape(tok_rows, kv_heads, head_width)
     values = v_linear.astype(jnp.bfloat16)
@@ -217,13 +218,18 @@
     dq_lin = back_query(dquery)[0].astype(jnp.bfloat16).reshape(tok_rows, q_heads * head_width)
     dk_lin = back_key(key_total)[0].astype(jnp.bfloat16).reshape(tok_rows, kv_heads * head_width)
     dv_lin = local_grads[1].astype(jnp.bfloat16)
-    joined_grad = jnp.concatenate([dq_lin, dk_lin, dv_lin], axis=1)
-    partial_grad = lax.dot_general(
-        joined_grad,
-        joined_rows.reshape(seq_count * row_block, joined_rows.shape[-1]),
+    flat_rows = joined_rows.reshape(seq_count * row_block, joined_rows.shape[-1])
+    query_part = lax.dot_general(
+        dq_lin, flat_rows[:, :q_cols], contract, preferred_element_type=jnp.float32
+    )
+    key_value_part = lax.dot_general(
+        jnp.concatenate([dk_lin, dv_lin], axis=1),
+        flat_rows[:, q_cols:],
         contract,
         preferred_element_type=jnp.float32,
     )
+    quarter_shape = (tok_rows, 2, 2, query_part.shape[1] // 4)
+    partial_grad = query_part.reshape(quarter_shape) + key_value_part.reshape(quarter_shape)
     grad_tokens = head_scatter_sum(partial_grad, "head")
     return (attended, grad_tokens)
 

time: 353 us -> 336 us (0.952)
  matrix products: 29.4 us -> 21.4 us
  local copies, waits for them, and re-layouts: 34.1 us -> 29 us
  other arithmetic: 18.7 us -> 13.8 us
    dot_general x1 -> x0, local copies, waits for them, and re-layouts: 14.2 us -> none  [body(): lax.dot_general(joined_grad, joined_rows.reshape(seq_count * row_block, j...]
    unnamed x46 -> x39, local copies, waits for them, and re-layouts: 8.26 us -> 21.6 us
    ppermute x6, waiting for transfers between devices: 57 us -> 52.9 us  [passed_along(): return lax.ppermute(block, axis, route)]
    dot_general x2 -> x4, matrix products: 12.9 us -> 10.2 us  [the longest x1 5.33 us: body(): jnp.einsum('tsr,src->tc', token_blocks, joined_rows[:, :, q_cols:], prefe...]
where the time goes in v7:
time: 336 us; the launch traced here: 332 us
  waiting for transfers between devices  206 us (61%)
  starting transfers between devices  43.4 us (13%)
  local copies, waits for them, and re-layouts  29 us (9%)
  matrix products  21.4 us (6%)
  between operations  18.7 us (6%)
  other arithmetic  13.8 us (4%)
    all_gather x1, waiting for transfers between devices, body(): lax.all_gather(jnp.concatenate([q_weight, k_weight, v_weight], axis=1), '...  128 us
    ppermute x6, waiting for transfers between devices, passed_along(): return lax.ppermute(block, axis, route)  52.9 us
    ppermute x6, starting transfers between devices, butterfly_sum(): lax.ppermute(value, axis, [(i, i ^ step) for i in range(size)])  22.6 us
    unnamed x39, local copies, waits for them, and re-layouts  21.6 us
    ppermute x6, starting transfers between devices, passed_along(): return lax.ppermute(block, axis, route)  20.7 us
    ppermute x1, waiting for transfers between devices, head_scatter_sum(): lax.ppermute(sent.astype(jnp.bfloat16), axis, [(i, i ^ 2) for i in range(...  15.9 us
  transfers between devices with their start and end apart: 15, of which 13 were waited for; matrix products, arithmetic and copies ran while one was open for 9% of the time, Pallas kernels for 0%

profile of v7, /device:TPU:38, one launch (start us, length us, event | category | flops | bytes accessed | tf_op | source)
XLA Modules:
  0.0 331.9 jit_solution(10263695443805138219)
XLA Ops:
  10.3 3.3 copy.43
  18.1 4.7 %collective-permute-start.4 = (f32[]{:T(128)}, f32[]{:T(128)}, u32[]{:S(2)}, u32[]{:S(2)}) collective-permute-start(f32[]{:T(128)} %add.138), channel_id=1, source_target_pairs={{0,8},{4,12},{8,0},{12,4},{16,24},{20,28},{24,16},{28,20},{32,40},... | collective-permute-start | bytes 20 | tf_op jit(solution)/shard_map/ppermute | solution.py:23
  23.7 8.2 %collective-permute-start.5 = (f32[]{:T(128)}, f32[]{:T(128)}, u32[]{:S(2)}, u32[]{:S(2)}) collective-permute-start(f32[]{:T(128)} %add.139), channel_id=1, source_target_pairs={{0,16},{4,20},{8,24},{12,28},{16,0},{20,4},{24,8},{28,12},{32,48},... | collective-permute-start | bytes 20 | tf_op jit(solution)/shard_map/ppermute | solution.py:23
  32.9 4.6 %collective-permute-start.6 = (f32[]{:T(128)}, f32[]{:T(128)}, u32[]{:S(2)}, u32[]{:S(2)}) collective-permute-start(f32[]{:T(128)} %add.140), channel_id=1, source_target_pairs={{0,32},{4,36},{8,40},{12,44},{16,48},{20,52},{24,56},{28,60},{32,0... | collective-permute-start | bytes 20 | tf_op jit(solution)/shard_map/ppermute | solution.py:23
  43.0 2.8 collective-permute-start.8
  45.8 2.5 collective-permute-done.8
  49.9 128.1 %all-gather.4.cloned.1.call-done = bf16[64,84,1024]{2,1,0:T(8,128)(2,1)} async-done(((bf16[1,84,1024]{2,1,0:T(8,128)(2,1)}), bf16[64,84,1024]{2,1,0:T(8,128)(2,1)}) %all-gather.4.cloned.1.call-update) | async-done | bytes 11010064 | tf_op jit(solution)/shard_map/all_gather | solution.py:147
  178.1 5.3 %fusion.12 = f32[256,512]{0,1:T(8,128)S(1)} fusion(bf16[256,64,84]{0,2,1:T(8,128)(2,1)} %reshape.223, bf16[64,84,1024]{2,1,0:T(8,128)(2,1)} %all-gather.4.cloned.1.call-done), kind=kOutput, calls=%fused_computation.29 | convolution fusion | flops 1409286144 | bytes 9175040 | tf_op jit(solution)/shard_map/tsr,src->tc/dot_general | solution.py:151
  183.7 5.5 %collective-permute-start = (bf16[2,256,256]{1,2,0:T(8,128)(2,1)S(1)}, bf16[2,256,256]{1,2,0:T(8,128)(2,1)S(1)}, u32[]{:S(2)}, u32[]{:S(2)}) collective-permute-start(bf16[2,256,256]{1,2,0:T(8,128)(2,1)S(1)} %pad_maximum_fusion.2), channel_id=1, source_target_pairs={{0,8},{4,12},{8,16},{12,20},{16,24},{20,28},{24,32},{28,36},{32,40... | collective-permute-start | bytes 786440 | tf_op jit(solution)/shard_map/ppermute | solution.py:16
  189.2 2.6 collective-permute-start.1
  193.6 11.5 %collective-permute-done = bf16[2,256,256]{1,2,0:T(8,128)(2,1)S(1)} collective-permute-done((bf16[2,256,256]{1,2,0:T(8,128)(2,1)S(1)}, bf16[2,256,256]{1,2,0:T(8,128)(2,1)S(1)}, u32[]{:S(2)}, u32[]{:S(2)}) %collective-permute-start) | collective-permute-done | bytes 262176 | tf_op jit(solution)/shard_map/ppermute | solution.py:16
  206.0 4.9 %collective-permute-start.2 = (bf16[2,512,256]{1,2,0:T(8,128)(2,1)}, bf16[2,512,256]{1,2,0:T(8,128)(2,1)}, u32[]{:S(2)}, u32[]{:S(2)}) collective-permute-start(bf16[2,512,256]{1,2,0:T(8,128)(2,1)} %pad_maximum_fusion.1), channel_id=1, source_target_pairs={{0,8},{4,12},{8,16},{12,20},{16,24},{20,28},{24,32},{28,36},{32,40... | collective-permute-start | bytes 1572872 | tf_op jit(solution)/shard_map/ppermute | solution.py:16
  213.7 14.0 %reshape.235 = bf16[5376,1024]{1,0:T(8,128)(2,1)} reshape(bf16[64,84,1024]{2,1,0:T(8,128)(2,1)} %all-gather.4.cloned.1.call-done) | data formatting | bytes 22020096
  227.7 10.0 %collective-permute-done.2 = bf16[2,512,256]{1,2,0:T(8,128)(2,1)} collective-permute-done((bf16[2,512,256]{1,2,0:T(8,128)(2,1)}, bf16[2,512,256]{1,2,0:T(8,128)(2,1)}, u32[]{:S(2)}, u32[]{:S(2)}) %collective-permute-start.2) | collective-permute-done | bytes 524320 | tf_op jit(solution)/shard_map/ppermute | solution.py:16
  243.4 2.6 multiply_reduce_fusion.1
  247.9 3.1 fusion.7
  252.2 2.8 collective-permute-start.9
  255.8 22.7 %collective-permute-done.9 = bf16[2,512,256]{1,2,0:T(8,128)(2,1)S(1)} collective-permute-done((bf16[2,512,256]{1,2,0:T(8,128)(2,1)S(1)}, bf16[2,512,256]{1,2,0:T(8,128)(2,1)S(1)}, u32[]{:S(2)}, u32[]{:S(2)}) %collective-permute-start.9) | collective-permute-done | bytes 524320 | tf_op jit(solution)/shard_map/ppermute | solution.py:16
  278.6 2.8 collective-permute-start.10
  283.8 7.3 %collective-permute-done.10 = bf16[2,256,256]{1,2,0:T(8,128)(2,1)S(1)} collective-permute-done((bf16[2,256,256]{1,2,0:T(8,128)(2,1)S(1)}, bf16[2,256,256]{1,2,0:T(8,128)(2,1)S(1)}, u32[]{:S(2)}, u32[]{:S(2)}) %collective-permute-start.10) | collective-permute-done | bytes 262176 | tf_op jit(solution)/shard_map/ppermute | solution.py:16
  297.1 2.4 copy-done
  299.7 3.2 collective-permute-done.12
  303.0 2.5 bitcast_add_fusion
  308.2 15.9 %collective-permute-done.13 = bf16[256,1344]{0,1:T(8,128)(2,1)S(1)} collective-permute-done((bf16[256,1344]{0,1:T(8,128)(2,1)}, bf16[256,1344]{0,1:T(8,128)(2,1)S(1)}, u32[]{:S(2)}, u32[]{:S(2)}) %collective-permute-start.13) | collective-permute-done | bytes 688160 | tf_op jit(solution)/shard_map/ppermute | solution.py:39
  (109 shorter events, 39.8 us)
Async XLA Ops:
  7.2 170.9 %all-gather.4.cloned.1.call-start = ((), (), s32[]{:S(2)}) async-start(), calls=%async_computation | async-start | bytes 11714560 | tf_op jit(solution)/shard_map/all_gather | solution.py:147
  10.2 6.7 %collective-permute-start.3 = (f32[]{:T(128)}, f32[]{:T(128)}, u32[]{:S(2)}, u32[]{:S(2)}) collective-permute-start(f32[]{:T(128)} %fusion.32), channel_id=1, source_target_pairs={{0,4},{4,0},{8,12},{12,8},{16,20},{20,16},{24,28},{28,24},{32,36},... | collective-permute-start | bytes 20 | tf_op jit(solution)/shard_map/ppermute | solution.py:23
  13.6 35.3 %copy-start.12 = (f32[256]{0:T(256)S(1)}, f32[256]{0:T(256)}, u32[]{:S(2)}) copy-start(f32[256]{0:T(256)} %param.17) | copy-start | bytes 3076
  13.6 35.3 %copy-start.13 = (s32[256]{0:T(256)S(1)}, s32[256]{0:T(256)}, u32[]{:S(2)}) copy-start(s32[256]{0:T(256)} %param.18) | copy-start | bytes 3076
  13.6 35.3 %copy-start.8 = (bf16[256,512]{1,0:T(8,128)(2,1)S(1)}, bf16[256,512]{1,0:T(8,128)(2,1)}, u32[]{:S(2)}) copy-start(bf16[256,512]{1,0:T(8,128)(2,1)} %param.19) | copy-start | bytes 786436
  18.1 5.0 %collective-permute-start.4 = (f32[]{:T(128)}, f32[]{:T(128)}, u32[]{:S(2)}, u32[]{:S(2)}) collective-permute-start(f32[]{:T(128)} %add.138), channel_id=1, source_target_pairs={{0,8},{4,12},{8,0},{12,4},{16,24},{20,28},{24,16},{28,20},{32,40},... | collective-permute-start | bytes 20 | tf_op jit(solution)/shard_map/ppermute | solution.py:23
  23.7 8.6 %collective-permute-start.5 = (f32[]{:T(128)}, f32[]{:T(128)}, u32[]{:S(2)}, u32[]{:S(2)}) collective-permute-start(f32[]{:T(128)} %add.139), channel_id=1, source_target_pairs={{0,16},{4,20},{8,24},{12,28},{16,0},{20,4},{24,8},{28,12},{32,48},... | collective-permute-start | bytes 20 | tf_op jit(solution)/shard_map/ppermute | solution.py:23
  32.9 5.3 %collective-permute-start.6 = (f32[]{:T(128)}, f32[]{:T(128)}, u32[]{:S(2)}, u32[]{:S(2)}) collective-permute-start(f32[]{:T(128)} %add.140), channel_id=1, source_target_pairs={{0,32},{4,36},{8,40},{12,44},{16,48},{20,52},{24,56},{28,60},{32,0... | collective-permute-start | bytes 20 | tf_op jit(solution)/shard_map/ppermute | solution.py:23
  38.7 3.8 %collective-permute-start.7 = (f32[]{:T(128)}, f32[]{:T(128)}, u32[]{:S(2)}, u32[]{:S(2)}) collective-permute-start(f32[]{:T(128)} %add.141), channel_id=1, source_target_pairs={{0,64},{4,68},{8,72},{12,76},{16,80},{20,84},{24,88},{28,92},{32,9... | collective-permute-start | bytes 20 | tf_op jit(solution)/shard_map/ppermute | solution.py:23
  43.0 5.3 %collective-permute-start.8 = (f32[]{:T(128)}, f32[]{:T(128)}, u32[]{:S(2)}, u32[]{:S(2)}) collective-permute-start(f32[]{:T(128)} %add.142), channel_id=1, source_target_pairs={{0,128},{4,132},{8,136},{12,140},{16,144},{20,148},{24,152},{28,15... | collective-permute-start | bytes 20 | tf_op jit(solution)/shard_map/ppermute | solution.py:23
  49.9 133.6 %copy-start.11 = (f32[128]{0:T(128)S(1)}, f32[128]{0:T(128)}, u32[]{:S(2)}) copy-start(f32[128]{0:T(128)} %param.15) | copy-start | bytes 1540
  178.1 13.8 %copy-start.2 = (bf16[256,64,84]{0,2,1:T(8,128)(2,1)S(1)}, bf16[256,64,84]{0,2,1:T(8,128)(2,1)}, u32[]{:S(2)}) copy-start(bf16[256,64,84]{0,2,1:T(8,128)(2,1)} %reshape.223) | copy-start | bytes 8257540
  183.7 27.2 %copy-start.10 = (f32[128]{0:T(128)S(1)}, f32[128]{0:T(128)}, u32[]{:S(2)}) copy-start(f32[128]{0:T(128)} %param.14) | copy-start | bytes 1540
  183.7 21.4 %collective-permute-start = (bf16[2,256,256]{1,2,0:T(8,128)(2,1)S(1)}, bf16[2,256,256]{1,2,0:T(8,128)(2,1)S(1)}, u32[]{:S(2)}, u32[]{:S(2)}) collective-permute-start(bf16[2,256,256]{1,2,0:T(8,128)(2,1)S(1)} %pad_maximum_fusion.2), channel_id=1, source_target_pairs={{0,8},{4,12},{8,16},{12,20},{16,24},{20,28},{24,32},{28,36},{32,40... | collective-permute-start | bytes 786440 | tf_op jit(solution)/shard_map/ppermute | solution.py:16
  189.2 15.9 %collective-permute-start.1 = (bf16[2,256,256]{1,2,0:T(8,128)(2,1)S(1)}, bf16[2,256,256]{1,2,0:T(8,128)(2,1)S(1)}, u32[]{:S(2)}, u32[]{:S(2)}) collective-permute-start(bf16[2,256,256]{1,2,0:T(8,128)(2,1)S(1)} %pad_maximum_fusion.2), channel_id=1, source_target_pairs={{0,4},{4,8},{8,12},{12,16},{16,20},{20,24},{24,28},{28,32},{32,36}... | collective-permute-start | bytes 786440 | tf_op jit(solution)/shard_map/ppermute | solution.py:16
  206.0 31.8 %collective-permute-start.2 = (bf16[2,512,256]{1,2,0:T(8,128)(2,1)}, bf16[2,512,256]{1,2,0:T(8,128)(2,1)}, u32[]{:S(2)}, u32[]{:S(2)}) collective-permute-start(bf16[2,512,256]{1,2,0:T(8,128)(2,1)} %pad_maximum_fusion.1), channel_id=1, source_target_pairs={{0,8},{4,12},{8,16},{12,20},{16,24},{20,28},{24,32},{28,36},{32,40... | collective-permute-start | bytes 1572872 | tf_op jit(solution)/shard_map/ppermute | solution.py:16
  251.0 41.8 %slice-start = ((s8[11010048]{0:T(1024)(128)(4,1)}), s8[4194304]{0:T(1024)(128)(4,1)S(1)}, s32[]{:S(2)}) async-start(s8[11010048]{0:T(1024)(128)(4,1)} %bitcast.102), calls=%async_computation.1 | async-start | bytes 8388608
  252.2 40.7 %slice-start.1 = ((s8[11010048]{0:T(1024)(128)(4,1)}), s8[4194304]{0:T(1024)(128)(4,1)S(1)}, s32[]{:S(2)}) async-start(s8[11010048]{0:T(1024)(128)(4,1)} %bitcast.102), calls=%async_computation.2 | async-start | bytes 8388608
  252.2 26.3 %collective-permute-start.9 = (bf16[2,512,256]{1,2,0:T(8,128)(2,1)S(1)}, bf16[2,512,256]{1,2,0:T(8,128)(2,1)S(1)}, u32[]{:S(2)}, u32[]{:S(2)}) collective-permute-start(bf16[2,512,256]{1,2,0:T(8,128)(2,1)S(1)} %fusion.18), channel_id=1, source_target_pairs={{8,0},{12,4},{16,8},{20,12},{24,16},{28,20},{32,24},{36,28},{40,32... | collective-permute-start | bytes 1572872 | tf_op jit(solution)/shard_map/ppermute | solution.py:16
  278.6 14.3 %slice-start.2 = ((s8[11010048]{0:T(1024)(128)(4,1)}), s8[2621440]{0:T(1024)(128)(4,1)S(1)}, s32[]{:S(2)}) async-start(s8[11010048]{0:T(1024)(128)(4,1)} %bitcast.102), calls=%async_computation.3 | async-start | bytes 5242880
  278.6 12.4 %collective-permute-start.10 = (bf16[2,256,256]{1,2,0:T(8,128)(2,1)S(1)}, bf16[2,256,256]{1,2,0:T(8,128)(2,1)S(1)}, u32[]{:S(2)}, u32[]{:S(2)}) collective-permute-start(bf16[2,256,256]{1,2,0:T(8,128)(2,1)S(1)} %get-tuple-element.14), channel_id=1, source_target_pairs={{8,0},{12,4},{16,8},{20,12},{24,16},{28,20},{32,24},{36,28},{40,32... | collective-permute-start | bytes 786440 | tf_op jit(solution)/shard_map/ppermute | solution.py:16
  281.4 11.0 %collective-permute-start.11 = (bf16[2,256,256]{1,2,0:T(8,128)(2,1)S(1)}, bf16[2,256,256]{1,2,0:T(8,128)(2,1)S(1)}, u32[]{:S(2)}, u32[]{:S(2)}) collective-permute-start(bf16[2,256,256]{1,2,0:T(8,128)(2,1)S(1)} %get-tuple-element.15), channel_id=1, source_target_pairs={{4,0},{8,4},{12,8},{16,12},{20,16},{24,20},{28,24},{32,28},{36,32}... | collective-permute-start | bytes 786440 | tf_op jit(solution)/shard_map/ppermute | solution.py:16
  299.6 3.3 %collective-permute-start.12 = (bf16[256,2,1344]{0,2,1:T(8,128)(2,1)S(1)}, bf16[256,2,1344]{0,2,1:T(8,128)(2,1)}, u32[]{:S(2)}, u32[]{:S(2)}) collective-permute-start(bf16[256,2,1344]{0,2,1:T(8,128)(2,1)S(1)} %fusion.10), channel_id=1, source_target_pairs={{0,1},{1,0},{2,3},{3,2},{4,5},{5,4},{6,7},{7,6},{8,9},{9,8},{10,11... | collective-permute-start | bytes 4128776 | tf_op jit(solution)/shard_map/ppermute | solution.py:35
  306.4 17.7 %collective-permute-start.13 = (bf16[256,1344]{0,1:T(8,128)(2,1)}, bf16[256,1344]{0,1:T(8,128)(2,1)S(1)}, u32[]{:S(2)}, u32[]{:S(2)}) collective-permute-start(bf16[256,1344]{0,1:T(8,128)(2,1)} %fusion.19), channel_id=1, source_target_pairs={{0,2},{1,3},{2,0},{3,1},{4,6},{5,7},{6,4},{7,5},{8,10},{9,11},{10,... | collective-permute-start | bytes 2064392 | tf_op jit(solution)/shard_map/ppermute | solution.py:39
  (10 other events, 68.0 us)
Sparse Core Ops, SparseCore 0:
  12.2 165.8 all-gather.3

commit v8 on v7

--- a/solution.py
+++ b/solution.py
@@ -164,10 +164,12 @@
     k_rot = norm_rotate(k_linear, k_gain, cosine, sine_table).astype(jnp.bfloat16)
     stacked = jnp.stack([k_rot.reshape(tok_rows, kv_heads * head_width), values])
     if pred_count == 4:
-        near_one = passed_along(stacked, "seq", 1)
         near_two = passed_along(stacked, "seq", 2)
-        far_pair = passed_along(jnp.concatenate([near_two, near_one], axis=1), "seq", 2)
-        extended = jnp.concatenate([far_pair, near_two, near_one, stacked], axis=1)
+        odd_pair = passed_along(jnp.concatenate([near_two, stacked], axis=1), "seq", 1)
+        far_one = passed_along(near_two, "seq", 2)
+        extended = jnp.concatenate(
+            [far_one, odd_pair[:, :tok_rows], near_two, odd_pair[:, tok_rows:], stacked], axis=1
+        )
     else:
         received = []
         for offset in range(1, pred_count + 1):
@@ -186,18 +188,22 @@
     )
     local_grads = stacked_grads[:, pred_count * tok_rows :]
     if pred_count == 4:
+        odd_back = passed_along(
+            jnp.concatenate(
+                [stacked_grads[:, tok_rows : 2 * tok_rows], stacked_grads[:, 3 * tok_rows : 4 * tok_rows]],
+                axis=1,
+            ).astype(jnp.bfloat16),
+            "seq",
+            -1,
+        ).astype(jnp.float32)
         far_back = passed_along(
-            stacked_grads[:, : 2 * tok_rows].astype(jnp.bfloat16), "seq", -2
+            stacked_grads[:, :tok_rows].astype(jnp.bfloat16), "seq", -2
         ).astype(jnp.float32)
-        near_sums = stacked_grads[:, 2 * tok_rows : 4 * tok_rows] + far_back
+        middle_sum = stacked_grads[:, 2 * tok_rows : 3 * tok_rows] + odd_back[:, :tok_rows] + far_back
         local_grads = (
             local_grads
-            + passed_along(near_sums[:, :tok_rows].astype(jnp.bfloat16), "seq", -2).astype(
-                jnp.float32
-            )
-            + passed_along(near_sums[:, tok_rows:].astype(jnp.bfloat16), "seq", -1).astype(
-                jnp.float32
-            )
+            + odd_back[:, tok_rows:]
+            + passed_along(middle_sum.astype(jnp.bfloat16), "seq", -2).astype(jnp.float32)
         )
     else:
         for offset in range(1, pred_count + 1):

time: 336 us -> 334 us (level)
  waiting for transfers between devices: 206 us -> 199 us
  local copies, waits for them, and re-layouts: 29 us -> 32.7 us
    ppermute x6, waiting for transfers between devices: 52.9 us -> 47.1 us  [passed_along(): return lax.ppermute(block, axis, route)]
    unnamed x39 -> x35, local copies, waits for them, and re-layouts: 21.6 us -> 25.4 us
  transfers between devices with their start and end apart: 15 -> 15, of which waited for: 13 -> 12; matrix products, arithmetic and copies ran while one was open for 9% -> 9% of each run, Pallas kernels for 0% -> 0%
where the time goes in v8:
time: 334 us; the launch traced here: 331 us
  waiting for transfers between devices  199 us (60%)
  starting transfers between devices  44.5 us (13%)
  local copies, waits for them, and re-layouts  32.7 us (10%)
  matrix products  21.4 us (6%)
  between operations  19.1 us (6%)
  other arithmetic  13.9 us (4%)
    all_gather x1, waiting for transfers between devices, body(): lax.all_gather(jnp.concatenate([q_weight, k_weight, v_weight], axis=1), '...  128 us
    ppermute x6, waiting for transfers between devices, passed_along(): return lax.ppermute(block, axis, route)  47.1 us
    unnamed x35, local copies, waits for them, and re-layouts  25.4 us
    ppermute x6, starting transfers between devices, butterfly_sum(): lax.ppermute(value, axis, [(i, i ^ step) for i in range(size)])  22.6 us
    ppermute x6, starting transfers between devices, passed_along(): return lax.ppermute(block, axis, route)  21.8 us
    ppermute x1, waiting for transfers between devices, head_scatter_sum(): lax.ppermute(sent.astype(jnp.bfloat16), axis, [(i, i ^ 2) for i in range(...  15.9 us
  transfers between devices with their start and end apart: 15, of which 12 were waited for; matrix products, arithmetic and copies ran while one was open for 9% of the time, Pallas kernels for 0%

profile of v8, /device:TPU:38, one launch (start us, length us, event | category | flops | bytes accessed | tf_op | source)
XLA Modules:
  0.0 331.0 jit_solution(11957134696743721484)
XLA Ops:
  10.3 3.3 copy.43
  13.6 2.3 reshape.223
  18.2 4.7 %collective-permute-start.4 = (f32[]{:T(128)}, f32[]{:T(128)}, u32[]{:S(2)}, u32[]{:S(2)}) collective-permute-start(f32[]{:T(128)} %add.141), channel_id=1, source_target_pairs={{0,8},{4,12},{8,0},{12,4},{16,24},{20,28},{24,16},{28,20},{32,40},... | collective-permute-start | bytes 20 | tf_op jit(solution)/shard_map/ppermute | solution.py:23
  23.7 8.2 %collective-permute-start.5 = (f32[]{:T(128)}, f32[]{:T(128)}, u32[]{:S(2)}, u32[]{:S(2)}) collective-permute-start(f32[]{:T(128)} %add.142), channel_id=1, source_target_pairs={{0,16},{4,20},{8,24},{12,28},{16,0},{20,4},{24,8},{28,12},{32,48},... | collective-permute-start | bytes 20 | tf_op jit(solution)/shard_map/ppermute | solution.py:23
  32.8 4.6 %collective-permute-start.6 = (f32[]{:T(128)}, f32[]{:T(128)}, u32[]{:S(2)}, u32[]{:S(2)}) collective-permute-start(f32[]{:T(128)} %add.143), channel_id=1, source_target_pairs={{0,32},{4,36},{8,40},{12,44},{16,48},{20,52},{24,56},{28,60},{32,0... | collective-permute-start | bytes 20 | tf_op jit(solution)/shard_map/ppermute | solution.py:23
  42.7 2.8 collective-permute-start.8
  45.5 2.3 collective-permute-done.8
  49.5 128.5 %all-gather.4.cloned.1.call-done = bf16[64,84,1024]{2,1,0:T(8,128)(2,1)} async-done(((bf16[1,84,1024]{2,1,0:T(8,128)(2,1)}), bf16[64,84,1024]{2,1,0:T(8,128)(2,1)}) %all-gather.4.cloned.1.call-update) | async-done | bytes 11010064 | tf_op jit(solution)/shard_map/all_gather | solution.py:147
  178.0 5.3 %fusion.13 = f32[256,512]{0,1:T(8,128)S(1)} fusion(bf16[256,64,84]{0,2,1:T(8,128)(2,1)} %reshape.223, bf16[64,84,1024]{2,1,0:T(8,128)(2,1)} %all-gather.4.cloned.1.call-done), kind=kOutput, calls=%fused_computation.30 | convolution fusion | flops 1409286144 | bytes 9175040 | tf_op jit(solution)/shard_map/tsr,src->tc/dot_general | solution.py:151
  183.6 5.5 %collective-permute-start = (bf16[2,256,256]{1,2,0:T(8,128)(2,1)S(1)}, bf16[2,256,256]{1,2,0:T(8,128)(2,1)}, u32[]{:S(2)}, u32[]{:S(2)}) collective-permute-start(bf16[2,256,256]{1,2,0:T(8,128)(2,1)S(1)} %pad_maximum_fusion.2), channel_id=1, source_target_pairs={{0,8},{4,12},{8,16},{12,20},{16,24},{20,28},{24,32},{28,36},{32,40... | collective-permute-start | bytes 786440 | tf_op jit(solution)/shard_map/ppermute | solution.py:16
  191.0 10.2 %collective-permute-done = bf16[2,256,256]{1,2,0:T(8,128)(2,1)} collective-permute-done((bf16[2,256,256]{1,2,0:T(8,128)(2,1)S(1)}, bf16[2,256,256]{1,2,0:T(8,128)(2,1)}, u32[]{:S(2)}, u32[]{:S(2)}) %collective-permute-start) | collective-permute-done | bytes 262176 | tf_op jit(solution)/shard_map/ppermute | solution.py:16
  204.9 5.9 %collective-permute-start.1 = (bf16[2,256,256]{1,2,0:T(8,128)(2,1)}, bf16[2,256,256]{1,2,0:T(8,128)(2,1)}, u32[]{:S(2)}, u32[]{:S(2)}) collective-permute-start(bf16[2,256,256]{1,2,0:T(8,128)(2,1)} %collective-permute-done), channel_id=1, source_target_pairs={{0,8},{4,12},{8,16},{12,20},{16,24},{20,28},{24,32},{28,36},{32,40... | collective-permute-start | bytes 786440 | tf_op jit(solution)/shard_map/ppermute | solution.py:16
  213.6 13.9 %reshape.235 = bf16[5376,1024]{1,0:T(8,128)(2,1)} reshape(bf16[64,84,1024]{2,1,0:T(8,128)(2,1)} %all-gather.4.cloned.1.call-done) | data formatting | bytes 22020096
  227.5 8.9 %collective-permute-done.1 = bf16[2,256,256]{1,2,0:T(8,128)(2,1)} collective-permute-done((bf16[2,256,256]{1,2,0:T(8,128)(2,1)}, bf16[2,256,256]{1,2,0:T(8,128)(2,1)}, u32[]{:S(2)}, u32[]{:S(2)}) %collective-permute-start.1) | collective-permute-done | bytes 262176 | tf_op jit(solution)/shard_map/ppermute | solution.py:16
  242.5 2.3 select_reduce_fusion
  244.8 2.6 multiply_reduce_fusion.1
  249.3 3.1 fusion.7
  258.7 19.8 %collective-permute-done.9 = bf16[2,512,256]{1,2,0:T(8,128)(2,1)S(1)} collective-permute-done((bf16[2,512,256]{1,2,0:T(8,128)(2,1)S(1)}, bf16[2,512,256]{1,2,0:T(8,128)(2,1)S(1)}, u32[]{:S(2)}, u32[]{:S(2)}) %collective-permute-start.9) | collective-permute-done | bytes 524320 | tf_op jit(solution)/shard_map/ppermute | solution.py:16
  278.8 4.3 %collective-permute-start.11 = (bf16[2,256,256]{1,2,0:T(8,128)(2,1)S(1)}, bf16[2,256,256]{1,2,0:T(8,128)(2,1)S(1)}, u32[]{:S(2)}, u32[]{:S(2)}) collective-permute-start(bf16[2,256,256]{1,2,0:T(8,128)(2,1)S(1)} %fusion.24), channel_id=1, source_target_pairs={{8,0},{12,4},{16,8},{20,12},{24,16},{28,20},{32,24},{36,28},{40,32... | collective-permute-start | bytes 786440 | tf_op jit(solution)/shard_map/ppermute | solution.py:16
  283.3 8.1 %collective-permute-done.11 = bf16[2,256,256]{1,2,0:T(8,128)(2,1)S(1)} collective-permute-done((bf16[2,256,256]{1,2,0:T(8,128)(2,1)S(1)}, bf16[2,256,256]{1,2,0:T(8,128)(2,1)S(1)}, u32[]{:S(2)}, u32[]{:S(2)}) %collective-permute-start.11) | collective-permute-done | bytes 262176 | tf_op jit(solution)/shard_map/ppermute | solution.py:16
  296.2 2.4 copy-done
  298.8 3.2 collective-permute-done.12
  302.0 2.5 bitcast_add_fusion
  307.2 15.9 %collective-permute-done.13 = bf16[256,1344]{0,1:T(8,128)(2,1)S(1)} collective-permute-done((bf16[256,1344]{0,1:T(8,128)(2,1)}, bf16[256,1344]{0,1:T(8,128)(2,1)S(1)}, u32[]{:S(2)}, u32[]{:S(2)}) %collective-permute-start.13) | collective-permute-done | bytes 688160 | tf_op jit(solution)/shard_map/ppermute | solution.py:39
  (107 shorter events, 41.1 us)
Async XLA Ops:
  7.2 170.8 %all-gather.4.cloned.1.call-start = ((), (), s32[]{:S(2)}) async-start(), calls=%async_computation | async-start | bytes 11714560 | tf_op jit(solution)/shard_map/all_gather | solution.py:147
  10.2 6.8 %collective-permute-start.3 = (f32[]{:T(128)}, f32[]{:T(128)}, u32[]{:S(2)}, u32[]{:S(2)}) collective-permute-start(f32[]{:T(128)} %fusion.33), channel_id=1, source_target_pairs={{0,4},{4,0},{8,12},{12,8},{16,20},{20,16},{24,28},{28,24},{32,36},... | collective-permute-start | bytes 20 | tf_op jit(solution)/shard_map/ppermute | solution.py:23
  13.6 34.9 %copy-start.8 = (f32[256]{0:T(256)S(1)}, f32[256]{0:T(256)}, u32[]{:S(2)}) copy-start(f32[256]{0:T(256)} %param.17) | copy-start | bytes 3076
  13.6 34.9 %copy-start.9 = (s32[256]{0:T(256)S(1)}, s32[256]{0:T(256)}, u32[]{:S(2)}) copy-start(s32[256]{0:T(256)} %param.18) | copy-start | bytes 3076
  13.6 34.9 %copy-start.4 = (bf16[256,512]{1,0:T(8,128)(2,1)S(1)}, bf16[256,512]{1,0:T(8,128)(2,1)}, u32[]{:S(2)}) copy-start(bf16[256,512]{1,0:T(8,128)(2,1)} %param.19) | copy-start | bytes 786436
  18.2 4.9 %collective-permute-start.4 = (f32[]{:T(128)}, f32[]{:T(128)}, u32[]{:S(2)}, u32[]{:S(2)}) collective-permute-start(f32[]{:T(128)} %add.141), channel_id=1, source_target_pairs={{0,8},{4,12},{8,0},{12,4},{16,24},{20,28},{24,16},{28,20},{32,40},... | collective-permute-start | bytes 20 | tf_op jit(solution)/shard_map/ppermute | solution.py:23
  23.7 8.4 %collective-permute-start.5 = (f32[]{:T(128)}, f32[]{:T(128)}, u32[]{:S(2)}, u32[]{:S(2)}) collective-permute-start(f32[]{:T(128)} %add.142), channel_id=1, source_target_pairs={{0,16},{4,20},{8,24},{12,28},{16,0},{20,4},{24,8},{28,12},{32,48},... | collective-permute-start | bytes 20 | tf_op jit(solution)/shard_map/ppermute | solution.py:23
  32.8 5.1 %collective-permute-start.6 = (f32[]{:T(128)}, f32[]{:T(128)}, u32[]{:S(2)}, u32[]{:S(2)}) collective-permute-start(f32[]{:T(128)} %add.143), channel_id=1, source_target_pairs={{0,32},{4,36},{8,40},{12,44},{16,48},{20,52},{24,56},{28,60},{32,0... | collective-permute-start | bytes 20 | tf_op jit(solution)/shard_map/ppermute | solution.py:23
  38.5 3.6 %collective-permute-start.7 = (f32[]{:T(128)}, f32[]{:T(128)}, u32[]{:S(2)}, u32[]{:S(2)}) collective-permute-start(f32[]{:T(128)} %add.144), channel_id=1, source_target_pairs={{0,64},{4,68},{8,72},{12,76},{16,80},{20,84},{24,88},{28,92},{32,9... | collective-permute-start | bytes 20 | tf_op jit(solution)/shard_map/ppermute | solution.py:23
  42.7 5.1 %collective-permute-start.8 = (f32[]{:T(128)}, f32[]{:T(128)}, u32[]{:S(2)}, u32[]{:S(2)}) collective-permute-start(f32[]{:T(128)} %add.145), channel_id=1, source_target_pairs={{0,128},{4,132},{8,136},{12,140},{16,144},{20,148},{24,152},{28,15... | collective-permute-start | bytes 20 | tf_op jit(solution)/shard_map/ppermute | solution.py:23
  49.5 133.9 %copy-start.7 = (f32[128]{0:T(128)S(1)}, f32[128]{0:T(128)}, u32[]{:S(2)}) copy-start(f32[128]{0:T(128)} %param.15) | copy-start | bytes 1540
  178.0 11.2 %copy-start.2 = (bf16[256,64,84]{0,2,1:T(8,128)(2,1)S(1)}, bf16[256,64,84]{0,2,1:T(8,128)(2,1)}, u32[]{:S(2)}) copy-start(bf16[256,64,84]{0,2,1:T(8,128)(2,1)} %reshape.223) | copy-start | bytes 8257540
  183.6 27.2 %copy-start.6 = (f32[128]{0:T(128)S(1)}, f32[128]{0:T(128)}, u32[]{:S(2)}) copy-start(f32[128]{0:T(128)} %param.14) | copy-start | bytes 1540
  183.6 17.5 %collective-permute-start = (bf16[2,256,256]{1,2,0:T(8,128)(2,1)S(1)}, bf16[2,256,256]{1,2,0:T(8,128)(2,1)}, u32[]{:S(2)}, u32[]{:S(2)}) collective-permute-start(bf16[2,256,256]{1,2,0:T(8,128)(2,1)S(1)} %pad_maximum_fusion.2), channel_id=1, source_target_pairs={{0,8},{4,12},{8,16},{12,20},{16,24},{20,28},{24,32},{28,36},{32,40... | collective-permute-start | bytes 786440 | tf_op jit(solution)/shard_map/ppermute | solution.py:16
  202.9 34.4 %collective-permute-start.2 = (bf16[2,512,256]{1,2,0:T(8,128)(2,1)}, bf16[2,512,256]{1,2,0:T(8,128)(2,1)}, u32[]{:S(2)}, u32[]{:S(2)}) collective-permute-start(bf16[2,512,256]{1,2,0:T(8,128)(2,1)} %maximum_maximum_fusion), channel_id=1, source_target_pairs={{0,4},{4,8},{8,12},{12,16},{16,20},{20,24},{24,28},{28,32},{32,36}... | collective-permute-start | bytes 1572872 | tf_op jit(solution)/shard_map/ppermute | solution.py:16
  204.9 31.5 %collective-permute-start.1 = (bf16[2,256,256]{1,2,0:T(8,128)(2,1)}, bf16[2,256,256]{1,2,0:T(8,128)(2,1)}, u32[]{:S(2)}, u32[]{:S(2)}) collective-permute-start(bf16[2,256,256]{1,2,0:T(8,128)(2,1)} %collective-permute-done), channel_id=1, source_target_pairs={{0,8},{4,12},{8,16},{12,20},{16,24},{20,28},{24,32},{28,36},{32,40... | collective-permute-start | bytes 786440 | tf_op jit(solution)/shard_map/ppermute | solution.py:16
  227.5 12.9 %copy-start.3 = (bf16[256,4,64]{2,0,1:T(8,128)(2,1)S(1)}, bf16[256,4,64]{2,0,1:T(8,128)(2,1)}, u32[]{:S(2)}) copy-start(bf16[256,4,64]{2,0,1:T(8,128)(2,1)} %copy.45) | copy-start | bytes 393220
  253.7 38.2 %slice-start = ((s8[11010048]{0:T(1024)(128)(4,1)}), s8[4194304]{0:T(1024)(128)(4,1)S(1)}, s32[]{:S(2)}) async-start(s8[11010048]{0:T(1024)(128)(4,1)} %bitcast.102), calls=%async_computation.1 | async-start | bytes 8388608
  253.8 24.7 %collective-permute-start.9 = (bf16[2,512,256]{1,2,0:T(8,128)(2,1)S(1)}, bf16[2,512,256]{1,2,0:T(8,128)(2,1)S(1)}, u32[]{:S(2)}, u32[]{:S(2)}) collective-permute-start(bf16[2,512,256]{1,2,0:T(8,128)(2,1)S(1)} %pad_maximum_fusion.1), channel_id=1, source_target_pairs={{4,0},{8,4},{12,8},{16,12},{20,16},{24,20},{28,24},{32,28},{36,32}... | collective-permute-start | bytes 1572872 | tf_op jit(solution)/shard_map/ppermute | solution.py:16
  256.6 22.1 %collective-permute-start.10 = (bf16[2,256,256]{1,2,0:T(8,128)(2,1)S(1)}, bf16[2,256,256]{1,2,0:T(8,128)(2,1)S(1)}, u32[]{:S(2)}, u32[]{:S(2)}) collective-permute-start(bf16[2,256,256]{1,2,0:T(8,128)(2,1)S(1)} %get-tuple-element.8), channel_id=1, source_target_pairs={{8,0},{12,4},{16,8},{20,12},{24,16},{28,20},{32,24},{36,28},{40,32... | collective-permute-start | bytes 786440 | tf_op jit(solution)/shard_map/ppermute | solution.py:16
  258.5 33.5 %slice-start.1 = ((s8[11010048]{0:T(1024)(128)(4,1)}), s8[4194304]{0:T(1024)(128)(4,1)S(1)}, s32[]{:S(2)}) async-start(s8[11010048]{0:T(1024)(128)(4,1)} %bitcast.102), calls=%async_computation.2 | async-start | bytes 8388608
  278.8 12.6 %collective-permute-start.11 = (bf16[2,256,256]{1,2,0:T(8,128)(2,1)S(1)}, bf16[2,256,256]{1,2,0:T(8,128)(2,1)S(1)}, u32[]{:S(2)}, u32[]{:S(2)}) collective-permute-start(bf16[2,256,256]{1,2,0:T(8,128)(2,1)S(1)} %fusion.24), channel_id=1, source_target_pairs={{8,0},{12,4},{16,8},{20,12},{24,16},{28,20},{32,24},{36,28},{40,32... | collective-permute-start | bytes 786440 | tf_op jit(solution)/shard_map/ppermute | solution.py:16
  298.7 3.3 %collective-permute-start.12 = (bf16[256,2,1344]{0,2,1:T(8,128)(2,1)S(1)}, bf16[256,2,1344]{0,2,1:T(8,128)(2,1)}, u32[]{:S(2)}, u32[]{:S(2)}) collective-permute-start(bf16[256,2,1344]{0,2,1:T(8,128)(2,1)S(1)} %fusion.11), channel_id=1, source_target_pairs={{0,1},{1,0},{2,3},{3,2},{4,5},{5,4},{6,7},{7,6},{8,9},{9,8},{10,11... | collective-permute-start | bytes 4128776 | tf_op jit(solution)/shard_map/ppermute | solution.py:35
  305.4 17.7 %collective-permute-start.13 = (bf16[256,1344]{0,1:T(8,128)(2,1)}, bf16[256,1344]{0,1:T(8,128)(2,1)S(1)}, u32[]{:S(2)}, u32[]{:S(2)}) collective-permute-start(bf16[256,1344]{0,1:T(8,128)(2,1)} %fusion.16), channel_id=1, source_target_pairs={{0,2},{1,3},{2,0},{3,1},{4,6},{5,7},{6,4},{7,5},{8,10},{9,11},{10,... | collective-permute-start | bytes 2064392 | tf_op jit(solution)/shard_map/ppermute | solution.py:39
  (6 other events, 29.7 us)
Sparse Core Ops, SparseCore 0:
  12.2 165.7 all-gather.3

commit v9 on v8

--- a/solution.py
+++ b/solution.py
@@ -186,6 +186,7 @@
             dvalues.reshape(key_span, kv_heads * head_width),
         ]
     )
+    late_rows, stacked_grads = lax.optimization_barrier((joined_rows[:, :, q_cols:], stacked_grads))
     local_grads = stacked_grads[:, pred_count * tok_rows :]
     if pred_count == 4:
         odd_back = passed_along(
@@ -224,13 +225,11 @@
     dq_lin = back_query(dquery)[0].astype(jnp.bfloat16).reshape(tok_rows, q_heads * head_width)
     dk_lin = back_key(key_total)[0].astype(jnp.bfloat16).reshape(tok_rows, kv_heads * head_width)
     dv_lin = local_grads[1].astype(jnp.bfloat16)
-    flat_rows = joined_rows.reshape(seq_count * row_block, joined_rows.shape[-1])
-    query_part = lax.dot_general(
-        dq_lin, flat_rows[:, :q_cols], contract, preferred_element_type=jnp.float32
-    )
+    query_rows = joined_rows[:, :, :q_cols].reshape(seq_count * row_block, q_cols)
+    query_part = lax.dot_general(dq_lin, query_rows, contract, preferred_element_type=jnp.float32)
     key_value_part = lax.dot_general(
         jnp.concatenate([dk_lin, dv_lin], axis=1),
-        flat_rows[:, q_cols:],
+        late_rows.reshape(seq_count * row_block, late_rows.shape[-1]),
         contract,
         preferred_element_type=jnp.float32,
     )

time: 334 us -> 348 us (1.042)
  waiting for transfers between devices: 199 us -> 172 us
  local copies, waits for them, and re-layouts: 32.7 us -> 52.4 us
  matrix products: 21.4 us -> 32 us
  other arithmetic: 13.9 us -> 20 us
  starting transfers between devices: 44.5 us -> 48.7 us
    ppermute x6, waiting for transfers between devices: 47.1 us -> 21.1 us  [passed_along(): return lax.ppermute(block, axis, route)]
    dot_general x0 -> x2, local copies, waits for them, and re-layouts: none -> 17.8 us  [the longest x1 8.91 us: body(): lax.dot_general(dq_lin, query_rows, contract, preferred_element_type=jnp....]
    unnamed x35 -> x40, local copies, waits for them, and re-layouts: 25.4 us -> 12.3 us
    dot_general x2, matrix products: 3.18 us -> 12.3 us  [the longest x1 6.51 us: body(): lax.dot_general(dq_lin, query_rows, contract, preferred_element_type=jnp....]
    slice x2 -> x1, local copies, waits for them, and re-layouts: 0.95 us -> 9.34 us  [body(): joined_rows[:, :, q_cols:]]
    another operation x2 -> x5, local copies, waits for them, and re-layouts: 1.93 us -> 6.41 us  [the longest x2 4.36 us: body(): jnp.stack([key_grads.reshape(key_span, kv_heads * head_width), dvalues.re...]
    ppermute x6, starting transfers between devices: 21.8 us -> 26.1 us  [passed_along(): return lax.ppermute(block, axis, route)]
  transfers between devices with their start and end apart: 15 -> 15, of which waited for: 12 -> 12; matrix products, arithmetic and copies ran while one was open for 9% -> 16% of each run, Pallas kernels for 0% -> 0%
where the time goes in v9:
time: 348 us; the launch traced here: 344 us
  waiting for transfers between devices  172 us (49%)
  local copies, waits for them, and re-layouts  52.4 us (15%)
  starting transfers between devices  48.7 us (14%)
  matrix products  32 us (9%)
  other arithmetic  20 us (6%)
  between operations  19.4 us (6%)
    all_gather x1, waiting for transfers between devices, body(): lax.all_gather(jnp.concatenate([q_weight, k_weight, v_weight], axis=1), '...  127 us
    ppermute x6, starting transfers between devices, passed_along(): return lax.ppermute(block, axis, route)  26.1 us
    ppermute x6, starting transfers between devices, butterfly_sum(): lax.ppermute(value, axis, [(i, i ^ step) for i in range(size)])  22.6 us
    ppermute x6, waiting for transfers between devices, passed_along(): return lax.ppermute(block, axis, route)  21.1 us
    ppermute x1, waiting for transfers between devices, head_scatter_sum(): lax.ppermute(sent.astype(jnp.bfloat16), axis, [(i, i ^ 2) for i in range(...  15.9 us
    unnamed x40, local copies, waits for them, and re-layouts  12.3 us
    slice x1, local copies, waits for them, and re-layouts, body(): joined_rows[:, :, q_cols:]  9.34 us
    dot_general x1, local copies, waits for them, and re-layouts, body(): lax.dot_general(dq_lin, query_rows, contract, preferred_element_type=jnp....  8.91 us
  transfers between devices with their start and end apart: 15, of which 12 were waited for; matrix products, arithmetic and copies ran while one was open for 16% of the time, Pallas kernels for 0%

profile of v9, /device:TPU:38, one launch (start us, length us, event | category | flops | bytes accessed | tf_op | source)
XLA Modules:
  0.0 344.5 jit_solution(3610390190720260936)
XLA Ops:
  11.6 3.3 copy.51
  19.4 4.7 %collective-permute-start.4 = (f32[]{:T(128)}, f32[]{:T(128)}, u32[]{:S(2)}, u32[]{:S(2)}) collective-permute-start(f32[]{:T(128)} %add.141), channel_id=1, source_target_pairs={{0,8},{4,12},{8,0},{12,4},{16,24},{20,28},{24,16},{28,20},{32,40},... | collective-permute-start | bytes 20 | tf_op jit(solution)/shard_map/ppermute | solution.py:23
  25.0 8.2 %collective-permute-start.5 = (f32[]{:T(128)}, f32[]{:T(128)}, u32[]{:S(2)}, u32[]{:S(2)}) collective-permute-start(f32[]{:T(128)} %add.142), channel_id=1, source_target_pairs={{0,16},{4,20},{8,24},{12,28},{16,0},{20,4},{24,8},{28,12},{32,48},... | collective-permute-start | bytes 20 | tf_op jit(solution)/shard_map/ppermute | solution.py:23
  34.1 4.6 %collective-permute-start.6 = (f32[]{:T(128)}, f32[]{:T(128)}, u32[]{:S(2)}, u32[]{:S(2)}) collective-permute-start(f32[]{:T(128)} %add.143), channel_id=1, source_target_pairs={{0,32},{4,36},{8,40},{12,44},{16,48},{20,52},{24,56},{28,60},{32,0... | collective-permute-start | bytes 20 | tf_op jit(solution)/shard_map/ppermute | solution.py:23
  44.2 2.8 collective-permute-start.8
  51.0 127.0 %all-gather.4.cloned.1.call-done = bf16[64,84,1024]{2,1,0:T(8,128)(2,1)} async-done(((bf16[1,84,1024]{2,1,0:T(8,128)(2,1)}), bf16[64,84,1024]{2,1,0:T(8,128)(2,1)}) %all-gather.4.cloned.1.call-update) | async-done | bytes 11010064 | tf_op jit(solution)/shard_map/all_gather | solution.py:147
  178.0 5.3 %convolution_bitcast_fusion.1 = f32[256,512]{0,1:T(8,128)S(1)} fusion(bf16[256,64,84]{0,2,1:T(8,128)(2,1)} %reshape.223, bf16[64,84,1024]{2,1,0:T(8,128)(2,1)} %all-gather.4.cloned.1.call-done), kind=kOutput, calls=%fused_computation.19 | convolution fusion | flops 1409286144 | bytes 9175040 | tf_op jit(solution)/shard_map/tsr,src->tc/dot_general | solution.py:151
  184.1 5.4 %collective-permute-start = (bf16[2,256,256]{1,2,0:T(8,128)(2,1)S(1)}, bf16[2,256,256]{1,2,0:T(8,128)(2,1)}, u32[]{:S(2)}, u32[]{:S(2)}) collective-permute-start(bf16[2,256,256]{1,2,0:T(8,128)(2,1)S(1)} %pad_maximum_fusion.2), channel_id=1, source_target_pairs={{0,8},{4,12},{8,16},{12,20},{16,24},{20,28},{24,32},{28,36},{32,40... | collective-permute-start | bytes 786440 | tf_op jit(solution)/shard_map/ppermute | solution.py:16
  191.3 9.3 %fusion.29 = (bf16[64,84,512]{2,1,0:T(8,128)(2,1)}, bf16[64,84,512]{2,1,0:T(8,128)(2,1)}) fusion(bf16[64,84,1024]{2,1,0:T(8,128)(2,1)} %all-gather.4.cloned.1.call-done), kind=kLoop, calls=%fused_computation.93 | loop fusion | bytes 22020096 | tf_op jit(solution)/shard_map/slice | solution.py:152
  205.2 5.9 %collective-permute-start.1 = (bf16[2,256,256]{1,2,0:T(8,128)(2,1)}, bf16[2,256,256]{1,2,0:T(8,128)(2,1)}, u32[]{:S(2)}, u32[]{:S(2)}) collective-permute-start(bf16[2,256,256]{1,2,0:T(8,128)(2,1)} %collective-permute-done), channel_id=1, source_target_pairs={{0,8},{4,12},{8,16},{12,20},{16,24},{20,28},{24,32},{28,36},{32,40... | collective-permute-start | bytes 786440 | tf_op jit(solution)/shard_map/ppermute | solution.py:16
  213.9 8.9 %dot_general.46 = bf16[2,2,1344,512]{3,2,1,0:T(8,128)(2,1)} reshape(bf16[64,84,512]{2,1,0:T(8,128)(2,1)} %get-tuple-element.13) | data formatting | bytes 11010048 | tf_op jit(solution)/shard_map/dot_general | solution.py:229
  222.8 13.9 %collective-permute-done.1 = bf16[2,256,256]{1,2,0:T(8,128)(2,1)} collective-permute-done((bf16[2,256,256]{1,2,0:T(8,128)(2,1)}, bf16[2,256,256]{1,2,0:T(8,128)(2,1)}, u32[]{:S(2)}, u32[]{:S(2)}) %collective-permute-start.1) | collective-permute-done | bytes 262176 | tf_op jit(solution)/shard_map/ppermute | solution.py:16
  245.2 2.6 multiply_reduce_fusion.1
  247.8 3.4 fusion.23
  251.2 3.1 fusion.1
  257.4 2.8 copy.65
  268.6 8.9 %dot_general.50 = bf16[2,2,1344,512]{3,2,1,0:T(8,128)(2,1)} reshape(bf16[64,84,512]{2,1,0:T(8,128)(2,1)} %get-tuple-element.5) | data formatting | bytes 11010048 | tf_op jit(solution)/shard_map/dot_general | solution.py:230
  278.6 6.0 %collective-permute-done.9 = bf16[2,512,256]{2,1,0:T(8,128)(2,1)} collective-permute-done((bf16[2,512,256]{2,1,0:T(8,128)(2,1)}, bf16[2,512,256]{2,1,0:T(8,128)(2,1)}, u32[]{:S(2)}, u32[]{:S(2)}) %collective-permute-start.9) | collective-permute-done | bytes 524320 | tf_op jit(solution)/shard_map/ppermute | solution.py:16
  286.9 9.0 %collective-permute-start.11 = (bf16[2,256,256]{2,1,0:T(8,128)(2,1)S(1)}, bf16[2,256,256]{2,1,0:T(8,128)(2,1)S(1)}, u32[]{:S(2)}, u32[]{:S(2)}) collective-permute-start(bf16[2,256,256]{2,1,0:T(8,128)(2,1)S(1)} %fusion.9), channel_id=1, source_target_pairs={{8,0},{12,4},{16,8},{20,12},{24,16},{28,20},{32,24},{36,28},{40,32... | collective-permute-start | bytes 786440 | tf_op jit(solution)/shard_map/ppermute | solution.py:16
  295.9 6.5 %fusion.33 = f32[256,2,2,1344]{0,3,2,1:T(8,128)} fusion(bf16[256,512,1,1]{0,1,3,2:T(8,128)(2,1)S(1)} %bitcast.118, bf16[2,2,1344,512]{3,2,1,0:T(8,128)(2,1)} %dot_general.46), kind=kOutput, calls=%fused_computation.97 | convolution fusion | flops 1409286144 | bytes 11272192 | tf_op jit(solution)/shard_map/dot_general | solution.py:229
  303.8 5.8 %convolution_add_fusion = f32[256,2,2,1344]{0,3,2,1:T(8,128)S(1)} fusion(f32[256,2,2,1344]{0,3,2,1:T(8,128)} %fusion.33, bf16[2,2,1344,512]{3,2,1,0:T(8,128)(2,1)} %dot_general.50, bf16[256,256]{1,0:T(8,128)(2,1)S(1)} %fusion.15, bf16[256,256]{1,0:T(8,128)(2,1)S(1)} %copy.91), kind=kOutput, calls=%fused_computation.7 | convolution fusion | flops 1411186688 | bytes 16777216 | tf_op jit(solution)/shard_map/dot_general | solution.py:230
  312.3 3.2 collective-permute-done.12
  315.5 2.5 bitcast_add_fusion
  320.7 15.9 %collective-permute-done.13 = bf16[256,1344]{0,1:T(8,128)(2,1)S(1)} collective-permute-done((bf16[256,1344]{0,1:T(8,128)(2,1)}, bf16[256,1344]{0,1:T(8,128)(2,1)S(1)}, u32[]{:S(2)}, u32[]{:S(2)}) %collective-permute-start.13) | collective-permute-done | bytes 688160 | tf_op jit(solution)/shard_map/ppermute | solution.py:39
  (117 shorter events, 55.9 us)
Async XLA Ops:
  7.2 170.8 %all-gather.4.cloned.1.call-start = ((), (), s32[]{:S(2)}) async-start(), calls=%async_computation | async-start | bytes 11714560 | tf_op jit(solution)/shard_map/all_gather | solution.py:147
  10.2 7.9 %collective-permute-start.3 = (f32[]{:T(128)}, f32[]{:T(128)}, u32[]{:S(2)}, u32[]{:S(2)}) collective-permute-start(f32[]{:T(128)} %fusion.18), channel_id=1, source_target_pairs={{0,4},{4,0},{8,12},{12,8},{16,20},{20,16},{24,28},{28,24},{32,36},... | collective-permute-start | bytes 20 | tf_op jit(solution)/shard_map/ppermute | solution.py:23
  14.9 35.1 %copy-start.14 = (f32[256]{0:T(256)S(1)}, f32[256]{0:T(256)}, u32[]{:S(2)}) copy-start(f32[256]{0:T(256)} %param.17) | copy-start | bytes 3076
  14.9 35.1 %copy-start.15 = (s32[256]{0:T(256)S(1)}, s32[256]{0:T(256)}, u32[]{:S(2)}) copy-start(s32[256]{0:T(256)} %param.18) | copy-start | bytes 3076
  14.9 35.1 %copy-start.7 = (bf16[256,512]{1,0:T(8,128)(2,1)S(1)}, bf16[256,512]{1,0:T(8,128)(2,1)}, u32[]{:S(2)}) copy-start(bf16[256,512]{1,0:T(8,128)(2,1)} %param.19) | copy-start | bytes 786436
  19.4 4.9 %collective-permute-start.4 = (f32[]{:T(128)}, f32[]{:T(128)}, u32[]{:S(2)}, u32[]{:S(2)}) collective-permute-start(f32[]{:T(128)} %add.141), channel_id=1, source_target_pairs={{0,8},{4,12},{8,0},{12,4},{16,24},{20,28},{24,16},{28,20},{32,40},... | collective-permute-start | bytes 20 | tf_op jit(solution)/shard_map/ppermute | solution.py:23
  25.0 8.4 %collective-permute-start.5 = (f32[]{:T(128)}, f32[]{:T(128)}, u32[]{:S(2)}, u32[]{:S(2)}) collective-permute-start(f32[]{:T(128)} %add.142), channel_id=1, source_target_pairs={{0,16},{4,20},{8,24},{12,28},{16,0},{20,4},{24,8},{28,12},{32,48},... | collective-permute-start | bytes 20 | tf_op jit(solution)/shard_map/ppermute | solution.py:23
  34.1 5.1 %collective-permute-start.6 = (f32[]{:T(128)}, f32[]{:T(128)}, u32[]{:S(2)}, u32[]{:S(2)}) collective-permute-start(f32[]{:T(128)} %add.143), channel_id=1, source_target_pairs={{0,32},{4,36},{8,40},{12,44},{16,48},{20,52},{24,56},{28,60},{32,0... | collective-permute-start | bytes 20 | tf_op jit(solution)/shard_map/ppermute | solution.py:23
  39.9 3.6 %collective-permute-start.7 = (f32[]{:T(128)}, f32[]{:T(128)}, u32[]{:S(2)}, u32[]{:S(2)}) collective-permute-start(f32[]{:T(128)} %add.144), channel_id=1, source_target_pairs={{0,64},{4,68},{8,72},{12,76},{16,80},{20,84},{24,88},{28,92},{32,9... | collective-permute-start | bytes 20 | tf_op jit(solution)/shard_map/ppermute | solution.py:23
  44.2 5.1 %collective-permute-start.8 = (f32[]{:T(128)}, f32[]{:T(128)}, u32[]{:S(2)}, u32[]{:S(2)}) collective-permute-start(f32[]{:T(128)} %add.145), channel_id=1, source_target_pairs={{0,128},{4,132},{8,136},{12,140},{16,144},{20,148},{24,152},{28,15... | collective-permute-start | bytes 20 | tf_op jit(solution)/shard_map/ppermute | solution.py:23
  51.0 132.4 %copy-start.12 = (f32[128]{0:T(128)S(1)}, f32[128]{0:T(128)}, u32[]{:S(2)}) copy-start(f32[128]{0:T(128)} %param.15) | copy-start | bytes 1540
  178.0 11.6 %copy-start.1 = (bf16[64,84,1024]{2,1,0:T(8,128)(2,1)S(1)}, bf16[64,84,1024]{2,1,0:T(8,128)(2,1)}, u32[]{:S(2)}) copy-start(bf16[64,84,1024]{2,1,0:T(8,128)(2,1)} %all-gather.4.cloned.1.call-done) | copy-start | bytes 33030148
  178.0 11.6 %copy-start.2 = (bf16[256,64,84]{0,2,1:T(8,128)(2,1)S(1)}, bf16[256,64,84]{0,2,1:T(8,128)(2,1)}, u32[]{:S(2)}) copy-start(bf16[256,64,84]{0,2,1:T(8,128)(2,1)} %reshape.223) | copy-start | bytes 8257540
  184.1 17.4 %collective-permute-start = (bf16[2,256,256]{1,2,0:T(8,128)(2,1)S(1)}, bf16[2,256,256]{1,2,0:T(8,128)(2,1)}, u32[]{:S(2)}, u32[]{:S(2)}) collective-permute-start(bf16[2,256,256]{1,2,0:T(8,128)(2,1)S(1)} %pad_maximum_fusion.2), channel_id=1, source_target_pairs={{0,8},{4,12},{8,16},{12,20},{16,24},{20,28},{24,32},{28,36},{32,40... | collective-permute-start | bytes 786440 | tf_op jit(solution)/shard_map/ppermute | solution.py:16
  191.3 19.9 %copy-start.10 = (f32[128]{0:T(128)S(1)}, f32[128]{0:T(128)}, u32[]{:S(2)}) copy-start(f32[128]{0:T(128)} %param.14) | copy-start | bytes 1540
  203.3 34.4 %collective-permute-start.2 = (bf16[2,512,256]{1,2,0:T(8,128)(2,1)}, bf16[2,512,256]{1,2,0:T(8,128)(2,1)}, u32[]{:S(2)}, u32[]{:S(2)}) collective-permute-start(bf16[2,512,256]{1,2,0:T(8,128)(2,1)} %maximum_maximum_fusion), channel_id=1, source_target_pairs={{0,4},{4,8},{8,12},{12,16},{16,20},{20,24},{24,28},{28,32},{32,36}... | collective-permute-start | bytes 1572872 | tf_op jit(solution)/shard_map/ppermute | solution.py:16
  205.2 31.6 %collective-permute-start.1 = (bf16[2,256,256]{1,2,0:T(8,128)(2,1)}, bf16[2,256,256]{1,2,0:T(8,128)(2,1)}, u32[]{:S(2)}, u32[]{:S(2)}) collective-permute-start(bf16[2,256,256]{1,2,0:T(8,128)(2,1)} %collective-permute-done), channel_id=1, source_target_pairs={{0,8},{4,12},{8,16},{12,20},{16,24},{20,28},{24,32},{28,36},{32,40... | collective-permute-start | bytes 786440 | tf_op jit(solution)/shard_map/ppermute | solution.py:16
  222.8 18.0 %copy-start.6 = (bf16[256,4,64]{2,0,1:T(8,128)(2,1)S(1)}, bf16[256,4,64]{2,0,1:T(8,128)(2,1)}, u32[]{:S(2)}) copy-start(bf16[256,4,64]{2,0,1:T(8,128)(2,1)} %copy.53) | copy-start | bytes 393220
  222.8 18.0 %copy-start.16 = (s32[2,2]{1,0:T(2,128)S(1)}, s32[2,2]{1,0:T(2,128)}, u32[]{:S(2)}) copy-start(s32[2,2]{1,0:T(2,128)} %lt.36) | copy-start | bytes 52
  263.2 22.6 %collective-permute-start.10 = (bf16[2,256,256]{2,1,0:T(8,128)(2,1)}, bf16[2,256,256]{2,1,0:T(8,128)(2,1)}, u32[]{:S(2)}, u32[]{:S(2)}) collective-permute-start(bf16[2,256,256]{2,1,0:T(8,128)(2,1)} %get-tuple-element.14), channel_id=1, source_target_pairs={{8,0},{12,4},{16,8},{20,12},{24,16},{28,20},{32,24},{36,28},{40,32... | collective-permute-start | bytes 786440 | tf_op jit(solution)/shard_map/ppermute | solution.py:16
  265.9 18.8 %collective-permute-start.9 = (bf16[2,512,256]{2,1,0:T(8,128)(2,1)}, bf16[2,512,256]{2,1,0:T(8,128)(2,1)}, u32[]{:S(2)}, u32[]{:S(2)}) collective-permute-start(bf16[2,512,256]{2,1,0:T(8,128)(2,1)} %pad_maximum_fusion.1), channel_id=1, source_target_pairs={{4,0},{8,4},{12,8},{16,12},{20,16},{24,20},{28,24},{32,28},{36,32}... | collective-permute-start | bytes 1572872 | tf_op jit(solution)/shard_map/ppermute | solution.py:16
  286.9 15.8 %collective-permute-start.11 = (bf16[2,256,256]{2,1,0:T(8,128)(2,1)S(1)}, bf16[2,256,256]{2,1,0:T(8,128)(2,1)S(1)}, u32[]{:S(2)}, u32[]{:S(2)}) collective-permute-start(bf16[2,256,256]{2,1,0:T(8,128)(2,1)S(1)} %fusion.9), channel_id=1, source_target_pairs={{8,0},{12,4},{16,8},{20,12},{24,16},{28,20},{32,24},{36,28},{40,32... | collective-permute-start | bytes 786440 | tf_op jit(solution)/shard_map/ppermute | solution.py:16
  312.2 3.3 collective-permute-start.12
  318.9 17.7 %collective-permute-start.13 = (bf16[256,1344]{0,1:T(8,128)(2,1)}, bf16[256,1344]{0,1:T(8,128)(2,1)S(1)}, u32[]{:S(2)}, u32[]{:S(2)}) collective-permute-start(bf16[256,1344]{0,1:T(8,128)(2,1)} %fusion.6), channel_id=1, source_target_pairs={{0,2},{1,3},{2,0},{3,1},{4,6},{5,7},{6,4},{7,5},{8,10},{9,11},{10,... | collective-permute-start | bytes 2064392 | tf_op jit(solution)/shard_map/ppermute | solution.py:39
  (8 other events, 29.6 us)
Sparse Core Ops, SparseCore 0:
  12.2 165.7 all-gather.3

commit v10 on v8

--- a/solution.py
+++ b/solution.py
@@ -236,7 +236,14 @@
     )
     quarter_shape = (tok_rows, 2, 2, query_part.shape[1] // 4)
     partial_grad = query_part.reshape(quarter_shape) + key_value_part.reshape(quarter_shape)
-    grad_tokens = head_scatter_sum(partial_grad, "head")
+    half_rows = tok_rows // 2
+    grad_tokens = jnp.concatenate(
+        [
+            head_scatter_sum(partial_grad[:half_rows], "head"),
+            head_scatter_sum(partial_grad[half_rows:], "head"),
+        ],
+        axis=0,
+    )
     return (attended, grad_tokens)
 
 

time: 334 us -> 331 us (level)
  waiting for transfers between devices: 199 us -> 195 us
    ppermute x1 -> x2, waiting for transfers between devices: 15.9 us -> 15 us  [head_scatter_sum(): lax.ppermute(sent.astype(jnp.bfloat16), axis, [(i, i ^ 2) for i in range(...]
  transfers between devices with their start and end apart: 15 -> 17, of which waited for: 12 -> 13; matrix products, arithmetic and copies ran while one was open for 9% -> 10% of each run, Pallas kernels for 0% -> 0%
where the time goes in v10:
time: 331 us; the launch traced here: 328 us
  waiting for transfers between devices  195 us (59%)
  starting transfers between devices  47 us (14%)
  local copies, waits for them, and re-layouts  32.4 us (10%)
  matrix products  21.4 us (6%)
  between operations  19.5 us (6%)
  other arithmetic  13 us (4%)
    all_gather x1, waiting for transfers between devices, body(): lax.all_gather(jnp.concatenate([q_weight, k_weight, v_weight], axis=1), '...  128 us
    ppermute x6, waiting for transfers between devices, passed_along(): return lax.ppermute(block, axis, route)  46.9 us
    unnamed x35, local copies, waits for them, and re-layouts  24.6 us
    ppermute x6, starting transfers between devices, butterfly_sum(): lax.ppermute(value, axis, [(i, i ^ step) for i in range(size)])  22.5 us
    ppermute x6, starting transfers between devices, passed_along(): return lax.ppermute(block, axis, route)  21.8 us
    ppermute x2, waiting for transfers between devices, head_scatter_sum(): lax.ppermute(sent.astype(jnp.bfloat16), axis, [(i, i ^ 2) for i in range(...  15 us
  transfers between devices with their start and end apart: 17, of which 13 were waited for; matrix products, arithmetic and copies ran while one was open for 10% of the time, Pallas kernels for 0%

profile of v10, /device:TPU:38, one launch (start us, length us, event | category | flops | bytes accessed | tf_op | source)
XLA Modules:
  0.0 328.3 jit_solution(11297158945184074099)
XLA Ops:
  10.3 3.3 %copy.45 = bf16[256,5376]{0,1:T(8,128)(2,1)S(1)} copy(bf16[256,5376]{1,0:T(8,128)(2,1)} %param.10) | data formatting | bytes 5505024 | tf_op args[0]
  13.6 2.3 reshape.225
  18.2 4.7 %collective-permute-start.4 = (f32[]{:T(128)}, f32[]{:T(128)}, u32[]{:S(2)}, u32[]{:S(2)}) collective-permute-start(f32[]{:T(128)} %add.152), channel_id=1, source_target_pairs={{0,8},{4,12},{8,0},{12,4},{16,24},{20,28},{24,16},{28,20},{32,40},... | collective-permute-start | bytes 20 | tf_op jit(solution)/shard_map/ppermute | solution.py:23
  23.8 8.2 %collective-permute-start.5 = (f32[]{:T(128)}, f32[]{:T(128)}, u32[]{:S(2)}, u32[]{:S(2)}) collective-permute-start(f32[]{:T(128)} %add.153), channel_id=1, source_target_pairs={{0,16},{4,20},{8,24},{12,28},{16,0},{20,4},{24,8},{28,12},{32,48},... | collective-permute-start | bytes 20 | tf_op jit(solution)/shard_map/ppermute | solution.py:23
  32.9 4.6 %collective-permute-start.6 = (f32[]{:T(128)}, f32[]{:T(128)}, u32[]{:S(2)}, u32[]{:S(2)}) collective-permute-start(f32[]{:T(128)} %add.154), channel_id=1, source_target_pairs={{0,32},{4,36},{8,40},{12,44},{16,48},{20,52},{24,56},{28,60},{32,0... | collective-permute-start | bytes 20 | tf_op jit(solution)/shard_map/ppermute | solution.py:23
  38.7 2.2 collective-permute-start.7
  43.0 2.8 collective-permute-start.8
  45.8 2.3 collective-permute-done.8
  49.9 128.1 %all-gather.4.cloned.1.call-done = bf16[64,84,1024]{2,1,0:T(8,128)(2,1)} async-done(((bf16[1,84,1024]{2,1,0:T(8,128)(2,1)}), bf16[64,84,1024]{2,1,0:T(8,128)(2,1)}) %all-gather.4.cloned.1.call-update) | async-done | bytes 11010064 | tf_op jit(solution)/shard_map/all_gather | solution.py:147
  178.0 5.3 %fusion.11 = f32[256,512]{0,1:T(8,128)S(1)} fusion(bf16[256,64,84]{0,2,1:T(8,128)(2,1)} %reshape.225, bf16[64,84,1024]{2,1,0:T(8,128)(2,1)} %all-gather.4.cloned.1.call-done), kind=kOutput, calls=%fused_computation.28 | convolution fusion | flops 1409286144 | bytes 9175040 | tf_op jit(solution)/shard_map/tsr,src->tc/dot_general | solution.py:151
  183.7 5.5 %collective-permute-start = (bf16[2,256,256]{1,2,0:T(8,128)(2,1)S(1)}, bf16[2,256,256]{1,2,0:T(8,128)(2,1)}, u32[]{:S(2)}, u32[]{:S(2)}) collective-permute-start(bf16[2,256,256]{1,2,0:T(8,128)(2,1)S(1)} %pad_maximum_fusion.3), channel_id=1, source_target_pairs={{0,8},{4,12},{8,16},{12,20},{16,24},{20,28},{24,32},{28,36},{32,40... | collective-permute-start | bytes 786440 | tf_op jit(solution)/shard_map/ppermute | solution.py:16
  191.0 10.2 %collective-permute-done = bf16[2,256,256]{1,2,0:T(8,128)(2,1)} collective-permute-done((bf16[2,256,256]{1,2,0:T(8,128)(2,1)S(1)}, bf16[2,256,256]{1,2,0:T(8,128)(2,1)}, u32[]{:S(2)}, u32[]{:S(2)}) %collective-permute-start) | collective-permute-done | bytes 262176 | tf_op jit(solution)/shard_map/ppermute | solution.py:16
  204.9 5.9 %collective-permute-start.1 = (bf16[2,256,256]{1,2,0:T(8,128)(2,1)}, bf16[2,256,256]{1,2,0:T(8,128)(2,1)}, u32[]{:S(2)}, u32[]{:S(2)}) collective-permute-start(bf16[2,256,256]{1,2,0:T(8,128)(2,1)} %collective-permute-done), channel_id=1, source_target_pairs={{0,8},{4,12},{8,16},{12,20},{16,24},{20,28},{24,32},{28,36},{32,40... | collective-permute-start | bytes 786440 | tf_op jit(solution)/shard_map/ppermute | solution.py:16
  213.6 14.1 %reshape.237 = bf16[5376,1024]{1,0:T(8,128)(2,1)} reshape(bf16[64,84,1024]{2,1,0:T(8,128)(2,1)} %all-gather.4.cloned.1.call-done) | data formatting | bytes 22020096
  227.7 8.8 %collective-permute-done.1 = bf16[2,256,256]{1,2,0:T(8,128)(2,1)} collective-permute-done((bf16[2,256,256]{1,2,0:T(8,128)(2,1)}, bf16[2,256,256]{1,2,0:T(8,128)(2,1)}, u32[]{:S(2)}, u32[]{:S(2)}) %collective-permute-start.1) | collective-permute-done | bytes 262176 | tf_op jit(solution)/shard_map/ppermute | solution.py:16
  242.5 2.3 select_reduce_fusion
  244.8 2.6 multiply_reduce_fusion.1
  249.4 3.1 fusion.7
  253.9 2.2 collective-permute-start.9
  258.7 19.8 %collective-permute-done.9 = bf16[2,512,256]{1,2,0:T(8,128)(2,1)S(1)} collective-permute-done((bf16[2,512,256]{1,2,0:T(8,128)(2,1)S(1)}, bf16[2,512,256]{1,2,0:T(8,128)(2,1)S(1)}, u32[]{:S(2)}, u32[]{:S(2)}) %collective-permute-start.9) | collective-permute-done | bytes 524320 | tf_op jit(solution)/shard_map/ppermute | solution.py:16
  278.9 4.3 %collective-permute-start.11 = (bf16[2,256,256]{1,2,0:T(8,128)(2,1)S(1)}, bf16[2,256,256]{1,2,0:T(8,128)(2,1)S(1)}, u32[]{:S(2)}, u32[]{:S(2)}) collective-permute-start(bf16[2,256,256]{1,2,0:T(8,128)(2,1)S(1)} %fusion.25), channel_id=1, source_target_pairs={{8,0},{12,4},{16,8},{20,12},{24,16},{28,20},{32,24},{36,28},{40,32... | collective-permute-start | bytes 786440 | tf_op jit(solution)/shard_map/ppermute | solution.py:16
  283.4 8.1 %collective-permute-done.11 = bf16[2,256,256]{1,2,0:T(8,128)(2,1)S(1)} collective-permute-done((bf16[2,256,256]{1,2,0:T(8,128)(2,1)S(1)}, bf16[2,256,256]{1,2,0:T(8,128)(2,1)S(1)}, u32[]{:S(2)}, u32[]{:S(2)}) %collective-permute-start.11) | collective-permute-done | bytes 262176 | tf_op jit(solution)/shard_map/ppermute | solution.py:16
  305.4 8.6 %collective-permute-done.13 = bf16[128,1344]{0,1:T(8,128)(2,1)S(1)} collective-permute-done((bf16[128,1344]{0,1:T(8,128)(2,1)S(1)}, bf16[128,1344]{0,1:T(8,128)(2,1)S(1)}, u32[]{:S(2)}, u32[]{:S(2)}) %collective-permute-start.13) | collective-permute-done | bytes 344096 | tf_op jit(solution)/shard_map/ppermute | solution.py:39
  314.1 6.4 %collective-permute-done.15 = bf16[128,1344]{0,1:T(8,128)(2,1)S(1)} collective-permute-done((bf16[128,1344]{0,1:T(8,128)(2,1)S(1)}, bf16[128,1344]{0,1:T(8,128)(2,1)S(1)}, u32[]{:S(2)}, u32[]{:S(2)}) %collective-permute-start.15) | collective-permute-done | bytes 344096 | tf_op jit(solution)/shard_map/ppermute | solution.py:39
  (117 shorter events, 43.0 us)
Async XLA Ops:
  7.2 170.9 %all-gather.4.cloned.1.call-start = ((), (), s32[]{:S(2)}) async-start(), calls=%async_computation | async-start | bytes 11714560 | tf_op jit(solution)/shard_map/all_gather | solution.py:147
  10.2 6.7 %collective-permute-start.3 = (f32[]{:T(128)}, f32[]{:T(128)}, u32[]{:S(2)}, u32[]{:S(2)}) collective-permute-start(f32[]{:T(128)} %fusion.36), channel_id=1, source_target_pairs={{0,4},{4,0},{8,12},{12,8},{16,20},{20,16},{24,28},{28,24},{32,36},... | collective-permute-start | bytes 20 | tf_op jit(solution)/shard_map/ppermute | solution.py:23
  13.6 35.3 %copy-start.8 = (f32[256]{0:T(256)S(1)}, f32[256]{0:T(256)}, u32[]{:S(2)}) copy-start(f32[256]{0:T(256)} %param.17) | copy-start | bytes 3076
  13.6 35.3 %copy-start.9 = (s32[256]{0:T(256)S(1)}, s32[256]{0:T(256)}, u32[]{:S(2)}) copy-start(s32[256]{0:T(256)} %param.18) | copy-start | bytes 3076
  13.6 35.3 %copy-start.4 = (bf16[256,512]{1,0:T(8,128)(2,1)S(1)}, bf16[256,512]{1,0:T(8,128)(2,1)}, u32[]{:S(2)}) copy-start(bf16[256,512]{1,0:T(8,128)(2,1)} %param.19) | copy-start | bytes 786436
  18.2 4.9 %collective-permute-start.4 = (f32[]{:T(128)}, f32[]{:T(128)}, u32[]{:S(2)}, u32[]{:S(2)}) collective-permute-start(f32[]{:T(128)} %add.152), channel_id=1, source_target_pairs={{0,8},{4,12},{8,0},{12,4},{16,24},{20,28},{24,16},{28,20},{32,40},... | collective-permute-start | bytes 20 | tf_op jit(solution)/shard_map/ppermute | solution.py:23
  23.8 8.4 %collective-permute-start.5 = (f32[]{:T(128)}, f32[]{:T(128)}, u32[]{:S(2)}, u32[]{:S(2)}) collective-permute-start(f32[]{:T(128)} %add.153), channel_id=1, source_target_pairs={{0,16},{4,20},{8,24},{12,28},{16,0},{20,4},{24,8},{28,12},{32,48},... | collective-permute-start | bytes 20 | tf_op jit(solution)/shard_map/ppermute | solution.py:23
  32.9 5.1 %collective-permute-start.6 = (f32[]{:T(128)}, f32[]{:T(128)}, u32[]{:S(2)}, u32[]{:S(2)}) collective-permute-start(f32[]{:T(128)} %add.154), channel_id=1, source_target_pairs={{0,32},{4,36},{8,40},{12,44},{16,48},{20,52},{24,56},{28,60},{32,0... | collective-permute-start | bytes 20 | tf_op jit(solution)/shard_map/ppermute | solution.py:23
  38.7 3.6 %collective-permute-start.7 = (f32[]{:T(128)}, f32[]{:T(128)}, u32[]{:S(2)}, u32[]{:S(2)}) collective-permute-start(f32[]{:T(128)} %add.155), channel_id=1, source_target_pairs={{0,64},{4,68},{8,72},{12,76},{16,80},{20,84},{24,88},{28,92},{32,9... | collective-permute-start | bytes 20 | tf_op jit(solution)/shard_map/ppermute | solution.py:23
  43.0 5.1 %collective-permute-start.8 = (f32[]{:T(128)}, f32[]{:T(128)}, u32[]{:S(2)}, u32[]{:S(2)}) collective-permute-start(f32[]{:T(128)} %add.156), channel_id=1, source_target_pairs={{0,128},{4,132},{8,136},{12,140},{16,144},{20,148},{24,152},{28,15... | collective-permute-start | bytes 20 | tf_op jit(solution)/shard_map/ppermute | solution.py:23
  49.9 133.6 %copy-start.7 = (f32[128]{0:T(128)S(1)}, f32[128]{0:T(128)}, u32[]{:S(2)}) copy-start(f32[128]{0:T(128)} %param.15) | copy-start | bytes 1540
  183.6 27.2 %copy-start.6 = (f32[128]{0:T(128)S(1)}, f32[128]{0:T(128)}, u32[]{:S(2)}) copy-start(f32[128]{0:T(128)} %param.14) | copy-start | bytes 1540
  183.7 17.5 %collective-permute-start = (bf16[2,256,256]{1,2,0:T(8,128)(2,1)S(1)}, bf16[2,256,256]{1,2,0:T(8,128)(2,1)}, u32[]{:S(2)}, u32[]{:S(2)}) collective-permute-start(bf16[2,256,256]{1,2,0:T(8,128)(2,1)S(1)} %pad_maximum_fusion.3), channel_id=1, source_target_pairs={{0,8},{4,12},{8,16},{12,20},{16,24},{20,28},{24,32},{28,36},{32,40... | collective-permute-start | bytes 786440 | tf_op jit(solution)/shard_map/ppermute | solution.py:16
  203.0 34.4 %collective-permute-start.2 = (bf16[2,512,256]{1,2,0:T(8,128)(2,1)}, bf16[2,512,256]{1,2,0:T(8,128)(2,1)}, u32[]{:S(2)}, u32[]{:S(2)}) collective-permute-start(bf16[2,512,256]{1,2,0:T(8,128)(2,1)} %maximum_maximum_fusion), channel_id=1, source_target_pairs={{0,4},{4,8},{8,12},{12,16},{16,20},{20,24},{24,28},{28,32},{32,36}... | collective-permute-start | bytes 1572872 | tf_op jit(solution)/shard_map/ppermute | solution.py:16
  204.9 31.5 %collective-permute-start.1 = (bf16[2,256,256]{1,2,0:T(8,128)(2,1)}, bf16[2,256,256]{1,2,0:T(8,128)(2,1)}, u32[]{:S(2)}, u32[]{:S(2)}) collective-permute-start(bf16[2,256,256]{1,2,0:T(8,128)(2,1)} %collective-permute-done), channel_id=1, source_target_pairs={{0,8},{4,12},{8,16},{12,20},{16,24},{20,28},{24,32},{28,36},{32,40... | collective-permute-start | bytes 786440 | tf_op jit(solution)/shard_map/ppermute | solution.py:16
  253.8 38.2 %slice-start = ((s8[11010048]{0:T(1024)(128)(4,1)}), s8[4194304]{0:T(1024)(128)(4,1)S(1)}, s32[]{:S(2)}) async-start(s8[11010048]{0:T(1024)(128)(4,1)} %bitcast.118), calls=%async_computation.1 | async-start | bytes 8388608
  253.9 24.7 %collective-permute-start.9 = (bf16[2,512,256]{1,2,0:T(8,128)(2,1)S(1)}, bf16[2,512,256]{1,2,0:T(8,128)(2,1)S(1)}, u32[]{:S(2)}, u32[]{:S(2)}) collective-permute-start(bf16[2,512,256]{1,2,0:T(8,128)(2,1)S(1)} %pad_maximum_fusion.2), channel_id=1, source_target_pairs={{4,0},{8,4},{12,8},{16,12},{20,16},{24,20},{28,24},{32,28},{36,32}... | collective-permute-start | bytes 1572872 | tf_op jit(solution)/shard_map/ppermute | solution.py:16
  256.6 22.1 %collective-permute-start.10 = (bf16[2,256,256]{1,2,0:T(8,128)(2,1)S(1)}, bf16[2,256,256]{1,2,0:T(8,128)(2,1)S(1)}, u32[]{:S(2)}, u32[]{:S(2)}) collective-permute-start(bf16[2,256,256]{1,2,0:T(8,128)(2,1)S(1)} %get-tuple-element.10), channel_id=1, source_target_pairs={{8,0},{12,4},{16,8},{20,12},{24,16},{28,20},{32,24},{36,28},{40,32... | collective-permute-start | bytes 786440 | tf_op jit(solution)/shard_map/ppermute | solution.py:16
  258.5 33.5 %slice-start.1 = ((s8[11010048]{0:T(1024)(128)(4,1)}), s8[4194304]{0:T(1024)(128)(4,1)S(1)}, s32[]{:S(2)}) async-start(s8[11010048]{0:T(1024)(128)(4,1)} %bitcast.118), calls=%async_computation.2 | async-start | bytes 8388608
  278.9 12.6 %collective-permute-start.11 = (bf16[2,256,256]{1,2,0:T(8,128)(2,1)S(1)}, bf16[2,256,256]{1,2,0:T(8,128)(2,1)S(1)}, u32[]{:S(2)}, u32[]{:S(2)}) collective-permute-start(bf16[2,256,256]{1,2,0:T(8,128)(2,1)S(1)} %fusion.25), channel_id=1, source_target_pairs={{8,0},{12,4},{16,8},{20,12},{24,16},{28,20},{32,24},{36,28},{40,32... | collective-permute-start | bytes 786440 | tf_op jit(solution)/shard_map/ppermute | solution.py:16
  299.0 2.5 collective-permute-start.12
  300.9 2.4 collective-permute-start.14
  303.0 11.0 %collective-permute-start.13 = (bf16[128,1344]{0,1:T(8,128)(2,1)S(1)}, bf16[128,1344]{0,1:T(8,128)(2,1)S(1)}, u32[]{:S(2)}, u32[]{:S(2)}) collective-permute-start(bf16[128,1344]{0,1:T(8,128)(2,1)S(1)} %fusion.26), channel_id=1, source_target_pairs={{0,2},{1,3},{2,0},{3,1},{4,6},{5,7},{6,4},{7,5},{8,10},{9,11},{10,... | collective-permute-start | bytes 1032200 | tf_op jit(solution)/shard_map/ppermute | solution.py:39
  303.5 17.0 %collective-permute-start.15 = (bf16[128,1344]{0,1:T(8,128)(2,1)S(1)}, bf16[128,1344]{0,1:T(8,128)(2,1)S(1)}, u32[]{:S(2)}, u32[]{:S(2)}) collective-permute-start(bf16[128,1344]{0,1:T(8,128)(2,1)S(1)} %fusion.27), channel_id=1, source_target_pairs={{0,2},{1,3},{2,0},{3,1},{4,6},{5,7},{6,4},{7,5},{8,10},{9,11},{10,... | collective-permute-start | bytes 1032200 | tf_op jit(solution)/shard_map/ppermute | solution.py:39
  (8 other events, 52.7 us)
Sparse Core Ops, SparseCore 0:
  12.2 165.8 all-gather.3

commit v11 on v10

--- a/solution.py
+++ b/solution.py
@@ -164,12 +164,11 @@
     k_rot = norm_rotate(k_linear, k_gain, cosine, sine_table).astype(jnp.bfloat16)
     stacked = jnp.stack([k_rot.reshape(tok_rows, kv_heads * head_width), values])
     if pred_count == 4:
+        near_one = passed_along(stacked, "seq", 1)
         near_two = passed_along(stacked, "seq", 2)
-        odd_pair = passed_along(jnp.concatenate([near_two, stacked], axis=1), "seq", 1)
+        near_three = passed_along(near_two, "seq", 1)
         far_one = passed_along(near_two, "seq", 2)
-        extended = jnp.concatenate(
-            [far_one, odd_pair[:, :tok_rows], near_two, odd_pair[:, tok_rows:], stacked], axis=1
-        )
+        extended = jnp.concatenate([far_one, near_three, near_two, near_one, stacked], axis=1)
     else:
         received = []
         for offset in range(1, pred_count + 1):

time: 331 us -> 327 us (0.988)
  waiting for transfers between devices: 195 us -> 175 us
  starting transfers between devices: 47 us -> 62.9 us
    ppermute x6 -> x7, waiting for transfers between devices: 46.9 us -> 26.1 us  [passed_along(): return lax.ppermute(block, axis, route)]
    ppermute x6 -> x7, starting transfers between devices: 21.8 us -> 37.7 us  [passed_along(): return lax.ppermute(block, axis, route)]
  transfers between devices with their start and end apart: 17 -> 18, of which waited for: 13 -> 13; matrix products, arithmetic and copies ran while one was open for 10% -> 11% of each run, Pallas kernels for 0% -> 0%
where the time goes in v11:
time: 327 us; the launch traced here: 322 us
  waiting for transfers between devices  175 us (54%)
  starting transfers between devices  62.9 us (19%)
  local copies, waits for them, and re-layouts  32.4 us (10%)
  matrix products  21.4 us (7%)
  between operations  18.8 us (6%)
  other arithmetic  12 us (4%)
    all_gather x1, waiting for transfers between devices, body(): lax.all_gather(jnp.concatenate([q_weight, k_weight, v_weight], axis=1), '...  128 us
    ppermute x7, starting transfers between devices, passed_along(): return lax.ppermute(block, axis, route)  37.7 us
    ppermute x7, waiting for transfers between devices, passed_along(): return lax.ppermute(block, axis, route)  26.1 us
    unnamed x35, local copies, waits for them, and re-layouts  24.6 us
    ppermute x6, starting transfers between devices, butterfly_sum(): lax.ppermute(value, axis, [(i, i ^ step) for i in range(size)])  22.6 us
    ppermute x2, waiting for transfers between devices, head_scatter_sum(): lax.ppermute(sent.astype(jnp.bfloat16), axis, [(i, i ^ 2) for i in range(...  15 us
  transfers between devices with their start and end apart: 18, of which 13 were waited for; matrix products, arithmetic and copies ran while one was open for 11% of the time, Pallas kernels for 0%

profile of v11, /device:TPU:38, one launch (start us, length us, event | category | flops | bytes accessed | tf_op | source)
XLA Modules:
  0.0 322.3 jit_solution(13895972108080014891)
XLA Ops:
  10.3 3.3 %copy.45 = bf16[256,5376]{0,1:T(8,128)(2,1)S(1)} copy(bf16[256,5376]{1,0:T(8,128)(2,1)} %param.10) | data formatting | bytes 5505024 | tf_op args[0]
  13.6 2.3 reshape.225
  18.1 4.7 %collective-permute-start.5 = (f32[]{:T(128)}, f32[]{:T(128)}, u32[]{:S(2)}, u32[]{:S(2)}) collective-permute-start(f32[]{:T(128)} %add.152), channel_id=1, source_target_pairs={{0,8},{4,12},{8,0},{12,4},{16,24},{20,28},{24,16},{28,20},{32,40},... | collective-permute-start | bytes 20 | tf_op jit(solution)/shard_map/ppermute | solution.py:23
  23.7 8.2 %collective-permute-start.6 = (f32[]{:T(128)}, f32[]{:T(128)}, u32[]{:S(2)}, u32[]{:S(2)}) collective-permute-start(f32[]{:T(128)} %add.153), channel_id=1, source_target_pairs={{0,16},{4,20},{8,24},{12,28},{16,0},{20,4},{24,8},{28,12},{32,48},... | collective-permute-start | bytes 20 | tf_op jit(solution)/shard_map/ppermute | solution.py:23
  32.9 4.6 %collective-permute-start.7 = (f32[]{:T(128)}, f32[]{:T(128)}, u32[]{:S(2)}, u32[]{:S(2)}) collective-permute-start(f32[]{:T(128)} %add.154), channel_id=1, source_target_pairs={{0,32},{4,36},{8,40},{12,44},{16,48},{20,52},{24,56},{28,60},{32,0... | collective-permute-start | bytes 20 | tf_op jit(solution)/shard_map/ppermute | solution.py:23
  43.0 2.8 collective-permute-start.9
  45.8 2.5 collective-permute-done.9
  49.9 128.1 %all-gather.4.cloned.1.call-done = bf16[64,84,1024]{2,1,0:T(8,128)(2,1)} async-done(((bf16[1,84,1024]{2,1,0:T(8,128)(2,1)}), bf16[64,84,1024]{2,1,0:T(8,128)(2,1)}) %all-gather.4.cloned.1.call-update) | async-done | bytes 11010064 | tf_op jit(solution)/shard_map/all_gather | solution.py:147
  178.1 5.3 %fusion.11 = f32[256,512]{0,1:T(8,128)S(1)} fusion(bf16[256,64,84]{0,2,1:T(8,128)(2,1)} %reshape.225, bf16[64,84,1024]{2,1,0:T(8,128)(2,1)} %all-gather.4.cloned.1.call-done), kind=kOutput, calls=%fused_computation.28 | convolution fusion | flops 1409286144 | bytes 9175040 | tf_op jit(solution)/shard_map/tsr,src->tc/dot_general | solution.py:151
  184.4 5.4 %collective-permute-start = (bf16[2,256,256]{1,2,0:T(8,128)(2,1)}, bf16[2,256,256]{1,2,0:T(8,128)(2,1)}, u32[]{:S(2)}, u32[]{:S(2)}) collective-permute-start(bf16[2,256,256]{1,2,0:T(8,128)(2,1)} %pad_maximum_fusion.3), channel_id=1, source_target_pairs={{0,8},{4,12},{8,16},{12,20},{16,24},{20,28},{24,32},{28,36},{32,40... | collective-permute-start | bytes 786440 | tf_op jit(solution)/shard_map/ppermute | solution.py:16
  189.8 2.6 collective-permute-start.3
  194.1 11.8 %collective-permute-done = bf16[2,256,256]{1,2,0:T(8,128)(2,1)} collective-permute-done((bf16[2,256,256]{1,2,0:T(8,128)(2,1)}, bf16[2,256,256]{1,2,0:T(8,128)(2,1)}, u32[]{:S(2)}, u32[]{:S(2)}) %collective-permute-start) | collective-permute-done | bytes 262176 | tf_op jit(solution)/shard_map/ppermute | solution.py:16
  212.8 14.0 %reshape.237 = bf16[5376,1024]{1,0:T(8,128)(2,1)} reshape(bf16[64,84,1024]{2,1,0:T(8,128)(2,1)} %all-gather.4.cloned.1.call-done) | data formatting | bytes 22020096
  233.0 2.3 select_reduce_fusion
  235.3 2.6 multiply_reduce_fusion.1
  239.8 3.1 fusion.7
  244.3 4.2 %collective-permute-start.10 = (bf16[2,512,256]{1,2,0:T(8,128)(2,1)S(1)}, bf16[2,512,256]{1,2,0:T(8,128)(2,1)S(1)}, u32[]{:S(2)}, u32[]{:S(2)}) collective-permute-start(bf16[2,512,256]{1,2,0:T(8,128)(2,1)S(1)} %pad_maximum_fusion.2), channel_id=1, source_target_pairs={{4,0},{8,4},{12,8},{16,12},{20,16},{24,20},{28,24},{32,28},{36,32}... | collective-permute-start | bytes 1572872 | tf_op jit(solution)/shard_map/ppermute | solution.py:16
  249.0 9.3 %collective-permute-start.11 = (bf16[2,256,256]{1,2,0:T(8,128)(2,1)S(1)}, bf16[2,256,256]{1,2,0:T(8,128)(2,1)S(1)}, u32[]{:S(2)}, u32[]{:S(2)}) collective-permute-start(bf16[2,256,256]{1,2,0:T(8,128)(2,1)S(1)} %get-tuple-element.10), channel_id=1, source_target_pairs={{8,0},{12,4},{16,8},{20,12},{24,16},{28,20},{32,24},{36,28},{40,32... | collective-permute-start | bytes 786440 | tf_op jit(solution)/shard_map/ppermute | solution.py:16
  258.6 4.5 %collective-permute-done.10 = bf16[2,512,256]{1,2,0:T(8,128)(2,1)S(1)} collective-permute-done((bf16[2,512,256]{1,2,0:T(8,128)(2,1)S(1)}, bf16[2,512,256]{1,2,0:T(8,128)(2,1)S(1)}, u32[]{:S(2)}, u32[]{:S(2)}) %collective-permute-start.10) | collective-permute-done | bytes 524320 | tf_op jit(solution)/shard_map/ppermute | solution.py:16
  263.3 4.2 %collective-permute-done.11 = bf16[2,256,256]{1,2,0:T(8,128)(2,1)S(1)} collective-permute-done((bf16[2,256,256]{1,2,0:T(8,128)(2,1)S(1)}, bf16[2,256,256]{1,2,0:T(8,128)(2,1)S(1)}, u32[]{:S(2)}, u32[]{:S(2)}) %collective-permute-start.11) | collective-permute-done | bytes 262176 | tf_op jit(solution)/shard_map/ppermute | solution.py:16
  267.6 12.2 %collective-permute-start.12 = (bf16[2,256,256]{1,2,0:T(8,128)(2,1)S(1)}, bf16[2,256,256]{1,2,0:T(8,128)(2,1)S(1)}, u32[]{:S(2)}, u32[]{:S(2)}) collective-permute-start(bf16[2,256,256]{1,2,0:T(8,128)(2,1)S(1)} %fusion.25), channel_id=1, source_target_pairs={{8,0},{12,4},{16,8},{20,12},{24,16},{28,20},{32,24},{36,28},{40,32... | collective-permute-start | bytes 786440 | tf_op jit(solution)/shard_map/ppermute | solution.py:16
  280.0 5.5 %collective-permute-done.12 = bf16[2,256,256]{1,2,0:T(8,128)(2,1)S(1)} collective-permute-done((bf16[2,256,256]{1,2,0:T(8,128)(2,1)S(1)}, bf16[2,256,256]{1,2,0:T(8,128)(2,1)S(1)}, u32[]{:S(2)}, u32[]{:S(2)}) %collective-permute-start.12) | collective-permute-done | bytes 262176 | tf_op jit(solution)/shard_map/ppermute | solution.py:16
  299.4 8.6 %collective-permute-done.14 = bf16[128,1344]{0,1:T(8,128)(2,1)S(1)} collective-permute-done((bf16[128,1344]{0,1:T(8,128)(2,1)S(1)}, bf16[128,1344]{0,1:T(8,128)(2,1)S(1)}, u32[]{:S(2)}, u32[]{:S(2)}) %collective-permute-start.14) | collective-permute-done | bytes 344096 | tf_op jit(solution)/shard_map/ppermute | solution.py:39
  308.1 6.4 %collective-permute-done.16 = bf16[128,1344]{0,1:T(8,128)(2,1)S(1)} collective-permute-done((bf16[128,1344]{0,1:T(8,128)(2,1)S(1)}, bf16[128,1344]{0,1:T(8,128)(2,1)S(1)}, u32[]{:S(2)}, u32[]{:S(2)}) %collective-permute-start.16) | collective-permute-done | bytes 344096 | tf_op jit(solution)/shard_map/ppermute | solution.py:39
  (118 shorter events, 45.0 us)
Async XLA Ops:
  7.2 170.9 %all-gather.4.cloned.1.call-start = ((), (), s32[]{:S(2)}) async-start(), calls=%async_computation | async-start | bytes 11714560 | tf_op jit(solution)/shard_map/all_gather | solution.py:147
  10.2 6.7 %collective-permute-start.4 = (f32[]{:T(128)}, f32[]{:T(128)}, u32[]{:S(2)}, u32[]{:S(2)}) collective-permute-start(f32[]{:T(128)} %fusion.36), channel_id=1, source_target_pairs={{0,4},{4,0},{8,12},{12,8},{16,20},{20,16},{24,28},{28,24},{32,36},... | collective-permute-start | bytes 20 | tf_op jit(solution)/shard_map/ppermute | solution.py:23
  13.6 35.3 %copy-start.8 = (f32[256]{0:T(256)S(1)}, f32[256]{0:T(256)}, u32[]{:S(2)}) copy-start(f32[256]{0:T(256)} %param.17) | copy-start | bytes 3076
  13.6 35.3 %copy-start.9 = (s32[256]{0:T(256)S(1)}, s32[256]{0:T(256)}, u32[]{:S(2)}) copy-start(s32[256]{0:T(256)} %param.18) | copy-start | bytes 3076
  13.6 35.3 %copy-start.4 = (bf16[256,512]{1,0:T(8,128)(2,1)S(1)}, bf16[256,512]{1,0:T(8,128)(2,1)}, u32[]{:S(2)}) copy-start(bf16[256,512]{1,0:T(8,128)(2,1)} %param.19) | copy-start | bytes 786436
  18.1 5.0 %collective-permute-start.5 = (f32[]{:T(128)}, f32[]{:T(128)}, u32[]{:S(2)}, u32[]{:S(2)}) collective-permute-start(f32[]{:T(128)} %add.152), channel_id=1, source_target_pairs={{0,8},{4,12},{8,0},{12,4},{16,24},{20,28},{24,16},{28,20},{32,40},... | collective-permute-start | bytes 20 | tf_op jit(solution)/shard_map/ppermute | solution.py:23
  23.7 8.6 %collective-permute-start.6 = (f32[]{:T(128)}, f32[]{:T(128)}, u32[]{:S(2)}, u32[]{:S(2)}) collective-permute-start(f32[]{:T(128)} %add.153), channel_id=1, source_target_pairs={{0,16},{4,20},{8,24},{12,28},{16,0},{20,4},{24,8},{28,12},{32,48},... | collective-permute-start | bytes 20 | tf_op jit(solution)/shard_map/ppermute | solution.py:23
  32.9 5.3 %collective-permute-start.7 = (f32[]{:T(128)}, f32[]{:T(128)}, u32[]{:S(2)}, u32[]{:S(2)}) collective-permute-start(f32[]{:T(128)} %add.154), channel_id=1, source_target_pairs={{0,32},{4,36},{8,40},{12,44},{16,48},{20,52},{24,56},{28,60},{32,0... | collective-permute-start | bytes 20 | tf_op jit(solution)/shard_map/ppermute | solution.py:23
  38.7 3.8 %collective-permute-start.8 = (f32[]{:T(128)}, f32[]{:T(128)}, u32[]{:S(2)}, u32[]{:S(2)}) collective-permute-start(f32[]{:T(128)} %add.155), channel_id=1, source_target_pairs={{0,64},{4,68},{8,72},{12,76},{16,80},{20,84},{24,88},{28,92},{32,9... | collective-permute-start | bytes 20 | tf_op jit(solution)/shard_map/ppermute | solution.py:23
  43.0 5.3 %collective-permute-start.9 = (f32[]{:T(128)}, f32[]{:T(128)}, u32[]{:S(2)}, u32[]{:S(2)}) collective-permute-start(f32[]{:T(128)} %add.156), channel_id=1, source_target_pairs={{0,128},{4,132},{8,136},{12,140},{16,144},{20,148},{24,152},{28,15... | collective-permute-start | bytes 20 | tf_op jit(solution)/shard_map/ppermute | solution.py:23
  49.9 133.6 %copy-start.7 = (f32[128]{0:T(128)S(1)}, f32[128]{0:T(128)}, u32[]{:S(2)}) copy-start(f32[128]{0:T(128)} %param.15) | copy-start | bytes 1540
  184.4 21.6 %collective-permute-start = (bf16[2,256,256]{1,2,0:T(8,128)(2,1)}, bf16[2,256,256]{1,2,0:T(8,128)(2,1)}, u32[]{:S(2)}, u32[]{:S(2)}) collective-permute-start(bf16[2,256,256]{1,2,0:T(8,128)(2,1)} %pad_maximum_fusion.3), channel_id=1, source_target_pairs={{0,8},{4,12},{8,16},{12,20},{16,24},{20,28},{24,32},{28,36},{32,40... | collective-permute-start | bytes 786440 | tf_op jit(solution)/shard_map/ppermute | solution.py:16
  189.8 40.0 %collective-permute-start.3 = (bf16[2,256,256]{1,2,0:T(8,128)(2,1)}, bf16[2,256,256]{1,2,0:T(8,128)(2,1)}, u32[]{:S(2)}, u32[]{:S(2)}) collective-permute-start(bf16[2,256,256]{1,2,0:T(8,128)(2,1)} %pad_maximum_fusion.3), channel_id=1, source_target_pairs={{0,4},{4,8},{8,12},{12,16},{16,20},{20,24},{24,28},{28,32},{32,36}... | collective-permute-start | bytes 786440 | tf_op jit(solution)/shard_map/ppermute | solution.py:16
  206.0 20.9 %collective-permute-start.1 = (bf16[2,256,256]{1,2,0:T(8,128)(2,1)}, bf16[2,256,256]{1,2,0:T(8,128)(2,1)}, u32[]{:S(2)}, u32[]{:S(2)}) collective-permute-start(bf16[2,256,256]{1,2,0:T(8,128)(2,1)} %collective-permute-done), channel_id=1, source_target_pairs={{0,8},{4,12},{8,16},{12,20},{16,24},{20,28},{24,32},{28,36},{32,40... | collective-permute-start | bytes 786440 | tf_op jit(solution)/shard_map/ppermute | solution.py:16
  208.0 19.8 %collective-permute-start.2 = (bf16[2,256,256]{1,2,0:T(8,128)(2,1)}, bf16[2,256,256]{1,2,0:T(8,128)(2,1)}, u32[]{:S(2)}, u32[]{:S(2)}) collective-permute-start(bf16[2,256,256]{1,2,0:T(8,128)(2,1)} %collective-permute-done), channel_id=1, source_target_pairs={{0,4},{4,8},{8,12},{12,16},{16,20},{20,24},{24,28},{28,32},{32,36}... | collective-permute-start | bytes 786440 | tf_op jit(solution)/shard_map/ppermute | solution.py:16
  244.2 41.8 %slice-start = ((s8[11010048]{0:T(1024)(128)(4,1)}), s8[4194304]{0:T(1024)(128)(4,1)S(1)}, s32[]{:S(2)}) async-start(s8[11010048]{0:T(1024)(128)(4,1)} %bitcast.118), calls=%async_computation.1 | async-start | bytes 8388608
  244.3 18.8 %collective-permute-start.10 = (bf16[2,512,256]{1,2,0:T(8,128)(2,1)S(1)}, bf16[2,512,256]{1,2,0:T(8,128)(2,1)S(1)}, u32[]{:S(2)}, u32[]{:S(2)}) collective-permute-start(bf16[2,512,256]{1,2,0:T(8,128)(2,1)S(1)} %pad_maximum_fusion.2), channel_id=1, source_target_pairs={{4,0},{8,4},{12,8},{16,12},{20,16},{24,20},{28,24},{32,28},{36,32}... | collective-permute-start | bytes 1572872 | tf_op jit(solution)/shard_map/ppermute | solution.py:16
  249.0 18.5 %collective-permute-start.11 = (bf16[2,256,256]{1,2,0:T(8,128)(2,1)S(1)}, bf16[2,256,256]{1,2,0:T(8,128)(2,1)S(1)}, u32[]{:S(2)}, u32[]{:S(2)}) collective-permute-start(bf16[2,256,256]{1,2,0:T(8,128)(2,1)S(1)} %get-tuple-element.10), channel_id=1, source_target_pairs={{8,0},{12,4},{16,8},{20,12},{24,16},{28,20},{32,24},{36,28},{40,32... | collective-permute-start | bytes 786440 | tf_op jit(solution)/shard_map/ppermute | solution.py:16
  258.4 27.6 %slice-start.1 = ((s8[11010048]{0:T(1024)(128)(4,1)}), s8[4194304]{0:T(1024)(128)(4,1)S(1)}, s32[]{:S(2)}) async-start(s8[11010048]{0:T(1024)(128)(4,1)} %bitcast.118), calls=%async_computation.2 | async-start | bytes 8388608
  267.6 17.8 %collective-permute-start.12 = (bf16[2,256,256]{1,2,0:T(8,128)(2,1)S(1)}, bf16[2,256,256]{1,2,0:T(8,128)(2,1)S(1)}, u32[]{:S(2)}, u32[]{:S(2)}) collective-permute-start(bf16[2,256,256]{1,2,0:T(8,128)(2,1)S(1)} %fusion.25), channel_id=1, source_target_pairs={{8,0},{12,4},{16,8},{20,12},{24,16},{28,20},{32,24},{36,28},{40,32... | collective-permute-start | bytes 786440 | tf_op jit(solution)/shard_map/ppermute | solution.py:16
  293.0 2.5 collective-permute-start.13
  294.9 2.4 collective-permute-start.15
  297.0 11.0 %collective-permute-start.14 = (bf16[128,1344]{0,1:T(8,128)(2,1)S(1)}, bf16[128,1344]{0,1:T(8,128)(2,1)S(1)}, u32[]{:S(2)}, u32[]{:S(2)}) collective-permute-start(bf16[128,1344]{0,1:T(8,128)(2,1)S(1)} %fusion.26), channel_id=1, source_target_pairs={{0,2},{1,3},{2,0},{3,1},{4,6},{5,7},{6,4},{7,5},{8,10},{9,11},{10,... | collective-permute-start | bytes 1032200 | tf_op jit(solution)/shard_map/ppermute | solution.py:39
  297.4 17.0 %collective-permute-start.16 = (bf16[128,1344]{0,1:T(8,128)(2,1)S(1)}, bf16[128,1344]{0,1:T(8,128)(2,1)S(1)}, u32[]{:S(2)}, u32[]{:S(2)}) collective-permute-start(bf16[128,1344]{0,1:T(8,128)(2,1)S(1)} %fusion.27), channel_id=1, source_target_pairs={{0,2},{1,3},{2,0},{3,1},{4,6},{5,7},{6,4},{7,5},{8,10},{9,11},{10,... | collective-permute-start | bytes 1032200 | tf_op jit(solution)/shard_map/ppermute | solution.py:39
  (9 other events, 71.1 us)
Sparse Core Ops, SparseCore 0:
  12.2 165.8 all-gather.3
